TPU v7x, 256 devices: a whole 4x4x8 slice. The times are simulated.
256 devices in a mesh: px: 32 (over z, x_hi, core), py: 8 (over y, x_lo).
Axes of the slice: x: 4 (x_hi: 2, x_lo: 2; x = x_hi * 2 + x_lo), y: 4, z: 8, core: 2. Of those that a mesh axis runs over, the one named last changes fastest.
Arguments:
- table: float32 [25, 50, 1000], replicated, may hold values from -1 to 1
- charge: float32 [128, 32, 8], P('px', 'py'), may hold values from 0.1 to 1
- hit_bins: int32 [128, 32, 8], P('px', 'py'), may hold values from 0 to 49
- hit_ticks: int32 [128, 32, 8], P('px', 'py'), may hold values from 0 to 23
- active: int32 [128, 32], P('px', 'py'), may hold values 0 or 1
- measured: bfloat16 [128, 32, 1024], P('px', 'py'), may hold values from -6 to 6
- row_module: int32 [128], replicated, may hold values from 0 to 6, as said below
- col_module: int32 [32], replicated, may hold values from 0 to 4, as said below
Outputs:
- current: bfloat16 [128, 32, 1024], P('px', 'py')
- table_grad: float32 [25, 50, 1000], P(None, None, 'py')
Inputs may be any that keep to these rules, and one draw needn't show every extreme that they name: `row_module`: starts at 0 and never falls; it rises by one at 6 rows. `col_module`: starts at 0 and never falls; it rises by one at 4 columns.
All inputs are finite; a program needn't handle non-finite values. No bound on the sum of `active` on one device may be relied on, other than what follows from the above.
Results may differ from a plain program's by a relative error of at most 0.014.
Values may be sent and summed in bfloat16 or wider, within the bound.
No kernel may reach another device: no remote copies, remote signals or barrier semaphores. Data moves between devices by JAX's collectives and lax.ppermute only.
A program may use at most 128 MiB of HBM per device.

v0:
```python
import jax
import jax.numpy as jnp
from jax import lax
from jax.sharding import PartitionSpec as P

BINS = 50
SHIFTS = 24


def passed_along(block, axis, distance):
    devices = range(lax.axis_size(axis))
    route = [(i - distance, i) for i in devices if i - distance in devices]
    return lax.ppermute(block, axis, route)


def bin_charges(charge, hit_bins, hit_ticks):
    tick_hot = (hit_ticks[..., None] == jnp.arange(SHIFTS, dtype=jnp.int32)).astype(jnp.float32)
    bin_hot = (hit_bins[..., None] == jnp.arange(BINS, dtype=jnp.int32)).astype(jnp.float32)
    weighted = charge[..., None] * tick_hot
    return jnp.einsum("xyks,xykb->xysb", weighted, bin_hot).astype(jnp.bfloat16)


def gather_offsets(source, rows, cols, count_x, count_y):
    pieces = []
    for row_off in range(-2, 3):
        for col_off in range(-2, 3):
            partial_value = source[
                2 - row_off : 2 - row_off + count_x, 2 - col_off : 2 - col_off + count_y
            ]
            row_same = rows[2 - row_off : 2 - row_off + count_x] == rows[2 : 2 + count_x]
            col_same = cols[2 - col_off : 2 - col_off + count_y] == cols[2 : 2 + count_y]
            allowed = row_same[:, None] & col_same[None, :]
            pieces.append(
                jnp.where(
                    allowed[:, :, None, None], partial_value, jnp.zeros((), partial_value.dtype)
                )
            )
    return jnp.stack(pieces, 0)


def shift_sum(partial_value, ticks):
    total = jnp.zeros(partial_value.shape[:2] + (ticks + SHIFTS,), jnp.float32)
    for offset in range(SHIFTS):
        total = total + jnp.pad(
            partial_value[:, :, offset, :], ((0, 0), (0, 0), (offset, SHIFTS - offset))
        )
    return total


def windows(resid, ticks):
    return jnp.stack([resid[:, :, offset : offset + ticks] for offset in range(SHIFTS)], axis=2)


def residual_of(prediction, measured, active):
    return (
        (prediction - measured.astype(jnp.float32)) * active.astype(jnp.float32)[..., None]
    ).astype(jnp.bfloat16)


def on_device(table, charge, hit_bins, hit_ticks, active, measured, row_module, col_module):
    tile_x, tile_y = (charge.shape[0], charge.shape[1])
    ticks = table.shape[2]
    parts_y = lax.axis_size("py")
    share = ticks // parts_y
    span = share + SHIFTS - 1
    weights = table.astype(jnp.bfloat16)
    row_start = lax.axis_index("px") * tile_x
    col_start = lax.axis_index("py") * tile_y

    deposits = jnp.stack(
        [charge, hit_bins.astype(jnp.float32), hit_ticks.astype(jnp.float32)], axis=-1
    )
    band = lax.all_gather(deposits, "py", axis=1, tiled=True)
    above = passed_along(band[tile_x - 2 :], "px", 1)
    below = passed_along(band[:2], "px", -1)
    wide = jnp.concatenate([above, band, below], axis=0)
    binned = bin_charges(
        wide[..., 0], wide[..., 1].astype(jnp.int32), wide[..., 2].astype(jnp.int32)
    )
    source = jnp.pad(binned, ((0, 0), (2, 2), (0, 0), (0, 0)))
    width = source.shape[1] - 4
    rows_wide = lax.dynamic_slice_in_dim(
        jnp.pad(row_module, 2, constant_values=-1), row_start, tile_x + 4, 0
    )
    cols_all = jnp.pad(col_module, 2, constant_values=-1)

    own_source = lax.dynamic_slice_in_dim(source, col_start, tile_y + 4, 1)
    own_cols = lax.dynamic_slice_in_dim(cols_all, col_start, tile_y + 4, 0)
    stacked = gather_offsets(own_source, rows_wide, own_cols, tile_x, tile_y)
    partial_value = jnp.einsum(
        "oxysb,obt->xyst", stacked, weights, preferred_element_type=jnp.float32
    )
    prediction = shift_sum(partial_value, ticks)
    resid = residual_of(prediction, measured, active)

    sent = jnp.stack(
        [resid[:, :, k * share : k * share + span] for k in range(parts_y)], axis=0
    )
    got = lax.all_to_all(sent, "py", 0, 0)
    band_resid = jnp.transpose(got, (1, 0, 2, 3)).reshape(tile_x, width, span)

    stacked_band = gather_offsets(source, rows_wide, cols_all, tile_x, width)
    gradient = jnp.einsum(
        "oxysb,xysu->obu",
        stacked_band,
        windows(band_resid, share),
        preferred_element_type=jnp.float32,
    )
    summed = lax.psum(gradient, "px")
    return (prediction.astype(jnp.bfloat16), summed / 16)


def solution(mesh):
    in_specs = (
        P(),
        P("px", "py", None),
        P("px", "py", None),
        P("px", "py", None),
        P("px", "py"),
        P("px", "py", None),
        P(),
        P(),
    )
    out_specs = (P("px", "py", None), P(None, None, "py"))
    return jax.shard_map(
        on_device, mesh=mesh, in_specs=in_specs, out_specs=out_specs, check_vma=False
    )
```

profile of v0, /device:TPU:1, one launch (start us, length us, event | category | flops | bytes accessed | tf_op | source)
XLA Modules:
  0.0 385.7 jit_solution(15461394324954869272)
XLA Ops:
  7.2 0.7 convert_bitcast_fusion
  7.9 0.7 pad_maximum_fusion.1
  8.6 24.1 %all_gather.3 = f32[4,32,8,3]{2,0,3,1:T(4,128)S(1)} all-gather(f32[4,4,8,3]{2,0,3,1:T(4,128)S(1)} %copy.144), channel_id=1, replica_groups=mesh['px'=32,'py'=8] {'py'}, dimensions={1}, use_global_device_ids=true | all-gather | bytes 13824 | tf_op jit(solution)/shard_map/all_gather | solution.py:73
  32.7 9.7 %collective-permute-start.1 = (f32[2,32,8,3]{2,0,3,1:T(2,128)S(1)}, f32[2,32,8,3]{2,0,3,1:T(2,128)S(1)}, u32[]{:S(2)}, u32[]{:S(2)}) collective-permute-start(f32[2,32,8,3]{2,0,3,1:T(2,128)S(1)} %get-tuple-element.30), channel_id=1, source_target_pairs={{8,0},{16,8},{24,16},{32,24},{40,32},{48,40},{56,48},{64,56},{72,6... | collective-permute-start | bytes 18440 | tf_op jit(solution)/shard_map/ppermute | solution.py:13
  42.5 3.0 collective-permute-start
  45.5 0.9 slice_compare_fusion
  46.4 0.7 pad_dynamic-slice_fusion.1
  47.1 0.7 pad_dynamic-slice_fusion
  48.1 0.1 copy.146
  48.2 0.7 convert_element_type.92
  49.5 2.9 convolution_convert_fusion
  52.5 0.1 constant_dynamic-update-slice_fusion.23
  52.8 0.1 constant_dynamic-update-slice_fusion.20
  53.4 0.1 constant_dynamic-update-slice_fusion.15
  54.4 0.1 constant_dynamic-update-slice_fusion.5
  55.1 1.3 slice-done
  56.3 0.6 slice-done.1
  56.9 2.6 fusion
  59.5 0.2 copy.351
  59.7 0.3 fusion.47
  60.0 1.2 fusion.46
  62.5 0.2 bitcast_dynamic-update-slice_fusion.19
  62.8 0.3 bitcast_dynamic-update-slice_fusion.18
  63.1 0.3 fusion.13
  63.4 0.3 bitcast_dynamic-update-slice_fusion.17
  63.8 0.3 bitcast_dynamic-update-slice_fusion.16
  64.1 0.3 bitcast_dynamic-update-slice_fusion.15
  64.5 0.3 bitcast_dynamic-update-slice_fusion.14
  64.8 0.3 fusion.11
  65.1 0.3 bitcast_dynamic-update-slice_fusion.13
  65.5 0.3 bitcast_dynamic-update-slice_fusion.12
  65.8 0.3 bitcast_dynamic-update-slice_fusion.11
  66.1 0.3 bitcast_dynamic-update-slice_fusion.10
  66.5 0.1 fusion.9
  66.6 0.3 bitcast_dynamic-update-slice_fusion.9
  67.0 0.3 bitcast_dynamic-update-slice_fusion.8
  67.3 0.3 bitcast_dynamic-update-slice_fusion.7
  67.6 0.3 bitcast_dynamic-update-slice_fusion.6
  68.0 0.3 fusion.8
  68.3 0.3 bitcast_dynamic-update-slice_fusion.5
  68.6 0.3 bitcast_dynamic-update-slice_fusion.4
  69.0 0.5 bitcast_dynamic-update-slice_fusion.3
  69.5 0.3 bitcast_dynamic-update-slice_fusion.2
  69.9 0.3 fusion.6
  70.3 2.0 multiply_convert_fusion
  72.3 4.6 %copy-done.1 = bf16[25,4,32,24,50]{4,3,2,1,0:T(8,128)(2,1)} copy-done((bf16[25,4,32,24,50]{4,3,2,1,0:T(8,128)(2,1)}, bf16[25,4,32,24,50]{4,3,2,1,0:T(8,128)(2,1)S(1)}, u32[]{:S(2)}) %copy-start.1) | copy-done | bytes 7680024
  76.8 0.6 constant_dynamic-update-slice_fusion.32
  77.4 0.7 constant_dynamic-update-slice_fusion.31
  78.1 0.7 constant_dynamic-update-slice_fusion.30
  78.8 0.7 constant_dynamic-update-slice_fusion.29
  79.5 0.7 constant_dynamic-update-slice_fusion.28
  80.1 0.7 constant_dynamic-update-slice_fusion.27
  80.8 0.7 constant_dynamic-update-slice_fusion.26
  81.5 0.7 constant_dynamic-update-slice_fusion.25
  82.2 3.7 all-to-all-start
  85.9 1.1 bitcast_dynamic-update-slice_fusion.1
  87.1 1.1 bitcast_dynamic-update-slice_fusion
  88.2 2.9 all-to-all-done
  91.1 0.1 slice_bitcast_fusion.20
  91.3 0.4 slice_bitcast_fusion.1
  93.1 2.6 stack.359
  95.7 12.7 %convolution_bitcast_fusion = f32[25,50,125]{2,1,0:T(8,128)} fusion(bf16[25,4,32,24,50]{4,3,2,1,0:T(8,128)(2,1)} %bitcast_dynamic-update-slice_fusion, bf16[4,32,24,125]{3,2,1,0:T(8,128)(2,1)S(1)} %stack.359), kind=kOutput, calls=%fused_computation.6 | convolution fusion | flops 960000000 | bytes 9073000 | tf_op jit(solution)/shard_map/oxysb,xysu->obu/dot_general | solution.py:103
  108.5 268.3 %all-reduce.29.cloned.1.call-done = f32[25,50,125]{2,1,0:T(8,128)} async-done(((f32[25,50,125]{2,1,0:T(8,128)}), f32[25,50,125]{2,1,0:T(8,128)}) %all-reduce.29.cloned.1.call-update) | async-done | bytes 625016 | tf_op jit(solution)/shard_map/psum | solution.py:109
  376.8 2.0 broadcast_multiply_fusion
  (94 shorter events, 5.6 us)
Async XLA Ops:
  32.7 16.2 %collective-permute-start.1 = (f32[2,32,8,3]{2,0,3,1:T(2,128)S(1)}, f32[2,32,8,3]{2,0,3,1:T(2,128)S(1)}, u32[]{:S(2)}, u32[]{:S(2)}) collective-permute-start(f32[2,32,8,3]{2,0,3,1:T(2,128)S(1)} %get-tuple-element.30), channel_id=1, source_target_pairs={{8,0},{16,8},{24,16},{32,24},{40,32},{48,40},{56,48},{64,56},{72,6... | collective-permute-start | bytes 18440 | tf_op jit(solution)/shard_map/ppermute | solution.py:13
  42.5 6.5 %collective-permute-start = (f32[2,32,8,3]{2,0,3,1:T(2,128)S(1)}, f32[2,32,8,3]{2,0,3,1:T(2,128)S(1)}, u32[]{:S(2)}, u32[]{:S(2)}) collective-permute-start(f32[2,32,8,3]{2,0,3,1:T(2,128)S(1)} %get-tuple-element.29), channel_id=1, source_target_pairs={{0,8},{8,16},{16,24},{24,32},{32,40},{40,48},{48,56},{56,64},{64,7... | collective-permute-start | bytes 18440 | tf_op jit(solution)/shard_map/ppermute | solution.py:13
  54.2 2.2 slice-start
  54.5 2.4 slice-start.1
  69.5 0.8 copy-start
  70.2 6.7 %copy-start.1 = (bf16[25,4,32,24,50]{4,3,2,1,0:T(8,128)(2,1)}, bf16[25,4,32,24,50]{4,3,2,1,0:T(8,128)(2,1)S(1)}, u32[]{:S(2)}) copy-start(bf16[25,4,32,24,50]{4,3,2,1,0:T(8,128)(2,1)S(1)} %fusion.6) | copy-start | bytes 23040004
  82.2 8.9 %all-to-all-start = ((bf16[8,4,4,148]{3,2,1,0:T(4,128)(2,1)}), bf16[8,4,4,148]{3,2,1,0:T(4,128)(2,1)S(1)}, u32[]{:S(2)}, u32[]{:S(2)}) async-start(bf16[8,4,4,148]{3,2,1,0:T(4,128)(2,1)} %constant_dynamic-update-slice_fusion.25), calls=%async_computation | async-start | bytes 131072 | tf_op jit(solution)/shard_map/all_to_all | solution.py:99
  85.9 290.9 %all-reduce.29.cloned.1.call-start = ((), (), s32[]{:S(2)}) async-start(), calls=%async_computation.1 | async-start | bytes 1433600 | tf_op jit(solution)/shard_map/psum | solution.py:109
Sparse Core Ops, SparseCore 0:
  108.6 268.1 all-reduce.28
where the time goes:
time: 387 us; the launch traced here: 386 us
  waiting for transfers between devices  271 us (70%)
  blocking collectives  24.1 us (6%)
  local copies, waits for them, and re-layouts  21.4 us (6%)
  other arithmetic  19.5 us (5%)
  matrix products  18.2 us (5%)
  starting transfers between devices  16.5 us (4%)
  between operations  14.8 us (4%)
    psum x1, waiting for transfers between devices, on_device(): summed = lax.psum(gradient, 'px')  268 us
    all_gather x1, blocking collectives, on_device(): band = lax.all_gather(deposits, 'py', axis=1, tiled=True)  24.1 us
    dot_general x1, matrix products, on_device(): jnp.einsum('oxysb,xysu->obu', stacked_band, windows(band_resid, share), p...  12.7 us
    ppermute x2, starting transfers between devices, passed_along(): return lax.ppermute(block, axis, route)  12.7 us
    unnamed x41, local copies, waits for them, and re-layouts  12.4 us
    unnamed x47, other arithmetic  10.9 us
  transfers between devices with their start and end apart: 4, of which 2 were waited for; matrix products, arithmetic and copies ran while one was open for 2% of the time, Pallas kernels for 0%

commit v1 on v0

--- a/solution.py
+++ b/solution.py
@@ -11,6 +11,32 @@
     devices = range(lax.axis_size(axis))
     route = [(i - distance, i) for i in devices if i - distance in devices]
     return lax.ppermute(block, axis, route)
+
+
+def tree_sum(value, axis):
+    count = lax.axis_size(axis)
+    me = lax.axis_index(axis)
+    steps = count.bit_length() - 1
+    rows = value.shape[0]
+    unit = -(-rows // count)
+    buf = jnp.pad(value, ((0, unit * count - rows),) + ((0, 0),) * (value.ndim - 1))
+    bits = []
+    for k in range(steps):
+        gap = 1 << k
+        bit = (me >> k) & 1
+        bits.append(bit)
+        half = buf.shape[0] // 2
+        keep = lax.dynamic_slice_in_dim(buf, bit * half, half, 0)
+        send = lax.dynamic_slice_in_dim(buf, (1 - bit) * half, half, 0)
+        got = lax.ppermute(send, axis, [(p, p ^ gap) for p in range(count)])
+        buf = keep + got
+    for k in reversed(range(steps)):
+        gap = 1 << k
+        got = lax.ppermute(buf, axis, [(p, p ^ gap) for p in range(count)])
+        low = jnp.where(bits[k] == 0, buf, got)
+        high = jnp.where(bits[k] == 0, got, buf)
+        buf = jnp.concatenate([low, high], axis=0)
+    return buf[:rows]
 
 
 def bin_charges(charge, hit_bins, hit_ticks):
@@ -70,7 +96,9 @@
     deposits = jnp.stack(
         [charge, hit_bins.astype(jnp.float32), hit_ticks.astype(jnp.float32)], axis=-1
     )
-    band = lax.all_gather(deposits, "py", axis=1, tiled=True)
+    spread = jnp.broadcast_to(deposits[None], (parts_y,) + deposits.shape)
+    band = jnp.transpose(lax.all_to_all(spread, "py", 0, 0), (1, 0, 2, 3, 4))
+    band = band.reshape((tile_x, parts_y * tile_y) + deposits.shape[2:])
     above = passed_along(band[tile_x - 2 :], "px", 1)
     below = passed_along(band[:2], "px", -1)
     wide = jnp.concatenate([above, band, below], axis=0)
@@ -106,7 +134,8 @@
         windows(band_resid, share),
         preferred_element_type=jnp.float32,
     )
-    summed = lax.psum(gradient, "px")
+    flat = gradient.reshape(-1, share)
+    summed = tree_sum(flat, "px").reshape(gradient.shape)
     return (prediction.astype(jnp.bfloat16), summed / 16)
 
 

time: 387 us -> 145 us (0.37)
  waiting for transfers between devices: 271 us -> 31.5 us
  starting transfers between devices: 16.5 us -> 51.7 us
  blocking collectives: 24.1 us -> 0 us
  between operations: 14.8 us -> 1.59 us
    psum x1 -> x0, waiting for transfers between devices: 268 us -> none  [on_device(): summed = lax.psum(gradient, 'px')]
    ppermute x0 -> x10, starting transfers between devices: none -> 34.2 us  [the longest x5 19.2 us: tree_sum(): got = lax.ppermute(send, axis, [(p, p ^ gap) for p in range(count)])]
    ppermute x0 -> x10, waiting for transfers between devices: none -> 25.5 us  [the longest x5 15.3 us: tree_sum(): got = lax.ppermute(buf, axis, [(p, p ^ gap) for p in range(count)])]
    all_gather x1 -> x0, blocking collectives: 24.1 us -> none  [on_device(): band = lax.all_gather(deposits, 'py', axis=1, tiled=True)]
    all_to_all x0 -> x1, starting transfers between devices: none -> 5.94 us  [on_device(): band = jnp.transpose(lax.all_to_all(spread, 'py', 0, 0), (1, 0, 2, 3, 4))]
    ppermute x2, starting transfers between devices: 12.7 us -> 8.27 us  [passed_along(): return lax.ppermute(block, axis, route)]
    unnamed x41 -> x44, local copies, waits for them, and re-layouts: 12.4 us -> 13.5 us
  transfers between devices with their start and end apart: 4 -> 14, of which waited for: 2 -> 13; matrix products, arithmetic and copies ran while one was open for 2% -> 4% of each run, Pallas kernels for 0% -> 0%
where the time goes in v1:
time: 145 us
  starting transfers between devices  51.7 us (36%)
  waiting for transfers between devices  31.5 us (22%)
  local copies, waits for them, and re-layouts  24 us (17%)
  other arithmetic  18.5 us (13%)
  matrix products  17.4 us (12%)
  between operations  1.59 us (1%)
    ppermute x5, starting transfers between devices, tree_sum(): got = lax.ppermute(send, axis, [(p, p ^ gap) for p in range(count)])  19.2 us
    ppermute x5, waiting for transfers between devices, tree_sum(): got = lax.ppermute(buf, axis, [(p, p ^ gap) for p in range(count)])  15.3 us
    ppermute x5, starting transfers between devices, tree_sum(): got = lax.ppermute(buf, axis, [(p, p ^ gap) for p in range(count)])  14.9 us
    unnamed x44, local copies, waits for them, and re-layouts  13.5 us
    dot_general x1, matrix products, on_device(): jnp.einsum('oxysb,xysu->obu', stacked_band, windows(band_resid, share), p...  11.9 us
    unnamed x47, other arithmetic  10.9 us
    ppermute x5, waiting for transfers between devices, tree_sum(): got = lax.ppermute(send, axis, [(p, p ^ gap) for p in range(count)])  10.2 us
    ppermute x2, starting transfers between devices, passed_along(): return lax.ppermute(block, axis, route)  8.27 us
  transfers between devices with their start and end apart: 14, of which 13 were waited for; matrix products, arithmetic and copies ran while one was open for 4% of the time, Pallas kernels for 0%

profile of v1, /device:TPU:1, one launch (start us, length us, event | category | flops | bytes accessed | tf_op | source)
XLA Modules:
  0.0 144.7 jit_solution(7010161525629354455)
XLA Ops:
  0.6 0.7 convert_bitcast_fusion
  1.3 0.7 pad_maximum_fusion.6
  2.1 0.8 reshape.927
  2.9 5.9 %all-to-all-start = ((f32[8,1,384]{2,1,0:T(1,128)}), f32[8,1,384]{2,1,0:T(1,128)S(1)}, u32[]{:S(2)}, u32[]{:S(2)}) async-start(f32[8,1,384]{2,1,0:T(1,128)} %reshape.927), calls=%async_computation | async-start | bytes 24576 | tf_op jit(solution)/shard_map/all_to_all | solution.py:100
  8.8 0.7 pad_dynamic-slice_fusion.2
  9.6 0.7 pad_dynamic-slice_fusion.3
  10.5 0.9 slice_compare_fusion
  11.4 2.5 %all-to-all-done = f32[8,1,384]{2,1,0:T(1,128)S(1)} async-done(((f32[8,1,384]{2,1,0:T(1,128)}), f32[8,1,384]{2,1,0:T(1,128)S(1)}, u32[]{:S(2)}, u32[]{:S(2)}) %all-to-all-start) | async-done | bytes 12320 | tf_op jit(solution)/shard_map/all_to_all | solution.py:100
  13.9 0.5 broadcast.907
  14.4 0.7 reduce
  15.4 4.0 %collective-permute-start.1 = (f32[2,32,8,3]{2,1,3,0:T(8,128)S(1)}, f32[2,32,8,3]{2,1,3,0:T(8,128)S(1)}, u32[]{:S(2)}, u32[]{:S(2)}) collective-permute-start(f32[2,32,8,3]{2,1,3,0:T(8,128)S(1)} %bitcast.410), channel_id=1, source_target_pairs={{8,0},{16,8},{24,16},{32,24},{40,32},{48,40},{56,48},{64,56},{72,6... | collective-permute-start | bytes 18440 | tf_op jit(solution)/shard_map/ppermute | solution.py:13
  19.5 4.3 %collective-permute-start = (f32[2,32,8,3]{2,1,3,0:T(8,128)S(1)}, f32[2,32,8,3]{2,1,3,0:T(8,128)S(1)}, u32[]{:S(2)}, u32[]{:S(2)}) collective-permute-start(f32[2,32,8,3]{2,1,3,0:T(8,128)S(1)} %bitcast.411), channel_id=1, source_target_pairs={{0,8},{8,16},{16,24},{24,32},{32,40},{40,48},{48,56},{56,64},{64,7... | collective-permute-start | bytes 18440 | tf_op jit(solution)/shard_map/ppermute | solution.py:13
  23.8 0.7 convert_element_type.94
  24.7 0.6 collective-permute-done
  25.8 2.9 %convolution_convert_fusion = bf16[8,32,24,50]{3,2,1,0:T(8,128)(2,1)S(1)} fusion(s32[8,32,8]{2,1,0:T(8,128)S(1)} %copy.148, bf16[8,32,8]{2,1,0:T(8,128)(2,1)S(1)} %copy.147, s32[8,32,8]{2,1,0:T(8,128)S(1)} %copy.146), kind=kOutput, calls=%fused_computation.4 | convolution fusion | flops 5115904 | bytes 634880 | tf_op jit(solution)/shard_map/xyks,xykb->xysb/dot_general | solution.py:46
  31.3 1.3 slice-done
  32.6 0.6 slice-done.1
  33.2 2.6 %fusion = f32[4,4,24,1000,1]{3,2,0,1,4:T(8,128)S(1)} fusion(f32[25,50,1000]{2,1,0:T(8,128)S(1)} %bitcast.414, bf16[25,4,4,24,50]{4,3,2,1,0:T(8,128)(2,1)S(1)} %constant_dynamic-update-slice_fusion), kind=kOutput, calls=%fused_computation | convolution fusion | flops 961249984 | bytes 7496000 | tf_op jit(solution)/shard_map/oxysb,obt->xyst/dot_general | solution.py:118
  36.3 1.2 fusion.48
  39.1 0.3 bitcast_dynamic-update-slice_fusion.18
  39.7 0.3 bitcast_dynamic-update-slice_fusion.17
  40.1 0.3 bitcast_dynamic-update-slice_fusion.16
  40.7 0.3 bitcast_dynamic-update-slice_fusion.14
  41.4 0.3 bitcast_dynamic-update-slice_fusion.13
  41.7 0.3 bitcast_dynamic-update-slice_fusion.12
  43.9 0.3 bitcast_dynamic-update-slice_fusion.6
  44.6 0.3 bitcast_dynamic-update-slice_fusion.5
  45.3 0.5 bitcast_dynamic-update-slice_fusion.3
  45.8 0.3 bitcast_dynamic-update-slice_fusion.2
  46.5 2.0 %multiply_convert_fusion = (bf16[4,4,1024]{2,1,0:T(4,128)(2,1)S(1)}, bf16[4,4,1024]{2,1,0:T(4,128)(2,1)}) fusion(bf16[4,4,1024]{2,1,0:T(4,128)(2,1)S(1)} %copy-done, f32[4,4]{1,0:T(4,128)S(1)} %convert_element_type.94, f32[4,4,1000]{2,1,0:T(4,128)S(1)} %bitcast.385, f32[4,4,1000]{2,1,0:T(4,128)S(1)} %bitcast.386, f32[4,4,1000]{2,1,0:T(4,128)S(1)} %bitcast.387, ...), kind=kLoop, calls=%fused_computation.170 | loop fusion | flops 458752 | bytes 1634368 | tf_op jit(solution)/shard_map/convert_element_type | solution.py:83
  48.6 4.5 %copy-done.1 = bf16[25,4,32,24,50]{4,3,2,1,0:T(8,128)(2,1)} copy-done((bf16[25,4,32,24,50]{4,3,2,1,0:T(8,128)(2,1)}, bf16[25,4,32,24,50]{4,3,2,1,0:T(8,128)(2,1)S(1)}, u32[]{:S(2)}) %copy-start.1) | copy-done | bytes 7680024
  53.1 0.6 constant_dynamic-update-slice_fusion.32
  53.7 0.7 constant_dynamic-update-slice_fusion.31
  54.4 0.7 constant_dynamic-update-slice_fusion.30
  55.1 0.7 constant_dynamic-update-slice_fusion.29
  55.7 0.7 constant_dynamic-update-slice_fusion.28
  56.4 0.7 constant_dynamic-update-slice_fusion.27
  57.1 0.7 constant_dynamic-update-slice_fusion.26
  57.8 0.7 constant_dynamic-update-slice_fusion.25
  58.4 3.4 %all-to-all-start.1 = ((bf16[8,4,4,148]{3,2,1,0:T(4,128)(2,1)}), bf16[8,4,4,148]{3,2,1,0:T(4,128)(2,1)S(1)}, u32[]{:S(2)}, u32[]{:S(2)}) async-start(bf16[8,4,4,148]{3,2,1,0:T(4,128)(2,1)} %constant_dynamic-update-slice_fusion.25), calls=%async_computation.1 | async-start | bytes 131072 | tf_op jit(solution)/shard_map/all_to_all | solution.py:127
  61.8 1.1 bitcast_dynamic-update-slice_fusion.1
  62.9 1.1 bitcast_dynamic-update-slice_fusion
  64.1 2.9 %all-to-all-done.1 = bf16[8,4,4,148]{3,2,1,0:T(4,128)(2,1)S(1)} async-done(((bf16[8,4,4,148]{3,2,1,0:T(4,128)(2,1)}), bf16[8,4,4,148]{3,2,1,0:T(4,128)(2,1)S(1)}, u32[]{:S(2)}, u32[]{:S(2)}) %all-to-all-start.1) | async-done | bytes 37920 | tf_op jit(solution)/shard_map/all_to_all | solution.py:127
  67.1 0.4 slice_bitcast_fusion.1
  68.9 2.6 %stack.359 = bf16[4,32,24,125]{3,2,1,0:T(8,128)(2,1)S(1)} concatenate(bf16[4,32,1,125]{3,2,1,0:T(2,128)(2,1)S(1)} %copy.197, bf16[4,32,1,125]{3,2,1,0:T(2,128)(2,1)S(1)} %copy.198, bf16[4,32,1,125]{3,2,1,0:T(2,128)(2,1)S(1)} %copy.199, bf16[4,32,1,125]{3,2,1,0:T(2,128)(2,1)S(1)} %copy.200, bf16[4,32,1,125]{3,2,1,0:T(2,128)(2,1)S(1)} %copy.201, ...), dimensions={2} | concatenate | bytes 1536000 | tf_op jit(solution)/shard_map/stack | solution.py:77
  71.5 11.9 %convolution_bitcast_fusion = f32[25,50,125]{2,1,0:T(8,128)S(1)} fusion(bf16[25,4,32,24,50]{4,3,2,1,0:T(8,128)(2,1)} %bitcast_dynamic-update-slice_fusion, bf16[4,32,24,125]{3,2,1,0:T(8,128)(2,1)S(1)} %stack.359), kind=kOutput, calls=%fused_computation.6 | convolution fusion | flops 960000000 | bytes 9073000 | tf_op jit(solution)/shard_map/oxysb,xysu->obu/dot_general | solution.py:131
  83.7 1.6 %collective-permute-done.2 = f32[640,125]{1,0:T(8,128)S(1)} collective-permute-done((f32[640,125]{1,0:T(8,128)S(1)}, f32[640,125]{1,0:T(8,128)S(1)}, u32[]{:S(2)}, u32[]{:S(2)}) %collective-permute-start.2) | collective-permute-done | bytes 320032 | tf_op jit(solution)/shard_map/ppermute | solution.py:31
  85.4 4.9 %collective-permute-start.3 = (f32[320,125]{1,0:T(8,128)S(1)}, f32[320,125]{1,0:T(8,128)S(1)}, u32[]{:S(2)}, u32[]{:S(2)}) collective-permute-start(f32[320,125]{1,0:T(8,128)S(1)} %constant_dynamic-slice_fusion.3), channel_id=1, source_target_pairs={{0,16},{8,24},{16,0},{24,8},{32,48},{40,56},{48,32},{56,40},{64,80... | collective-permute-start | bytes 480008 | tf_op jit(solution)/shard_map/ppermute | solution.py:31
  90.3 4.2 %collective-permute-done.3 = f32[320,125]{1,0:T(8,128)S(1)} collective-permute-done((f32[320,125]{1,0:T(8,128)S(1)}, f32[320,125]{1,0:T(8,128)S(1)}, u32[]{:S(2)}, u32[]{:S(2)}) %collective-permute-start.3) | collective-permute-done | bytes 160032 | tf_op jit(solution)/shard_map/ppermute | solution.py:31
  94.5 3.1 %collective-permute-start.4 = (f32[160,125]{1,0:T(8,128)S(1)}, f32[160,125]{1,0:T(8,128)S(1)}, u32[]{:S(2)}, u32[]{:S(2)}) collective-permute-start(f32[160,125]{1,0:T(8,128)S(1)} %constant_dynamic-slice_fusion.2), channel_id=1, source_target_pairs={{0,32},{8,40},{16,48},{24,56},{32,0},{40,8},{48,16},{56,24},{64,96... | collective-permute-start | bytes 240008 | tf_op jit(solution)/shard_map/ppermute | solution.py:31
  97.7 1.8 %collective-permute-done.4 = f32[160,125]{1,0:T(8,128)S(1)} collective-permute-done((f32[160,125]{1,0:T(8,128)S(1)}, f32[160,125]{1,0:T(8,128)S(1)}, u32[]{:S(2)}, u32[]{:S(2)}) %collective-permute-start.4) | collective-permute-done | bytes 80032 | tf_op jit(solution)/shard_map/ppermute | solution.py:31
  99.5 3.3 %collective-permute-start.5 = (f32[80,125]{1,0:T(8,128)S(1)}, f32[80,125]{1,0:T(8,128)S(1)}, u32[]{:S(2)}, u32[]{:S(2)}) collective-permute-start(f32[80,125]{1,0:T(8,128)S(1)} %constant_dynamic-slice_fusion.1), channel_id=1, source_target_pairs={{0,64},{8,72},{16,80},{24,88},{32,96},{40,104},{48,112},{56,120},{... | collective-permute-start | bytes 120008 | tf_op jit(solution)/shard_map/ppermute | solution.py:31
  102.8 1.4 collective-permute-done.5
  104.2 7.8 %collective-permute-start.6 = (f32[40,125]{1,0:T(8,128)S(1)}, f32[40,125]{1,0:T(8,128)S(1)}, u32[]{:S(2)}, u32[]{:S(2)}) collective-permute-start(f32[40,125]{1,0:T(8,128)S(1)} %constant_dynamic-slice_fusion), channel_id=1, source_target_pairs={{0,128},{8,136},{16,144},{24,152},{32,160},{40,168},{48,176},{56,1... | collective-permute-start | bytes 60008 | tf_op jit(solution)/shard_map/ppermute | solution.py:31
  112.1 1.2 collective-permute-done.6
  113.2 5.4 %collective-permute-start.7 = (f32[40,125]{1,0:T(8,128)S(1)}, f32[40,125]{1,0:T(8,128)S(1)}, u32[]{:S(2)}, u32[]{:S(2)}) collective-permute-start(f32[40,125]{1,0:T(8,128)S(1)} %dynamic-slice_add_fusion.3), channel_id=1, source_target_pairs={{0,128},{8,136},{16,144},{24,152},{32,160},{40,168},{48,176},{56,1... | collective-permute-start | bytes 60008 | tf_op jit(solution)/shard_map/ppermute | solution.py:35
  118.6 1.2 collective-permute-done.7
  119.8 0.5 collective-permute-start.8
  120.3 3.9 %collective-permute-done.8 = f32[80,125]{1,0:T(8,128)S(1)} collective-permute-done((f32[80,125]{1,0:T(8,128)S(1)}, f32[80,125]{1,0:T(8,128)S(1)}, u32[]{:S(2)}, u32[]{:S(2)}) %collective-permute-start.8) | collective-permute-done | bytes 40032 | tf_op jit(solution)/shard_map/ppermute | solution.py:35
  124.4 3.3 %collective-permute-done.9 = f32[160,125]{1,0:T(8,128)S(1)} collective-permute-done((f32[160,125]{1,0:T(8,128)S(1)}, f32[160,125]{1,0:T(8,128)S(1)}, u32[]{:S(2)}, u32[]{:S(2)}) %collective-permute-start.9) | collective-permute-done | bytes 80032 | tf_op jit(solution)/shard_map/ppermute | solution.py:35
  127.8 5.7 %collective-permute-done.10 = f32[320,125]{1,0:T(8,128)S(1)} collective-permute-done((f32[320,125]{1,0:T(8,128)S(1)}, f32[320,125]{1,0:T(8,128)S(1)}, u32[]{:S(2)}, u32[]{:S(2)}) %collective-permute-start.10) | collective-permute-done | bytes 160032 | tf_op jit(solution)/shard_map/ppermute | solution.py:35
  133.6 8.9 %collective-permute-start.11 = (f32[640,125]{1,0:T(8,128)S(1)}, f32[640,125]{1,0:T(8,128)S(1)}, u32[]{:S(2)}, u32[]{:S(2)}) collective-permute-start(f32[640,125]{1,0:T(8,128)S(1)} %pad_maximum_fusion.1), channel_id=1, source_target_pairs={{0,8},{8,0},{16,24},{24,16},{32,40},{40,32},{48,56},{56,48},{64,72... | collective-permute-start | bytes 960008 | tf_op jit(solution)/shard_map/ppermute | solution.py:35
  142.4 1.3 collective-permute-done.11
  143.8 0.9 div.10
  (141 shorter events, 11.6 us)
Async XLA Ops:
  2.9 11.0 %all-to-all-start = ((f32[8,1,384]{2,1,0:T(1,128)}), f32[8,1,384]{2,1,0:T(1,128)S(1)}, u32[]{:S(2)}, u32[]{:S(2)}) async-start(f32[8,1,384]{2,1,0:T(1,128)} %reshape.927), calls=%async_computation | async-start | bytes 24576 | tf_op jit(solution)/shard_map/all_to_all | solution.py:100
  15.4 9.2 %collective-permute-start.1 = (f32[2,32,8,3]{2,1,3,0:T(8,128)S(1)}, f32[2,32,8,3]{2,1,3,0:T(8,128)S(1)}, u32[]{:S(2)}, u32[]{:S(2)}) collective-permute-start(f32[2,32,8,3]{2,1,3,0:T(8,128)S(1)} %bitcast.410), channel_id=1, source_target_pairs={{8,0},{16,8},{24,16},{32,24},{40,32},{48,40},{56,48},{64,56},{72,6... | collective-permute-start | bytes 18440 | tf_op jit(solution)/shard_map/ppermute | solution.py:13
  19.5 5.9 %collective-permute-start = (f32[2,32,8,3]{2,1,3,0:T(8,128)S(1)}, f32[2,32,8,3]{2,1,3,0:T(8,128)S(1)}, u32[]{:S(2)}, u32[]{:S(2)}) collective-permute-start(f32[2,32,8,3]{2,1,3,0:T(8,128)S(1)} %bitcast.411), channel_id=1, source_target_pairs={{0,8},{8,16},{16,24},{24,32},{32,40},{40,48},{48,56},{56,64},{64,7... | collective-permute-start | bytes 18440 | tf_op jit(solution)/shard_map/ppermute | solution.py:13
  30.4 2.2 %slice-start = ((s8[5734400]{0:T(1024)(128)(4,1)}), s8[4194304]{0:T(1024)(128)(4,1)S(1)}, s32[]{:S(2)}) async-start(s8[5734400]{0:T(1024)(128)(4,1)} %bitcast.413), calls=%async_computation.2 | async-start | bytes 8388608
  30.8 2.4 %slice-start.1 = ((s8[5734400]{0:T(1024)(128)(4,1)}), s8[1540096]{0:T(1024)(128)(4,1)S(1)}, s32[]{:S(2)}) async-start(s8[5734400]{0:T(1024)(128)(4,1)} %bitcast.413), calls=%async_computation.3 | async-start | bytes 3080192
  45.8 0.8 copy-start
  46.4 6.7 %copy-start.1 = (bf16[25,4,32,24,50]{4,3,2,1,0:T(8,128)(2,1)}, bf16[25,4,32,24,50]{4,3,2,1,0:T(8,128)(2,1)S(1)}, u32[]{:S(2)}) copy-start(bf16[25,4,32,24,50]{4,3,2,1,0:T(8,128)(2,1)S(1)} %fusion.6) | copy-start | bytes 23040004
  58.4 8.5 %all-to-all-start.1 = ((bf16[8,4,4,148]{3,2,1,0:T(4,128)(2,1)}), bf16[8,4,4,148]{3,2,1,0:T(4,128)(2,1)S(1)}, u32[]{:S(2)}, u32[]{:S(2)}) async-start(bf16[8,4,4,148]{3,2,1,0:T(4,128)(2,1)} %constant_dynamic-update-slice_fusion.25), calls=%async_computation.1 | async-start | bytes 131072 | tf_op jit(solution)/shard_map/all_to_all | solution.py:127
  83.6 1.7 %collective-permute-start.2 = (f32[640,125]{1,0:T(8,128)S(1)}, f32[640,125]{1,0:T(8,128)S(1)}, u32[]{:S(2)}, u32[]{:S(2)}) collective-permute-start(f32[640,125]{1,0:T(8,128)S(1)} %pad_dynamic-slice_fusion), channel_id=1, source_target_pairs={{0,8},{8,0},{16,24},{24,16},{32,40},{40,32},{48,56},{56,48},{64,72... | collective-permute-start | bytes 960008 | tf_op jit(solution)/shard_map/ppermute | solution.py:31
  85.4 9.1 %collective-permute-start.3 = (f32[320,125]{1,0:T(8,128)S(1)}, f32[320,125]{1,0:T(8,128)S(1)}, u32[]{:S(2)}, u32[]{:S(2)}) collective-permute-start(f32[320,125]{1,0:T(8,128)S(1)} %constant_dynamic-slice_fusion.3), channel_id=1, source_target_pairs={{0,16},{8,24},{16,0},{24,8},{32,48},{40,56},{48,32},{56,40},{64,80... | collective-permute-start | bytes 480008 | tf_op jit(solution)/shard_map/ppermute | solution.py:31
  94.5 5.0 %collective-permute-start.4 = (f32[160,125]{1,0:T(8,128)S(1)}, f32[160,125]{1,0:T(8,128)S(1)}, u32[]{:S(2)}, u32[]{:S(2)}) collective-permute-start(f32[160,125]{1,0:T(8,128)S(1)} %constant_dynamic-slice_fusion.2), channel_id=1, source_target_pairs={{0,32},{8,40},{16,48},{24,56},{32,0},{40,8},{48,16},{56,24},{64,96... | collective-permute-start | bytes 240008 | tf_op jit(solution)/shard_map/ppermute | solution.py:31
  99.5 4.7 %collective-permute-start.5 = (f32[80,125]{1,0:T(8,128)S(1)}, f32[80,125]{1,0:T(8,128)S(1)}, u32[]{:S(2)}, u32[]{:S(2)}) collective-permute-start(f32[80,125]{1,0:T(8,128)S(1)} %constant_dynamic-slice_fusion.1), channel_id=1, source_target_pairs={{0,64},{8,72},{16,80},{24,88},{32,96},{40,104},{48,112},{56,120},{... | collective-permute-start | bytes 120008 | tf_op jit(solution)/shard_map/ppermute | solution.py:31
  104.2 9.0 %collective-permute-start.6 = (f32[40,125]{1,0:T(8,128)S(1)}, f32[40,125]{1,0:T(8,128)S(1)}, u32[]{:S(2)}, u32[]{:S(2)}) collective-permute-start(f32[40,125]{1,0:T(8,128)S(1)} %constant_dynamic-slice_fusion), channel_id=1, source_target_pairs={{0,128},{8,136},{16,144},{24,152},{32,160},{40,168},{48,176},{56,1... | collective-permute-start | bytes 60008 | tf_op jit(solution)/shard_map/ppermute | solution.py:31
  113.2 6.5 %collective-permute-start.7 = (f32[40,125]{1,0:T(8,128)S(1)}, f32[40,125]{1,0:T(8,128)S(1)}, u32[]{:S(2)}, u32[]{:S(2)}) collective-permute-start(f32[40,125]{1,0:T(8,128)S(1)} %dynamic-slice_add_fusion.3), channel_id=1, source_target_pairs={{0,128},{8,136},{16,144},{24,152},{32,160},{40,168},{48,176},{56,1... | collective-permute-start | bytes 60008 | tf_op jit(solution)/shard_map/ppermute | solution.py:35
  119.8 4.5 %collective-permute-start.8 = (f32[80,125]{1,0:T(8,128)S(1)}, f32[80,125]{1,0:T(8,128)S(1)}, u32[]{:S(2)}, u32[]{:S(2)}) collective-permute-start(f32[80,125]{1,0:T(8,128)S(1)} %pad_maximum_fusion.5), channel_id=1, source_target_pairs={{0,64},{8,72},{16,80},{24,88},{32,96},{40,104},{48,112},{56,120},{... | collective-permute-start | bytes 120008 | tf_op jit(solution)/shard_map/ppermute | solution.py:35
  124.3 3.4 %collective-permute-start.9 = (f32[160,125]{1,0:T(8,128)S(1)}, f32[160,125]{1,0:T(8,128)S(1)}, u32[]{:S(2)}, u32[]{:S(2)}) collective-permute-start(f32[160,125]{1,0:T(8,128)S(1)} %pad_maximum_fusion.4), channel_id=1, source_target_pairs={{0,32},{8,40},{16,48},{24,56},{32,0},{40,8},{48,16},{56,24},{64,96... | collective-permute-start | bytes 240008 | tf_op jit(solution)/shard_map/ppermute | solution.py:35
  127.7 5.8 %collective-permute-start.10 = (f32[320,125]{1,0:T(8,128)S(1)}, f32[320,125]{1,0:T(8,128)S(1)}, u32[]{:S(2)}, u32[]{:S(2)}) collective-permute-start(f32[320,125]{1,0:T(8,128)S(1)} %pad_maximum_fusion.2), channel_id=1, source_target_pairs={{0,16},{8,24},{16,0},{24,8},{32,48},{40,56},{48,32},{56,40},{64,80... | collective-permute-start | bytes 480008 | tf_op jit(solution)/shard_map/ppermute | solution.py:35
  133.6 10.1 %collective-permute-start.11 = (f32[640,125]{1,0:T(8,128)S(1)}, f32[640,125]{1,0:T(8,128)S(1)}, u32[]{:S(2)}, u32[]{:S(2)}) collective-permute-start(f32[640,125]{1,0:T(8,128)S(1)} %pad_maximum_fusion.1), channel_id=1, source_target_pairs={{0,8},{8,0},{16,24},{24,16},{32,40},{40,32},{48,56},{56,48},{64,72... | collective-permute-start | bytes 960008 | tf_op jit(solution)/shard_map/ppermute | solution.py:35

commit v2 on v1

--- a/solution.py
+++ b/solution.py
@@ -37,6 +37,18 @@
         high = jnp.where(bits[k] == 0, got, buf)
         buf = jnp.concatenate([low, high], axis=0)
     return buf[:rows]
+
+
+def exchange_sum(value, axis):
+    count = lax.axis_size(axis)
+    rows = value.shape[0]
+    unit = -(-rows // count)
+    buf = jnp.pad(value, ((0, unit * count - rows),) + ((0, 0),) * (value.ndim - 1))
+    pieces = buf.reshape((count, unit) + value.shape[1:])
+    mine = jnp.sum(lax.all_to_all(pieces, axis, 0, 0), axis=0)
+    spread = jnp.broadcast_to(mine[None], pieces.shape)
+    every = lax.all_to_all(spread, axis, 0, 0)
+    return every.reshape(buf.shape)[:rows]
 
 
 def bin_charges(charge, hit_bins, hit_ticks):
@@ -135,7 +147,7 @@
         preferred_element_type=jnp.float32,
     )
     flat = gradient.reshape(-1, share)
-    summed = tree_sum(flat, "px").reshape(gradient.shape)
+    summed = exchange_sum(flat, "px").reshape(gradient.shape)
     return (prediction.astype(jnp.bfloat16), summed / 16)
 
 

time: 145 us -> 144 us (level)
  blocking collectives: 0 us -> 58.6 us
  starting transfers between devices: 51.7 us -> 17.6 us
  waiting for transfers between devices: 31.5 us -> 5.97 us
    all_to_all x0 -> x2, blocking collectives: none -> 58.6 us  [the longest x1 33.4 us: exchange_sum(): mine = jnp.sum(lax.all_to_all(pieces, axis, 0, 0), axis=0)]
    ppermute x10 -> x0, starting transfers between devices: 34.2 us -> none  [the longest x5 19.2 us: tree_sum(): got = lax.ppermute(send, axis, [(p, p ^ gap) for p in range(count)])]
    ppermute x10 -> x0, waiting for transfers between devices: 25.5 us -> none  [the longest x5 15.3 us: tree_sum(): got = lax.ppermute(buf, axis, [(p, p ^ gap) for p in range(count)])]
  transfers between devices with their start and end apart: 14 -> 4, of which waited for: 13 -> 3; matrix products, arithmetic and copies ran while one was open for 4% -> 4% of each run, Pallas kernels for 0% -> 0%
where the time goes in v2:
time: 144 us; the launch traced here: 143 us
  blocking collectives  58.6 us (41%)
  local copies, waits for them, and re-layouts  24 us (17%)
  other arithmetic  18.2 us (13%)
  starting transfers between devices  17.6 us (12%)
  matrix products  17.4 us (12%)
  waiting for transfers between devices  5.97 us (4%)
  between operations  1.45 us (1%)
    all_to_all x1, blocking collectives, exchange_sum(): mine = jnp.sum(lax.all_to_all(pieces, axis, 0, 0), axis=0)  33.4 us
    all_to_all x1, blocking collectives, exchange_sum(): every = lax.all_to_all(spread, axis, 0, 0)  25.3 us
    unnamed x44, local copies, waits for them, and re-layouts  13.5 us
    dot_general x1, matrix products, on_device(): jnp.einsum('oxysb,xysu->obu', stacked_band, windows(band_resid, share), p...  11.8 us
    unnamed x47, other arithmetic  10.9 us
    ppermute x2, starting transfers between devices, passed_along(): return lax.ppermute(block, axis, route)  8.27 us
    all_to_all x1, starting transfers between devices, on_device(): band = jnp.transpose(lax.all_to_all(spread, 'py', 0, 0), (1, 0, 2, 3, 4))  5.94 us
    another operation x27, local copies, waits for them, and re-layouts, windows(): jnp.stack([resid[:, :, offset:offset + ticks] for offset in range(SHIFTS)...  4.37 us
  transfers between devices with their start and end apart: 4, of which 3 were waited for; matrix products, arithmetic and copies ran while one was open for 4% of the time, Pallas kernels for 0%

profile of v2, /device:TPU:1, one launch (start us, length us, event | category | flops | bytes accessed | tf_op | source)
XLA Modules:
  0.0 143.2 jit_solution(15842186651399824312)
XLA Ops:
  0.6 0.7 convert_bitcast_fusion
  1.3 0.7 pad_maximum_fusion.1
  2.1 0.8 reshape.936
  2.9 5.9 %all-to-all-start = ((f32[8,1,384]{2,1,0:T(1,128)}), f32[8,1,384]{2,1,0:T(1,128)S(1)}, u32[]{:S(2)}, u32[]{:S(2)}) async-start(f32[8,1,384]{2,1,0:T(1,128)} %reshape.936), calls=%async_computation | async-start | bytes 24576 | tf_op jit(solution)/shard_map/all_to_all | solution.py:112
  8.8 0.7 pad_dynamic-slice_fusion
  9.6 0.7 pad_dynamic-slice_fusion.1
  10.5 0.9 slice_compare_fusion
  11.4 2.5 %all-to-all-done = f32[8,1,384]{2,1,0:T(1,128)S(1)} async-done(((f32[8,1,384]{2,1,0:T(1,128)}), f32[8,1,384]{2,1,0:T(1,128)S(1)}, u32[]{:S(2)}, u32[]{:S(2)}) %all-to-all-start) | async-done | bytes 12320 | tf_op jit(solution)/shard_map/all_to_all | solution.py:112
  13.9 0.5 broadcast.908
  14.4 0.7 reduce
  15.1 0.3 reshape.937
  15.4 4.0 %collective-permute-start.1 = (f32[2,32,8,3]{2,1,3,0:T(8,128)S(1)}, f32[2,32,8,3]{2,1,3,0:T(8,128)S(1)}, u32[]{:S(2)}, u32[]{:S(2)}) collective-permute-start(f32[2,32,8,3]{2,1,3,0:T(8,128)S(1)} %bitcast.414), channel_id=1, source_target_pairs={{8,0},{16,8},{24,16},{32,24},{40,32},{48,40},{56,48},{64,56},{72,6... | collective-permute-start | bytes 18440 | tf_op jit(solution)/shard_map/ppermute | solution.py:13
  19.5 4.3 %collective-permute-start = (f32[2,32,8,3]{2,1,3,0:T(8,128)S(1)}, f32[2,32,8,3]{2,1,3,0:T(8,128)S(1)}, u32[]{:S(2)}, u32[]{:S(2)}) collective-permute-start(f32[2,32,8,3]{2,1,3,0:T(8,128)S(1)} %bitcast.415), channel_id=1, source_target_pairs={{0,8},{8,16},{16,24},{24,32},{32,40},{40,48},{48,56},{56,64},{64,7... | collective-permute-start | bytes 18440 | tf_op jit(solution)/shard_map/ppermute | solution.py:13
  23.8 0.7 convert_element_type.94
  24.7 0.6 collective-permute-done
  25.8 2.9 %convolution_convert_fusion = bf16[8,32,24,50]{3,2,1,0:T(8,128)(2,1)S(1)} fusion(s32[8,32,8]{2,1,0:T(8,128)S(1)} %copy.148, bf16[8,32,8]{2,1,0:T(8,128)(2,1)S(1)} %copy.147, s32[8,32,8]{2,1,0:T(8,128)S(1)} %copy.146), kind=kOutput, calls=%fused_computation.4 | convolution fusion | flops 5115904 | bytes 634880 | tf_op jit(solution)/shard_map/xyks,xykb->xysb/dot_general | solution.py:58
  31.3 1.3 slice-done
  32.6 0.6 slice-done.1
  33.2 2.6 %fusion = f32[4,4,24,1000,1]{3,2,0,1,4:T(8,128)S(1)} fusion(f32[25,50,1000]{2,1,0:T(8,128)S(1)} %bitcast.418, bf16[25,4,4,24,50]{4,3,2,1,0:T(8,128)(2,1)S(1)} %constant_dynamic-update-slice_fusion), kind=kOutput, calls=%fused_computation | convolution fusion | flops 961249984 | bytes 7496000 | tf_op jit(solution)/shard_map/oxysb,obt->xyst/dot_general | solution.py:130
  35.8 0.2 copy.349
  36.0 0.3 fusion.47
  36.3 1.2 fusion.46
  38.8 0.2 bitcast_dynamic-update-slice_fusion.19
  39.1 0.3 bitcast_dynamic-update-slice_fusion.18
  39.4 0.3 fusion.13
  39.7 0.3 bitcast_dynamic-update-slice_fusion.17
  40.1 0.3 bitcast_dynamic-update-slice_fusion.16
  40.4 0.3 bitcast_dynamic-update-slice_fusion.15
  40.7 0.3 bitcast_dynamic-update-slice_fusion.14
  41.1 0.3 fusion.11
  41.4 0.3 bitcast_dynamic-update-slice_fusion.13
  41.7 0.3 bitcast_dynamic-update-slice_fusion.12
  42.1 0.3 bitcast_dynamic-update-slice_fusion.11
  42.4 0.3 bitcast_dynamic-update-slice_fusion.10
  42.9 0.3 bitcast_dynamic-update-slice_fusion.9
  43.2 0.3 bitcast_dynamic-update-slice_fusion.8
  43.6 0.3 bitcast_dynamic-update-slice_fusion.7
  43.9 0.3 bitcast_dynamic-update-slice_fusion.6
  44.3 0.3 fusion.8
  44.6 0.3 bitcast_dynamic-update-slice_fusion.5
  44.9 0.3 bitcast_dynamic-update-slice_fusion.4
  45.3 0.5 bitcast_dynamic-update-slice_fusion.3
  45.8 0.3 bitcast_dynamic-update-slice_fusion.2
  46.1 0.3 fusion.6
  46.5 2.0 %multiply_convert_fusion = (bf16[4,4,1024]{2,1,0:T(4,128)(2,1)S(1)}, bf16[4,4,1024]{2,1,0:T(4,128)(2,1)}) fusion(bf16[4,4,1024]{2,1,0:T(4,128)(2,1)S(1)} %copy-done, f32[4,4]{1,0:T(4,128)S(1)} %convert_element_type.94, f32[4,4,1000]{2,1,0:T(4,128)S(1)} %bitcast.389, f32[4,4,1000]{2,1,0:T(4,128)S(1)} %bitcast.390, f32[4,4,1000]{2,1,0:T(4,128)S(1)} %bitcast.391, ...), kind=kLoop, calls=%fused_computation.157 | loop fusion | flops 458752 | bytes 1634368 | tf_op jit(solution)/shard_map/convert_element_type | solution.py:95
  48.5 4.6 %copy-done.1 = bf16[25,4,32,24,50]{4,3,2,1,0:T(8,128)(2,1)} copy-done((bf16[25,4,32,24,50]{4,3,2,1,0:T(8,128)(2,1)}, bf16[25,4,32,24,50]{4,3,2,1,0:T(8,128)(2,1)S(1)}, u32[]{:S(2)}) %copy-start.1) | copy-done | bytes 7680024
  53.1 0.6 constant_dynamic-update-slice_fusion.32
  53.7 0.7 constant_dynamic-update-slice_fusion.31
  54.4 0.7 constant_dynamic-update-slice_fusion.30
  55.1 0.7 constant_dynamic-update-slice_fusion.29
  55.7 0.7 constant_dynamic-update-slice_fusion.28
  56.4 0.7 constant_dynamic-update-slice_fusion.27
  57.1 0.7 constant_dynamic-update-slice_fusion.26
  57.8 0.7 constant_dynamic-update-slice_fusion.25
  58.4 3.4 %all-to-all-start.1 = ((bf16[8,4,4,148]{3,2,1,0:T(4,128)(2,1)}), bf16[8,4,4,148]{3,2,1,0:T(4,128)(2,1)S(1)}, u32[]{:S(2)}, u32[]{:S(2)}) async-start(bf16[8,4,4,148]{3,2,1,0:T(4,128)(2,1)} %constant_dynamic-update-slice_fusion.25), calls=%async_computation.1 | async-start | bytes 131072 | tf_op jit(solution)/shard_map/all_to_all | solution.py:139
  61.8 1.1 bitcast_dynamic-update-slice_fusion.1
  62.9 1.1 bitcast_dynamic-update-slice_fusion
  64.1 2.8 %all-to-all-done.1 = bf16[8,4,4,148]{3,2,1,0:T(4,128)(2,1)S(1)} async-done(((bf16[8,4,4,148]{3,2,1,0:T(4,128)(2,1)}), bf16[8,4,4,148]{3,2,1,0:T(4,128)(2,1)S(1)}, u32[]{:S(2)}, u32[]{:S(2)}) %all-to-all-start.1) | async-done | bytes 37920 | tf_op jit(solution)/shard_map/all_to_all | solution.py:139
  67.1 0.4 slice_bitcast_fusion.1
  68.9 2.6 %stack.359 = bf16[4,32,24,125]{3,2,1,0:T(8,128)(2,1)S(1)} concatenate(bf16[4,32,1,125]{3,2,1,0:T(2,128)(2,1)S(1)} %copy.197, bf16[4,32,1,125]{3,2,1,0:T(2,128)(2,1)S(1)} %copy.198, bf16[4,32,1,125]{3,2,1,0:T(2,128)(2,1)S(1)} %copy.199, bf16[4,32,1,125]{3,2,1,0:T(2,128)(2,1)S(1)} %copy.200, bf16[4,32,1,125]{3,2,1,0:T(2,128)(2,1)S(1)} %copy.201, ...), dimensions={2} | concatenate | bytes 1536000 | tf_op jit(solution)/shard_map/stack | solution.py:89
  71.5 11.8 %convolution_bitcast_fusion = f32[25,50,125]{2,1,0:T(8,128)S(1)} fusion(bf16[25,4,32,24,50]{4,3,2,1,0:T(8,128)(2,1)} %bitcast_dynamic-update-slice_fusion, bf16[4,32,24,125]{3,2,1,0:T(8,128)(2,1)S(1)} %stack.359), kind=kOutput, calls=%fused_computation.6 | convolution fusion | flops 960000000 | bytes 9073000 | tf_op jit(solution)/shard_map/oxysb,xysu->obu/dot_general | solution.py:143
  83.5 33.4 %all_to_all.20 = f32[32,40,125]{2,1,0:T(8,128)S(1)} all-to-all(f32[32,40,125]{2,1,0:T(8,128)S(1)} %bitcast.385), channel_id=1, replica_groups=mesh['px'=32,'py'=8] {'px'}, dimensions={0} | all-to-all | bytes 1280000 | tf_op jit(solution)/shard_map/all_to_all | solution.py:48
  117.0 25.3 %all_to_all.21 = f32[32,40,125]{2,1,0:T(8,128)S(1)} all-to-all(f32[32,40,125]{2,1,0:T(8,128)S(1)} %broadcast_in_dim.526), channel_id=1, replica_groups=mesh['px'=32,'py'=8] {'px'}, dimensions={0} | all-to-all | bytes 1280000 | tf_op jit(solution)/shard_map/all_to_all | solution.py:50
  142.3 0.9 div.10
  (107 shorter events, 6.6 us)
Async XLA Ops:
  2.9 11.0 %all-to-all-start = ((f32[8,1,384]{2,1,0:T(1,128)}), f32[8,1,384]{2,1,0:T(1,128)S(1)}, u32[]{:S(2)}, u32[]{:S(2)}) async-start(f32[8,1,384]{2,1,0:T(1,128)} %reshape.936), calls=%async_computation | async-start | bytes 24576 | tf_op jit(solution)/shard_map/all_to_all | solution.py:112
  15.4 9.2 %collective-permute-start.1 = (f32[2,32,8,3]{2,1,3,0:T(8,128)S(1)}, f32[2,32,8,3]{2,1,3,0:T(8,128)S(1)}, u32[]{:S(2)}, u32[]{:S(2)}) collective-permute-start(f32[2,32,8,3]{2,1,3,0:T(8,128)S(1)} %bitcast.414), channel_id=1, source_target_pairs={{8,0},{16,8},{24,16},{32,24},{40,32},{48,40},{56,48},{64,56},{72,6... | collective-permute-start | bytes 18440 | tf_op jit(solution)/shard_map/ppermute | solution.py:13
  19.5 5.9 %collective-permute-start = (f32[2,32,8,3]{2,1,3,0:T(8,128)S(1)}, f32[2,32,8,3]{2,1,3,0:T(8,128)S(1)}, u32[]{:S(2)}, u32[]{:S(2)}) collective-permute-start(f32[2,32,8,3]{2,1,3,0:T(8,128)S(1)} %bitcast.415), channel_id=1, source_target_pairs={{0,8},{8,16},{16,24},{24,32},{32,40},{40,48},{48,56},{56,64},{64,7... | collective-permute-start | bytes 18440 | tf_op jit(solution)/shard_map/ppermute | solution.py:13
  30.4 2.2 %slice-start = ((s8[5734400]{0:T(1024)(128)(4,1)}), s8[4194304]{0:T(1024)(128)(4,1)S(1)}, s32[]{:S(2)}) async-start(s8[5734400]{0:T(1024)(128)(4,1)} %bitcast.417), calls=%async_computation.4 | async-start | bytes 8388608
  30.8 2.4 %slice-start.1 = ((s8[5734400]{0:T(1024)(128)(4,1)}), s8[1540096]{0:T(1024)(128)(4,1)S(1)}, s32[]{:S(2)}) async-start(s8[5734400]{0:T(1024)(128)(4,1)} %bitcast.417), calls=%async_computation.5 | async-start | bytes 3080192
  45.8 0.8 copy-start
  46.4 6.7 %copy-start.1 = (bf16[25,4,32,24,50]{4,3,2,1,0:T(8,128)(2,1)}, bf16[25,4,32,24,50]{4,3,2,1,0:T(8,128)(2,1)S(1)}, u32[]{:S(2)}) copy-start(bf16[25,4,32,24,50]{4,3,2,1,0:T(8,128)(2,1)S(1)} %fusion.6) | copy-start | bytes 23040004
  58.4 8.5 %all-to-all-start.1 = ((bf16[8,4,4,148]{3,2,1,0:T(4,128)(2,1)}), bf16[8,4,4,148]{3,2,1,0:T(4,128)(2,1)S(1)}, u32[]{:S(2)}, u32[]{:S(2)}) async-start(bf16[8,4,4,148]{3,2,1,0:T(4,128)(2,1)} %constant_dynamic-update-slice_fusion.25), calls=%async_computation.1 | async-start | bytes 131072 | tf_op jit(solution)/shard_map/all_to_all | solution.py:139

commit v3 on v2

--- a/solution.py
+++ b/solution.py
@@ -5,10 +5,15 @@
 
 BINS = 50
 SHIFTS = 24
+PX = ("pxa", "pxc")
+
+
+def px_index():
+    return lax.axis_index("pxa") * 2 + lax.axis_index("pxc")
 
 
 def passed_along(block, axis, distance):
-    devices = range(lax.axis_size(axis))
+    devices = range(lax.axis_size("pxa") * 2)
     route = [(i - distance, i) for i in devices if i - distance in devices]
     return lax.ppermute(block, axis, route)
 
@@ -51,6 +56,27 @@
     return every.reshape(buf.shape)[:rows]
 
 
+def chip_sum(value):
+    count = lax.axis_size("pxa")
+    core = lax.axis_index("pxc")
+    swap = [(0, 1), (1, 0)]
+    rows = value.shape[0]
+    unit = -(-rows // (2 * count))
+    buf = jnp.pad(value, ((0, 2 * unit * count - rows),) + ((0, 0),) * (value.ndim - 1))
+    half = unit * count
+    keep = lax.dynamic_slice_in_dim(buf, core * half, half, 0)
+    send = lax.dynamic_slice_in_dim(buf, (1 - core) * half, half, 0)
+    part = keep + lax.ppermute(send, "pxc", swap)
+    pieces = part.reshape((count, unit) + value.shape[1:])
+    mine = jnp.sum(lax.all_to_all(pieces, "pxa", 0, 0), axis=0).astype(jnp.bfloat16)
+    spread = jnp.broadcast_to(mine[None], pieces.shape)
+    ours = lax.all_to_all(spread, "pxa", 0, 0).reshape((half,) + value.shape[1:])
+    theirs = lax.ppermute(ours, "pxc", swap)
+    low = jnp.where(core == 0, ours, theirs)
+    high = jnp.where(core == 0, theirs, ours)
+    return jnp.concatenate([low, high], axis=0)[:rows].astype(jnp.float32)
+
+
 def bin_charges(charge, hit_bins, hit_ticks):
     tick_hot = (hit_ticks[..., None] == jnp.arange(SHIFTS, dtype=jnp.int32)).astype(jnp.float32)
     bin_hot = (hit_bins[..., None] == jnp.arange(BINS, dtype=jnp.int32)).astype(jnp.float32)
@@ -102,7 +128,7 @@
     share = ticks // parts_y
     span = share + SHIFTS - 1
     weights = table.astype(jnp.bfloat16)
-    row_start = lax.axis_index("px") * tile_x
+    row_start = px_index() * tile_x
     col_start = lax.axis_index("py") * tile_y
 
     deposits = jnp.stack(
@@ -111,8 +137,8 @@
     spread = jnp.broadcast_to(deposits[None], (parts_y,) + deposits.shape)
     band = jnp.transpose(lax.all_to_all(spread, "py", 0, 0), (1, 0, 2, 3, 4))
     band = band.reshape((tile_x, parts_y * tile_y) + deposits.shape[2:])
-    above = passed_along(band[tile_x - 2 :], "px", 1)
-    below = passed_along(band[:2], "px", -1)
+    above = passed_along(band[tile_x - 2 :], PX, 1)
+    below = passed_along(band[:2], PX, -1)
     wide = jnp.concatenate([above, band, below], axis=0)
     binned = bin_charges(
         wide[..., 0], wide[..., 1].astype(jnp.int32), wide[..., 2].astype(jnp.int32)
@@ -147,7 +173,7 @@
         preferred_element_type=jnp.float32,
     )
     flat = gradient.reshape(-1, share)
-    summed = exchange_sum(flat, "px").reshape(gradient.shape)
+    summed = chip_sum(flat).reshape(gradient.shape)
     return (prediction.astype(jnp.bfloat16), summed / 16)
 
 
@@ -163,6 +189,15 @@
         P(),
     )
     out_specs = (P("px", "py", None), P(None, None, "py"))
+    rows_of = mesh.shape["px"]
+    split = jax.sharding.Mesh(
+        mesh.devices.reshape((rows_of // 2, 2) + mesh.devices.shape[1:]), ("pxa", "pxc", "py")
+    )
+    rename = lambda spec: P(*[PX if part == "px" else part for part in spec])
     return jax.shard_map(
-        on_device, mesh=mesh, in_specs=in_specs, out_specs=out_specs, check_vma=False
-    )
+        on_device,
+        mesh=split,
+        in_specs=tuple(rename(spec) for spec in in_specs),
+        out_specs=tuple(rename(spec) for spec in out_specs),
+        check_vma=False,
+    )

time: 144 us -> 131 us (0.910)
  blocking collectives: 58.6 us -> 40.8 us
  waiting for transfers between devices: 5.97 us -> 8.62 us
  starting transfers between devices: 17.6 us -> 19.9 us
    all_to_all x2, blocking collectives: 58.6 us -> 40.8 us  [the longest x1 26.7 us: chip_sum(): lax.all_to_all(pieces, 'pxa', 0, 0)]
    ppermute x0 -> x2, waiting for transfers between devices: none -> 2.64 us  [the longest x1 1.61 us: chip_sum(): part = keep + lax.ppermute(send, 'pxc', swap)]
    ppermute x0 -> x2, starting transfers between devices: none -> 2.32 us  [the longest x1 2.22 us: chip_sum(): theirs = lax.ppermute(ours, 'pxc', swap)]
  transfers between devices with their start and end apart: 4 -> 6, of which waited for: 3 -> 5; matrix products, arithmetic and copies ran while one was open for 4% -> 4% of each run, Pallas kernels for 0% -> 0%
where the time goes in v3:
time: 131 us; the launch traced here: 130 us
  blocking collectives  40.8 us (31%)
  local copies, waits for them, and re-layouts  24 us (18%)
  starting transfers between devices  19.9 us (15%)
  other arithmetic  18.3 us (14%)
  matrix products  17.4 us (13%)
  waiting for transfers between devices  8.62 us (7%)
  between operations  1.48 us (1%)
    all_to_all x1, blocking collectives, chip_sum(): lax.all_to_all(pieces, 'pxa', 0, 0)  26.7 us
    all_to_all x1, blocking collectives, chip_sum(): lax.all_to_all(spread, 'pxa', 0, 0).reshape((half,) + value.shape[1:])  14.1 us
    unnamed x44, local copies, waits for them, and re-layouts  13.5 us
    dot_general x1, matrix products, on_device(): jnp.einsum('oxysb,xysu->obu', stacked_band, windows(band_resid, share), p...  11.9 us
    unnamed x47, other arithmetic  10.9 us
    ppermute x2, starting transfers between devices, passed_along(): return lax.ppermute(block, axis, route)  8.27 us
    all_to_all x1, starting transfers between devices, on_device(): band = jnp.transpose(lax.all_to_all(spread, 'py', 0, 0), (1, 0, 2, 3, 4))  5.94 us
    another operation x27, local copies, waits for them, and re-layouts, windows(): jnp.stack([resid[:, :, offset:offset + ticks] for offset in range(SHIFTS)...  4.37 us
  transfers between devices with their start and end apart: 6, of which 5 were waited for; matrix products, arithmetic and copies ran while one was open for 4% of the time, Pallas kernels for 0%

profile of v3, /device:TPU:1, one launch (start us, length us, event | category | flops | bytes accessed | tf_op | source)
XLA Modules:
  0.0 130.5 jit_solution(3796368701419380441)
XLA Ops:
  0.6 0.7 convert_bitcast_fusion
  1.3 0.7 pad_maximum_fusion.2
  2.1 0.8 reshape.938
  2.9 5.9 %all-to-all-start = ((f32[8,1,384]{2,1,0:T(1,128)}), f32[8,1,384]{2,1,0:T(1,128)S(1)}, u32[]{:S(2)}, u32[]{:S(2)}) async-start(f32[8,1,384]{2,1,0:T(1,128)} %reshape.938), calls=%async_computation | async-start | bytes 24576 | tf_op jit(solution)/shard_map/all_to_all | solution.py:138
  8.8 0.7 pad_dynamic-slice_fusion.2
  9.6 0.7 pad_dynamic-slice_fusion.3
  10.5 0.9 slice_compare_fusion
  11.4 2.5 %all-to-all-done = f32[8,1,384]{2,1,0:T(1,128)S(1)} async-done(((f32[8,1,384]{2,1,0:T(1,128)}), f32[8,1,384]{2,1,0:T(1,128)S(1)}, u32[]{:S(2)}, u32[]{:S(2)}) %all-to-all-start) | async-done | bytes 12320 | tf_op jit(solution)/shard_map/all_to_all | solution.py:138
  13.9 0.5 broadcast.908
  14.4 0.7 reduce
  15.4 4.0 %collective-permute-start.1 = (f32[2,32,8,3]{2,1,3,0:T(8,128)S(1)}, f32[2,32,8,3]{2,1,3,0:T(8,128)S(1)}, u32[]{:S(2)}, u32[]{:S(2)}) collective-permute-start(f32[2,32,8,3]{2,1,3,0:T(8,128)S(1)} %bitcast.416), channel_id=1, source_target_pairs={{8,0},{16,8},{24,16},{32,24},{40,32},{48,40},{56,48},{64,56},{72,6... | collective-permute-start | bytes 18440 | tf_op jit(solution)/shard_map/ppermute | solution.py:18
  19.5 4.3 %collective-permute-start = (f32[2,32,8,3]{2,1,3,0:T(8,128)S(1)}, f32[2,32,8,3]{2,1,3,0:T(8,128)S(1)}, u32[]{:S(2)}, u32[]{:S(2)}) collective-permute-start(f32[2,32,8,3]{2,1,3,0:T(8,128)S(1)} %bitcast.417), channel_id=1, source_target_pairs={{0,8},{8,16},{16,24},{24,32},{32,40},{40,48},{48,56},{56,64},{64,7... | collective-permute-start | bytes 18440 | tf_op jit(solution)/shard_map/ppermute | solution.py:18
  23.8 0.7 convert_element_type.104
  24.7 0.6 collective-permute-done
  25.8 2.9 %convolution_convert_fusion = bf16[8,32,24,50]{3,2,1,0:T(8,128)(2,1)S(1)} fusion(s32[8,32,8]{2,1,0:T(8,128)S(1)} %copy.148, bf16[8,32,8]{2,1,0:T(8,128)(2,1)S(1)} %copy.147, s32[8,32,8]{2,1,0:T(8,128)S(1)} %copy.146), kind=kOutput, calls=%fused_computation.4 | convolution fusion | flops 5115904 | bytes 634880 | tf_op jit(solution)/shard_map/xyks,xykb->xysb/dot_general | solution.py:84
  31.3 1.3 slice-done
  32.6 0.6 slice-done.1
  33.2 2.6 %fusion = f32[4,4,24,1000,1]{3,2,0,1,4:T(8,128)S(1)} fusion(f32[25,50,1000]{2,1,0:T(8,128)S(1)} %bitcast.420, bf16[25,4,4,24,50]{4,3,2,1,0:T(8,128)(2,1)S(1)} %constant_dynamic-update-slice_fusion), kind=kOutput, calls=%fused_computation | convolution fusion | flops 961249984 | bytes 7496000 | tf_op jit(solution)/shard_map/oxysb,obt->xyst/dot_general | solution.py:156
  36.0 0.3 fusion.48
  36.3 1.2 fusion.47
  39.1 0.3 bitcast_dynamic-update-slice_fusion.18
  39.4 0.3 fusion.13
  39.7 0.3 bitcast_dynamic-update-slice_fusion.17
  40.1 0.3 bitcast_dynamic-update-slice_fusion.16
  40.4 0.3 bitcast_dynamic-update-slice_fusion.15
  40.7 0.3 bitcast_dynamic-update-slice_fusion.14
  41.1 0.3 fusion.11
  41.4 0.3 bitcast_dynamic-update-slice_fusion.13
  41.7 0.3 bitcast_dynamic-update-slice_fusion.12
  42.1 0.3 bitcast_dynamic-update-slice_fusion.11
  42.4 0.3 bitcast_dynamic-update-slice_fusion.10
  42.9 0.3 bitcast_dynamic-update-slice_fusion.9
  43.2 0.3 bitcast_dynamic-update-slice_fusion.8
  43.6 0.3 bitcast_dynamic-update-slice_fusion.7
  43.9 0.3 bitcast_dynamic-update-slice_fusion.6
  44.3 0.3 fusion.8
  44.6 0.3 bitcast_dynamic-update-slice_fusion.5
  44.9 0.3 bitcast_dynamic-update-slice_fusion.4
  45.3 0.5 bitcast_dynamic-update-slice_fusion.3
  45.8 0.3 bitcast_dynamic-update-slice_fusion.2
  46.1 0.3 fusion.6
  46.5 2.0 %multiply_convert_fusion = (bf16[4,4,1024]{2,1,0:T(4,128)(2,1)S(1)}, bf16[4,4,1024]{2,1,0:T(4,128)(2,1)}) fusion(bf16[4,4,1024]{2,1,0:T(4,128)(2,1)S(1)} %copy-done, f32[4,4]{1,0:T(4,128)S(1)} %convert_element_type.104, f32[4,4,1000]{2,1,0:T(4,128)S(1)} %bitcast.391, f32[4,4,1000]{2,1,0:T(4,128)S(1)} %bitcast.392, f32[4,4,1000]{2,1,0:T(4,128)S(1)} %bitcast.393, ...), kind=kLoop, calls=%fused_computation.163 | loop fusion | flops 458752 | bytes 1634368 | tf_op jit(solution)/shard_map/convert_element_type | solution.py:121
  48.6 4.5 %copy-done.1 = bf16[25,4,32,24,50]{4,3,2,1,0:T(8,128)(2,1)} copy-done((bf16[25,4,32,24,50]{4,3,2,1,0:T(8,128)(2,1)}, bf16[25,4,32,24,50]{4,3,2,1,0:T(8,128)(2,1)S(1)}, u32[]{:S(2)}) %copy-start.1) | copy-done | bytes 7680024
  53.1 0.6 constant_dynamic-update-slice_fusion.32
  53.7 0.7 constant_dynamic-update-slice_fusion.31
  54.4 0.7 constant_dynamic-update-slice_fusion.30
  55.1 0.7 constant_dynamic-update-slice_fusion.29
  55.7 0.7 constant_dynamic-update-slice_fusion.28
  56.4 0.7 constant_dynamic-update-slice_fusion.27
  57.1 0.7 constant_dynamic-update-slice_fusion.26
  57.8 0.7 constant_dynamic-update-slice_fusion.25
  58.4 3.4 %all-to-all-start.1 = ((bf16[8,4,4,148]{3,2,1,0:T(4,128)(2,1)}), bf16[8,4,4,148]{3,2,1,0:T(4,128)(2,1)S(1)}, u32[]{:S(2)}, u32[]{:S(2)}) async-start(bf16[8,4,4,148]{3,2,1,0:T(4,128)(2,1)} %constant_dynamic-update-slice_fusion.25), calls=%async_computation.1 | async-start | bytes 131072 | tf_op jit(solution)/shard_map/all_to_all | solution.py:165
  61.8 1.1 bitcast_dynamic-update-slice_fusion.1
  62.9 1.1 bitcast_dynamic-update-slice_fusion
  64.1 2.9 %all-to-all-done.1 = bf16[8,4,4,148]{3,2,1,0:T(4,128)(2,1)S(1)} async-done(((bf16[8,4,4,148]{3,2,1,0:T(4,128)(2,1)}), bf16[8,4,4,148]{3,2,1,0:T(4,128)(2,1)S(1)}, u32[]{:S(2)}, u32[]{:S(2)}) %all-to-all-start.1) | async-done | bytes 37920 | tf_op jit(solution)/shard_map/all_to_all | solution.py:165
  67.1 0.4 slice_bitcast_fusion.1
  68.9 2.6 %stack.359 = bf16[4,32,24,125]{3,2,1,0:T(8,128)(2,1)S(1)} concatenate(bf16[4,32,1,125]{3,2,1,0:T(2,128)(2,1)S(1)} %copy.197, bf16[4,32,1,125]{3,2,1,0:T(2,128)(2,1)S(1)} %copy.198, bf16[4,32,1,125]{3,2,1,0:T(2,128)(2,1)S(1)} %copy.199, bf16[4,32,1,125]{3,2,1,0:T(2,128)(2,1)S(1)} %copy.200, bf16[4,32,1,125]{3,2,1,0:T(2,128)(2,1)S(1)} %copy.201, ...), dimensions={2} | concatenate | bytes 1536000 | tf_op jit(solution)/shard_map/stack | solution.py:115
  71.5 11.9 %convolution_bitcast_fusion = f32[25,50,125]{2,1,0:T(8,128)S(1)} fusion(bf16[25,4,32,24,50]{4,3,2,1,0:T(8,128)(2,1)} %bitcast_dynamic-update-slice_fusion, bf16[4,32,24,125]{3,2,1,0:T(8,128)(2,1)S(1)} %stack.359), kind=kOutput, calls=%fused_computation.6 | convolution fusion | flops 960000000 | bytes 9073000 | tf_op jit(solution)/shard_map/oxysb,xysu->obu/dot_general | solution.py:169
  83.6 1.6 %collective-permute-done.2 = f32[640,125]{1,0:T(8,128)S(1)} collective-permute-done((f32[640,125]{1,0:T(8,128)S(1)}, f32[640,125]{1,0:T(8,128)S(1)}, u32[]{:S(2)}, u32[]{:S(2)}) %collective-permute-start.2) | collective-permute-done | bytes 320032 | tf_op jit(solution)/shard_map/ppermute | solution.py:69
  85.3 26.7 %all_to_all.20 = f32[16,40,125]{2,1,0:T(8,128)S(1)} all-to-all(f32[16,40,125]{2,1,0:T(8,128)S(1)} %bitcast.388), channel_id=1, replica_groups=mesh['pxa'=16,'pxc'=2,'py'=8] {'pxa'}, dimensions={0} | all-to-all | bytes 640000 | tf_op jit(solution)/shard_map/all_to_all | solution.py:71
  112.1 14.1 %all_to_all.21 = bf16[16,40,125]{2,1,0:T(8,128)(2,1)S(1)} all-to-all(bf16[16,40,125]{2,1,0:T(8,128)(2,1)S(1)} %broadcast_in_dim.526), channel_id=1, replica_groups=mesh['pxa'=16,'pxc'=2,'py'=8] {'pxa'}, dimensions={0} | all-to-all | bytes 320000 | tf_op jit(solution)/shard_map/all_to_all | solution.py:73
  126.2 2.2 %collective-permute-start.3 = (bf16[640,125]{1,0:T(8,128)(2,1)S(1)}, bf16[640,125]{1,0:T(8,128)(2,1)S(1)}, u32[]{:S(2)}, u32[]{:S(2)}) collective-permute-start(bf16[640,125]{1,0:T(8,128)(2,1)S(1)} %bitcast.390), channel_id=1, source_target_pairs={{0,8},{8,0},{1,9},{9,1},{2,10},{10,2},{3,11},{11,3},{4,12},{12,4},... | collective-permute-start | bytes 480008 | tf_op jit(solution)/shard_map/ppermute | solution.py:74
  128.4 1.0 collective-permute-done.3
  129.6 0.9 div.10
  (113 shorter events, 7.5 us)
Async XLA Ops:
  2.9 11.0 %all-to-all-start = ((f32[8,1,384]{2,1,0:T(1,128)}), f32[8,1,384]{2,1,0:T(1,128)S(1)}, u32[]{:S(2)}, u32[]{:S(2)}) async-start(f32[8,1,384]{2,1,0:T(1,128)} %reshape.938), calls=%async_computation | async-start | bytes 24576 | tf_op jit(solution)/shard_map/all_to_all | solution.py:138
  15.4 9.2 %collective-permute-start.1 = (f32[2,32,8,3]{2,1,3,0:T(8,128)S(1)}, f32[2,32,8,3]{2,1,3,0:T(8,128)S(1)}, u32[]{:S(2)}, u32[]{:S(2)}) collective-permute-start(f32[2,32,8,3]{2,1,3,0:T(8,128)S(1)} %bitcast.416), channel_id=1, source_target_pairs={{8,0},{16,8},{24,16},{32,24},{40,32},{48,40},{56,48},{64,56},{72,6... | collective-permute-start | bytes 18440 | tf_op jit(solution)/shard_map/ppermute | solution.py:18
  19.5 5.9 %collective-permute-start = (f32[2,32,8,3]{2,1,3,0:T(8,128)S(1)}, f32[2,32,8,3]{2,1,3,0:T(8,128)S(1)}, u32[]{:S(2)}, u32[]{:S(2)}) collective-permute-start(f32[2,32,8,3]{2,1,3,0:T(8,128)S(1)} %bitcast.417), channel_id=1, source_target_pairs={{0,8},{8,16},{16,24},{24,32},{32,40},{40,48},{48,56},{56,64},{64,7... | collective-permute-start | bytes 18440 | tf_op jit(solution)/shard_map/ppermute | solution.py:18
  30.4 2.2 %slice-start = ((s8[5734400]{0:T(1024)(128)(4,1)}), s8[4194304]{0:T(1024)(128)(4,1)S(1)}, s32[]{:S(2)}) async-start(s8[5734400]{0:T(1024)(128)(4,1)} %bitcast.419), calls=%async_computation.4 | async-start | bytes 8388608
  30.8 2.4 %slice-start.1 = ((s8[5734400]{0:T(1024)(128)(4,1)}), s8[1540096]{0:T(1024)(128)(4,1)S(1)}, s32[]{:S(2)}) async-start(s8[5734400]{0:T(1024)(128)(4,1)} %bitcast.419), calls=%async_computation.5 | async-start | bytes 3080192
  45.8 0.8 copy-start
  46.4 6.7 %copy-start.1 = (bf16[25,4,32,24,50]{4,3,2,1,0:T(8,128)(2,1)}, bf16[25,4,32,24,50]{4,3,2,1,0:T(8,128)(2,1)S(1)}, u32[]{:S(2)}) copy-start(bf16[25,4,32,24,50]{4,3,2,1,0:T(8,128)(2,1)S(1)} %fusion.6) | copy-start | bytes 23040004
  58.4 8.5 %all-to-all-start.1 = ((bf16[8,4,4,148]{3,2,1,0:T(4,128)(2,1)}), bf16[8,4,4,148]{3,2,1,0:T(4,128)(2,1)S(1)}, u32[]{:S(2)}, u32[]{:S(2)}) async-start(bf16[8,4,4,148]{3,2,1,0:T(4,128)(2,1)} %constant_dynamic-update-slice_fusion.25), calls=%async_computation.1 | async-start | bytes 131072 | tf_op jit(solution)/shard_map/all_to_all | solution.py:165
  83.5 1.7 %collective-permute-start.2 = (f32[640,125]{1,0:T(8,128)S(1)}, f32[640,125]{1,0:T(8,128)S(1)}, u32[]{:S(2)}, u32[]{:S(2)}) collective-permute-start(f32[640,125]{1,0:T(8,128)S(1)} %pad_dynamic-slice_fusion), channel_id=1, source_target_pairs={{0,8},{8,0},{1,9},{9,1},{2,10},{10,2},{3,11},{11,3},{4,12},{12,4},... | collective-permute-start | bytes 960008 | tf_op jit(solution)/shard_map/ppermute | solution.py:69
  126.2 3.3 %collective-permute-start.3 = (bf16[640,125]{1,0:T(8,128)(2,1)S(1)}, bf16[640,125]{1,0:T(8,128)(2,1)S(1)}, u32[]{:S(2)}, u32[]{:S(2)}) collective-permute-start(bf16[640,125]{1,0:T(8,128)(2,1)S(1)} %bitcast.390), channel_id=1, source_target_pairs={{0,8},{8,0},{1,9},{9,1},{2,10},{10,2},{3,11},{11,3},{4,12},{12,4},... | collective-permute-start | bytes 480008 | tf_op jit(solution)/shard_map/ppermute | solution.py:74

commit v4 on v3

--- a/solution.py
+++ b/solution.py
@@ -67,8 +67,9 @@
     keep = lax.dynamic_slice_in_dim(buf, core * half, half, 0)
     send = lax.dynamic_slice_in_dim(buf, (1 - core) * half, half, 0)
     part = keep + lax.ppermute(send, "pxc", swap)
-    pieces = part.reshape((count, unit) + value.shape[1:])
-    mine = jnp.sum(lax.all_to_all(pieces, "pxa", 0, 0), axis=0).astype(jnp.bfloat16)
+    pieces = part.reshape((count, unit) + value.shape[1:]).astype(jnp.bfloat16)
+    got = lax.all_to_all(pieces, "pxa", 0, 0).astype(jnp.float32)
+    mine = jnp.sum(got, axis=0).astype(jnp.bfloat16)
     spread = jnp.broadcast_to(mine[None], pieces.shape)
     ours = lax.all_to_all(spread, "pxa", 0, 0).reshape((half,) + value.shape[1:])
     theirs = lax.ppermute(ours, "pxc", swap)

time: 131 us -> 128 us (0.977)
  blocking collectives: 40.8 us -> 36.3 us
    all_to_all x1, blocking collectives: 26.7 us -> 23.5 us  [chip_sum(): got = lax.all_to_all(pieces, 'pxa', 0, 0).astype(jnp.float32)]
  transfers between devices with their start and end apart: 6 -> 6, of which waited for: 5 -> 5; matrix products, arithmetic and copies ran while one was open for 4% -> 5% of each run, Pallas kernels for 0% -> 0%
where the time goes in v4:
time: 128 us; the launch traced here: 127 us
  blocking collectives  36.3 us (28%)
  local copies, waits for them, and re-layouts  24 us (19%)
  starting transfers between devices  21 us (16%)
  other arithmetic  18.4 us (14%)
  matrix products  17.4 us (14%)
  waiting for transfers between devices  8.62 us (7%)
  between operations  1.48 us (1%)
    all_to_all x1, blocking collectives, chip_sum(): got = lax.all_to_all(pieces, 'pxa', 0, 0).astype(jnp.float32)  23.5 us
    unnamed x44, local copies, waits for them, and re-layouts  13.5 us
    all_to_all x1, blocking collectives, chip_sum(): lax.all_to_all(spread, 'pxa', 0, 0).reshape((half,) + value.shape[1:])  12.9 us
    dot_general x1, matrix products, on_device(): jnp.einsum('oxysb,xysu->obu', stacked_band, windows(band_resid, share), p...  11.9 us
    unnamed x47, other arithmetic  10.9 us
    ppermute x2, starting transfers between devices, passed_along(): return lax.ppermute(block, axis, route)  8.27 us
    all_to_all x1, starting transfers between devices, on_device(): band = jnp.transpose(lax.all_to_all(spread, 'py', 0, 0), (1, 0, 2, 3, 4))  5.94 us
    another operation x27, local copies, waits for them, and re-layouts, windows(): jnp.stack([resid[:, :, offset:offset + ticks] for offset in range(SHIFTS)...  4.37 us
  transfers between devices with their start and end apart: 6, of which 5 were waited for; matrix products, arithmetic and copies ran while one was open for 5% of the time, Pallas kernels for 0%

profile of v4, /device:TPU:1, one launch (start us, length us, event | category | flops | bytes accessed | tf_op | source)
XLA Modules:
  0.0 127.2 jit_solution(9537517125860591846)
XLA Ops:
  0.6 0.7 convert_bitcast_fusion
  1.3 0.7 pad_maximum_fusion.2
  2.1 0.8 reshape.934
  2.9 5.9 %all-to-all-start = ((f32[8,1,384]{2,1,0:T(1,128)}), f32[8,1,384]{2,1,0:T(1,128)S(1)}, u32[]{:S(2)}, u32[]{:S(2)}) async-start(f32[8,1,384]{2,1,0:T(1,128)} %reshape.934), calls=%async_computation | async-start | bytes 24576 | tf_op jit(solution)/shard_map/all_to_all | solution.py:139
  8.8 0.7 pad_dynamic-slice_fusion.2
  9.6 0.7 pad_dynamic-slice_fusion.3
  10.5 0.9 slice_compare_fusion
  11.4 2.5 %all-to-all-done = f32[8,1,384]{2,1,0:T(1,128)S(1)} async-done(((f32[8,1,384]{2,1,0:T(1,128)}), f32[8,1,384]{2,1,0:T(1,128)S(1)}, u32[]{:S(2)}, u32[]{:S(2)}) %all-to-all-start) | async-done | bytes 12320 | tf_op jit(solution)/shard_map/all_to_all | solution.py:139
  13.9 0.5 broadcast.908
  14.4 0.7 reduce.1
  15.4 4.0 %collective-permute-start.1 = (f32[2,32,8,3]{2,1,3,0:T(8,128)S(1)}, f32[2,32,8,3]{2,1,3,0:T(8,128)S(1)}, u32[]{:S(2)}, u32[]{:S(2)}) collective-permute-start(f32[2,32,8,3]{2,1,3,0:T(8,128)S(1)} %bitcast.416), channel_id=1, source_target_pairs={{8,0},{16,8},{24,16},{32,24},{40,32},{48,40},{56,48},{64,56},{72,6... | collective-permute-start | bytes 18440 | tf_op jit(solution)/shard_map/ppermute | solution.py:18
  19.5 4.3 %collective-permute-start = (f32[2,32,8,3]{2,1,3,0:T(8,128)S(1)}, f32[2,32,8,3]{2,1,3,0:T(8,128)S(1)}, u32[]{:S(2)}, u32[]{:S(2)}) collective-permute-start(f32[2,32,8,3]{2,1,3,0:T(8,128)S(1)} %bitcast.417), channel_id=1, source_target_pairs={{0,8},{8,16},{16,24},{24,32},{32,40},{40,48},{48,56},{56,64},{64,7... | collective-permute-start | bytes 18440 | tf_op jit(solution)/shard_map/ppermute | solution.py:18
  23.8 0.7 convert_element_type.105
  24.7 0.6 collective-permute-done
  25.8 2.9 %convolution_convert_fusion = bf16[8,32,24,50]{3,2,1,0:T(8,128)(2,1)S(1)} fusion(s32[8,32,8]{2,1,0:T(8,128)S(1)} %copy.148, bf16[8,32,8]{2,1,0:T(8,128)(2,1)S(1)} %copy.147, s32[8,32,8]{2,1,0:T(8,128)S(1)} %copy.146), kind=kOutput, calls=%fused_computation.4 | convolution fusion | flops 5115904 | bytes 634880 | tf_op jit(solution)/shard_map/xyks,xykb->xysb/dot_general | solution.py:85
  31.3 1.3 %slice-done = s8[4194304]{0:T(1024)(128)(4,1)S(1)} async-done(((s8[5734400]{0:T(1024)(128)(4,1)}), s8[4194304]{0:T(1024)(128)(4,1)S(1)}, s32[]{:S(2)}) %slice-start) | async-done | bytes 4194328
  32.6 0.6 slice-done.1
  33.2 2.6 %fusion = f32[4,4,24,1000,1]{3,2,0,1,4:T(8,128)S(1)} fusion(f32[25,50,1000]{2,1,0:T(8,128)S(1)} %bitcast.420, bf16[25,4,4,24,50]{4,3,2,1,0:T(8,128)(2,1)S(1)} %constant_dynamic-update-slice_fusion), kind=kOutput, calls=%fused_computation | convolution fusion | flops 961249984 | bytes 7496000 | tf_op jit(solution)/shard_map/oxysb,obt->xyst/dot_general | solution.py:157
  36.0 0.3 fusion.49
  36.3 1.2 fusion.48
  39.1 0.3 bitcast_dynamic-update-slice_fusion.18
  39.4 0.3 fusion.13
  39.7 0.3 bitcast_dynamic-update-slice_fusion.17
  40.1 0.3 bitcast_dynamic-update-slice_fusion.16
  40.4 0.3 bitcast_dynamic-update-slice_fusion.15
  40.7 0.3 bitcast_dynamic-update-slice_fusion.14
  41.1 0.3 fusion.11
  41.4 0.3 bitcast_dynamic-update-slice_fusion.13
  41.7 0.3 bitcast_dynamic-update-slice_fusion.12
  42.1 0.3 bitcast_dynamic-update-slice_fusion.11
  42.4 0.3 bitcast_dynamic-update-slice_fusion.10
  42.9 0.3 bitcast_dynamic-update-slice_fusion.9
  43.2 0.3 bitcast_dynamic-update-slice_fusion.8
  43.6 0.3 bitcast_dynamic-update-slice_fusion.7
  43.9 0.3 bitcast_dynamic-update-slice_fusion.6
  44.3 0.3 fusion.8
  44.6 0.3 bitcast_dynamic-update-slice_fusion.5
  44.9 0.3 bitcast_dynamic-update-slice_fusion.4
  45.3 0.5 bitcast_dynamic-update-slice_fusion.3
  45.8 0.3 bitcast_dynamic-update-slice_fusion.2
  46.1 0.3 fusion.6
  46.5 2.0 %multiply_convert_fusion = (bf16[4,4,1024]{2,1,0:T(4,128)(2,1)S(1)}, bf16[4,4,1024]{2,1,0:T(4,128)(2,1)}) fusion(bf16[4,4,1024]{2,1,0:T(4,128)(2,1)S(1)} %copy-done, f32[4,4]{1,0:T(4,128)S(1)} %convert_element_type.105, f32[4,4,1000]{2,1,0:T(4,128)S(1)} %bitcast.391, f32[4,4,1000]{2,1,0:T(4,128)S(1)} %bitcast.392, f32[4,4,1000]{2,1,0:T(4,128)S(1)} %bitcast.393, ...), kind=kLoop, calls=%fused_computation.164 | loop fusion | flops 458752 | bytes 1634368 | tf_op jit(solution)/shard_map/convert_element_type | solution.py:122
  48.6 4.5 %copy-done.1 = bf16[25,4,32,24,50]{4,3,2,1,0:T(8,128)(2,1)} copy-done((bf16[25,4,32,24,50]{4,3,2,1,0:T(8,128)(2,1)}, bf16[25,4,32,24,50]{4,3,2,1,0:T(8,128)(2,1)S(1)}, u32[]{:S(2)}) %copy-start.1) | copy-done | bytes 7680024
  53.1 0.6 constant_dynamic-update-slice_fusion.32
  53.7 0.7 constant_dynamic-update-slice_fusion.31
  54.4 0.7 constant_dynamic-update-slice_fusion.30
  55.1 0.7 constant_dynamic-update-slice_fusion.29
  55.7 0.7 constant_dynamic-update-slice_fusion.28
  56.4 0.7 constant_dynamic-update-slice_fusion.27
  57.1 0.7 constant_dynamic-update-slice_fusion.26
  57.8 0.7 constant_dynamic-update-slice_fusion.25
  58.4 3.4 %all-to-all-start.1 = ((bf16[8,4,4,148]{3,2,1,0:T(4,128)(2,1)}), bf16[8,4,4,148]{3,2,1,0:T(4,128)(2,1)S(1)}, u32[]{:S(2)}, u32[]{:S(2)}) async-start(bf16[8,4,4,148]{3,2,1,0:T(4,128)(2,1)} %constant_dynamic-update-slice_fusion.25), calls=%async_computation.1 | async-start | bytes 131072 | tf_op jit(solution)/shard_map/all_to_all | solution.py:166
  61.8 1.1 bitcast_dynamic-update-slice_fusion.1
  62.9 1.1 bitcast_dynamic-update-slice_fusion
  64.1 2.9 %all-to-all-done.1 = bf16[8,4,4,148]{3,2,1,0:T(4,128)(2,1)S(1)} async-done(((bf16[8,4,4,148]{3,2,1,0:T(4,128)(2,1)}), bf16[8,4,4,148]{3,2,1,0:T(4,128)(2,1)S(1)}, u32[]{:S(2)}, u32[]{:S(2)}) %all-to-all-start.1) | async-done | bytes 37920 | tf_op jit(solution)/shard_map/all_to_all | solution.py:166
  67.1 0.4 slice_bitcast_fusion.1
  68.9 2.6 %stack.359 = bf16[4,32,24,125]{3,2,1,0:T(8,128)(2,1)S(1)} concatenate(bf16[4,32,1,125]{3,2,1,0:T(2,128)(2,1)S(1)} %copy.197, bf16[4,32,1,125]{3,2,1,0:T(2,128)(2,1)S(1)} %copy.198, bf16[4,32,1,125]{3,2,1,0:T(2,128)(2,1)S(1)} %copy.199, bf16[4,32,1,125]{3,2,1,0:T(2,128)(2,1)S(1)} %copy.200, bf16[4,32,1,125]{3,2,1,0:T(2,128)(2,1)S(1)} %copy.201, ...), dimensions={2} | concatenate | bytes 1536000 | tf_op jit(solution)/shard_map/stack | solution.py:116
  71.5 11.9 %convolution_bitcast_fusion = f32[25,50,125]{2,1,0:T(8,128)S(1)} fusion(bf16[25,4,32,24,50]{4,3,2,1,0:T(8,128)(2,1)} %bitcast_dynamic-update-slice_fusion, bf16[4,32,24,125]{3,2,1,0:T(8,128)(2,1)S(1)} %stack.359), kind=kOutput, calls=%fused_computation.6 | convolution fusion | flops 960000000 | bytes 9073000 | tf_op jit(solution)/shard_map/oxysb,xysu->obu/dot_general | solution.py:170
  83.6 1.6 %collective-permute-done.2 = f32[640,125]{1,0:T(8,128)S(1)} collective-permute-done((f32[640,125]{1,0:T(8,128)S(1)}, f32[640,125]{1,0:T(8,128)S(1)}, u32[]{:S(2)}, u32[]{:S(2)}) %collective-permute-start.2) | collective-permute-done | bytes 320032 | tf_op jit(solution)/shard_map/ppermute | solution.py:69
  85.4 23.5 %all_to_all.20 = bf16[16,40,125]{2,1,0:T(8,128)(2,1)S(1)} all-to-all(bf16[16,40,125]{2,1,0:T(8,128)(2,1)S(1)} %bitcast.390), channel_id=1, replica_groups=mesh['pxa'=16,'pxc'=2,'py'=8] {'pxa'}, dimensions={0} | all-to-all | bytes 320000 | tf_op jit(solution)/shard_map/all_to_all | solution.py:71
  108.9 12.9 %all_to_all.21 = bf16[16,40,125]{2,1,0:T(8,128)(2,1)S(1)} all-to-all(bf16[16,40,125]{2,1,0:T(8,128)(2,1)S(1)} %broadcast_in_dim.526), channel_id=1, replica_groups=mesh['pxa'=16,'pxc'=2,'py'=8] {'pxa'}, dimensions={0} | all-to-all | bytes 320000 | tf_op jit(solution)/shard_map/all_to_all | solution.py:74
  121.8 3.4 %collective-permute-start.3 = (bf16[640,125]{1,0:T(8,128)(2,1)S(1)}, bf16[640,125]{1,0:T(8,128)(2,1)S(1)}, u32[]{:S(2)}, u32[]{:S(2)}) collective-permute-start(bf16[640,125]{1,0:T(8,128)(2,1)S(1)} %bitcast.389), channel_id=1, source_target_pairs={{0,8},{8,0},{1,9},{9,1},{2,10},{10,2},{3,11},{11,3},{4,12},{12,4},... | collective-permute-start | bytes 480008 | tf_op jit(solution)/shard_map/ppermute | solution.py:75
  125.1 1.0 collective-permute-done.3
  126.3 0.9 div.10
  (113 shorter events, 7.5 us)
Async XLA Ops:
  2.9 11.0 %all-to-all-start = ((f32[8,1,384]{2,1,0:T(1,128)}), f32[8,1,384]{2,1,0:T(1,128)S(1)}, u32[]{:S(2)}, u32[]{:S(2)}) async-start(f32[8,1,384]{2,1,0:T(1,128)} %reshape.934), calls=%async_computation | async-start | bytes 24576 | tf_op jit(solution)/shard_map/all_to_all | solution.py:139
  15.4 9.2 %collective-permute-start.1 = (f32[2,32,8,3]{2,1,3,0:T(8,128)S(1)}, f32[2,32,8,3]{2,1,3,0:T(8,128)S(1)}, u32[]{:S(2)}, u32[]{:S(2)}) collective-permute-start(f32[2,32,8,3]{2,1,3,0:T(8,128)S(1)} %bitcast.416), channel_id=1, source_target_pairs={{8,0},{16,8},{24,16},{32,24},{40,32},{48,40},{56,48},{64,56},{72,6... | collective-permute-start | bytes 18440 | tf_op jit(solution)/shard_map/ppermute | solution.py:18
  19.5 5.9 %collective-permute-start = (f32[2,32,8,3]{2,1,3,0:T(8,128)S(1)}, f32[2,32,8,3]{2,1,3,0:T(8,128)S(1)}, u32[]{:S(2)}, u32[]{:S(2)}) collective-permute-start(f32[2,32,8,3]{2,1,3,0:T(8,128)S(1)} %bitcast.417), channel_id=1, source_target_pairs={{0,8},{8,16},{16,24},{24,32},{32,40},{40,48},{48,56},{56,64},{64,7... | collective-permute-start | bytes 18440 | tf_op jit(solution)/shard_map/ppermute | solution.py:18
  30.4 2.2 %slice-start = ((s8[5734400]{0:T(1024)(128)(4,1)}), s8[4194304]{0:T(1024)(128)(4,1)S(1)}, s32[]{:S(2)}) async-start(s8[5734400]{0:T(1024)(128)(4,1)} %bitcast.419), calls=%async_computation.4 | async-start | bytes 8388608
  30.8 2.4 %slice-start.1 = ((s8[5734400]{0:T(1024)(128)(4,1)}), s8[1540096]{0:T(1024)(128)(4,1)S(1)}, s32[]{:S(2)}) async-start(s8[5734400]{0:T(1024)(128)(4,1)} %bitcast.419), calls=%async_computation.5 | async-start | bytes 3080192
  45.8 0.8 copy-start
  46.4 6.7 %copy-start.1 = (bf16[25,4,32,24,50]{4,3,2,1,0:T(8,128)(2,1)}, bf16[25,4,32,24,50]{4,3,2,1,0:T(8,128)(2,1)S(1)}, u32[]{:S(2)}) copy-start(bf16[25,4,32,24,50]{4,3,2,1,0:T(8,128)(2,1)S(1)} %fusion.6) | copy-start | bytes 23040004
  58.4 8.5 %all-to-all-start.1 = ((bf16[8,4,4,148]{3,2,1,0:T(4,128)(2,1)}), bf16[8,4,4,148]{3,2,1,0:T(4,128)(2,1)S(1)}, u32[]{:S(2)}, u32[]{:S(2)}) async-start(bf16[8,4,4,148]{3,2,1,0:T(4,128)(2,1)} %constant_dynamic-update-slice_fusion.25), calls=%async_computation.1 | async-start | bytes 131072 | tf_op jit(solution)/shard_map/all_to_all | solution.py:166
  83.5 1.7 %collective-permute-start.2 = (f32[640,125]{1,0:T(8,128)S(1)}, f32[640,125]{1,0:T(8,128)S(1)}, u32[]{:S(2)}, u32[]{:S(2)}) collective-permute-start(f32[640,125]{1,0:T(8,128)S(1)} %pad_dynamic-slice_fusion), channel_id=1, source_target_pairs={{0,8},{8,0},{1,9},{9,1},{2,10},{10,2},{3,11},{11,3},{4,12},{12,4},... | collective-permute-start | bytes 960008 | tf_op jit(solution)/shard_map/ppermute | solution.py:69
  121.8 4.4 %collective-permute-start.3 = (bf16[640,125]{1,0:T(8,128)(2,1)S(1)}, bf16[640,125]{1,0:T(8,128)(2,1)S(1)}, u32[]{:S(2)}, u32[]{:S(2)}) collective-permute-start(bf16[640,125]{1,0:T(8,128)(2,1)S(1)} %bitcast.389), channel_id=1, source_target_pairs={{0,8},{8,0},{1,9},{9,1},{2,10},{10,2},{3,11},{11,3},{4,12},{12,4},... | collective-permute-start | bytes 480008 | tf_op jit(solution)/shard_map/ppermute | solution.py:75

commit v5 on v4

--- a/solution.py
+++ b/solution.py
@@ -5,15 +5,15 @@
 
 BINS = 50
 SHIFTS = 24
-PX = ("pxa", "pxc")
+PX = ("pza", "pxh", "pxc")
 
 
 def px_index():
-    return lax.axis_index("pxa") * 2 + lax.axis_index("pxc")
+    return lax.axis_index("pza") * 4 + lax.axis_index("pxh") * 2 + lax.axis_index("pxc")
 
 
 def passed_along(block, axis, distance):
-    devices = range(lax.axis_size("pxa") * 2)
+    devices = range(lax.axis_size("pza") * 4)
     route = [(i - distance, i) for i in devices if i - distance in devices]
     return lax.ppermute(block, axis, route)
 
@@ -57,25 +57,32 @@
 
 
 def chip_sum(value):
-    count = lax.axis_size("pxa")
-    core = lax.axis_index("pxc")
     swap = [(0, 1), (1, 0)]
+    count = lax.axis_size("pza")
     rows = value.shape[0]
-    unit = -(-rows // (2 * count))
-    buf = jnp.pad(value, ((0, 2 * unit * count - rows),) + ((0, 0),) * (value.ndim - 1))
-    half = unit * count
-    keep = lax.dynamic_slice_in_dim(buf, core * half, half, 0)
-    send = lax.dynamic_slice_in_dim(buf, (1 - core) * half, half, 0)
-    part = keep + lax.ppermute(send, "pxc", swap)
-    pieces = part.reshape((count, unit) + value.shape[1:]).astype(jnp.bfloat16)
-    got = lax.all_to_all(pieces, "pxa", 0, 0).astype(jnp.float32)
+    unit = -(-rows // (4 * count))
+    buf = jnp.pad(value, ((0, 4 * unit * count - rows),) + ((0, 0),) * (value.ndim - 1))
+    sides = []
+    for axis in ("pxc", "pxh"):
+        side = lax.axis_index(axis)
+        sides.append(side)
+        half = buf.shape[0] // 2
+        keep = lax.dynamic_slice_in_dim(buf, side * half, half, 0)
+        send = lax.dynamic_slice_in_dim(buf, (1 - side) * half, half, 0)
+        if axis != "pxc":
+            send = send.astype(jnp.bfloat16)
+        buf = keep + lax.ppermute(send, axis, swap).astype(jnp.float32)
+    pieces = buf.reshape((count, unit) + value.shape[1:]).astype(jnp.bfloat16)
+    got = lax.all_to_all(pieces, "pza", 0, 0).astype(jnp.float32)
     mine = jnp.sum(got, axis=0).astype(jnp.bfloat16)
     spread = jnp.broadcast_to(mine[None], pieces.shape)
-    ours = lax.all_to_all(spread, "pxa", 0, 0).reshape((half,) + value.shape[1:])
-    theirs = lax.ppermute(ours, "pxc", swap)
-    low = jnp.where(core == 0, ours, theirs)
-    high = jnp.where(core == 0, theirs, ours)
-    return jnp.concatenate([low, high], axis=0)[:rows].astype(jnp.float32)
+    ours = lax.all_to_all(spread, "pza", 0, 0).reshape((count * unit,) + value.shape[1:])
+    for axis, side in zip(("pxh", "pxc"), reversed(sides)):
+        theirs = lax.ppermute(ours, axis, swap)
+        low = jnp.where(side == 0, ours, theirs)
+        high = jnp.where(side == 0, theirs, ours)
+        ours = jnp.concatenate([low, high], axis=0)
+    return ours[:rows].astype(jnp.float32)
 
 
 def bin_charges(charge, hit_bins, hit_ticks):
@@ -192,7 +199,8 @@
     out_specs = (P("px", "py", None), P(None, None, "py"))
     rows_of = mesh.shape["px"]
     split = jax.sharding.Mesh(
-        mesh.devices.reshape((rows_of // 2, 2) + mesh.devices.shape[1:]), ("pxa", "pxc", "py")
+        mesh.devices.reshape((rows_of // 4, 2, 2) + mesh.devices.shape[1:]),
+        ("pza", "pxh", "pxc", "py"),
     )
     rename = lambda spec: P(*[PX if part == "px" else part for part in spec])
     return jax.shard_map(

time: 128 us -> 133 us (1.039)
  blocking collectives: 36.3 us -> 27.8 us
  waiting for transfers between devices: 8.62 us -> 15.8 us
  starting transfers between devices: 21 us -> 27.6 us
    all_to_all x2, blocking collectives: 36.3 us -> 27.8 us  [the longest x1 18 us: chip_sum(): got = lax.all_to_all(pieces, 'pza', 0, 0).astype(jnp.float32)]
    ppermute x2 -> x4, waiting for transfers between devices: 2.64 us -> 9.81 us  [the longest x2 5.76 us: chip_sum(): theirs = lax.ppermute(ours, axis, swap)]
    ppermute x2 -> x4, starting transfers between devices: 3.45 us -> 10.1 us  [the longest x2 5.11 us: chip_sum(): theirs = lax.ppermute(ours, axis, swap)]
  transfers between devices with their start and end apart: 6 -> 8, of which waited for: 5 -> 7; matrix products, arithmetic and copies ran while one was open for 5% -> 4% of each run, Pallas kernels for 0% -> 0%
where the time goes in v5:
time: 133 us
  blocking collectives  27.8 us (21%)
  starting transfers between devices  27.6 us (21%)
  local copies, waits for them, and re-layouts  24 us (18%)
  other arithmetic  18.4 us (14%)
  matrix products  17.4 us (13%)
  waiting for transfers between devices  15.8 us (12%)
  between operations  1.51 us (1%)
    all_to_all x1, blocking collectives, chip_sum(): got = lax.all_to_all(pieces, 'pza', 0, 0).astype(jnp.float32)  18 us
    unnamed x44, local copies, waits for them, and re-layouts  13.5 us
    dot_general x1, matrix products, on_device(): jnp.einsum('oxysb,xysu->obu', stacked_band, windows(band_resid, share), p...  11.9 us
    unnamed x47, other arithmetic  10.9 us
    all_to_all x1, blocking collectives, chip_sum(): lax.all_to_all(spread, 'pza', 0, 0)  9.78 us
    ppermute x2, starting transfers between devices, passed_along(): return lax.ppermute(block, axis, route)  8.27 us
    all_to_all x1, starting transfers between devices, on_device(): band = jnp.transpose(lax.all_to_all(spread, 'py', 0, 0), (1, 0, 2, 3, 4))  5.94 us
    ppermute x2, waiting for transfers between devices, chip_sum(): theirs = lax.ppermute(ours, axis, swap)  5.76 us
  transfers between devices with their start and end apart: 8, of which 7 were waited for; matrix products, arithmetic and copies ran while one was open for 4% of the time, Pallas kernels for 0%

profile of v5, /device:TPU:1, one launch (start us, length us, event | category | flops | bytes accessed | tf_op | source)
XLA Modules:
  0.0 132.5 jit_solution(1243790608911474648)
XLA Ops:
  0.6 0.7 convert_bitcast_fusion
  1.3 0.7 pad_maximum_fusion.3
  2.1 0.8 reshape.934
  2.9 5.9 %all-to-all-start = ((f32[8,1,384]{2,1,0:T(1,128)}), f32[8,1,384]{2,1,0:T(1,128)S(1)}, u32[]{:S(2)}, u32[]{:S(2)}) async-start(f32[8,1,384]{2,1,0:T(1,128)} %reshape.934), calls=%async_computation | async-start | bytes 24576 | tf_op jit(solution)/shard_map/all_to_all | solution.py:146
  8.8 0.7 pad_dynamic-slice_fusion.2
  9.6 0.7 pad_dynamic-slice_fusion.3
  10.5 0.9 slice_compare_fusion
  11.4 2.5 %all-to-all-done = f32[8,1,384]{2,1,0:T(1,128)S(1)} async-done(((f32[8,1,384]{2,1,0:T(1,128)}), f32[8,1,384]{2,1,0:T(1,128)S(1)}, u32[]{:S(2)}, u32[]{:S(2)}) %all-to-all-start) | async-done | bytes 12320 | tf_op jit(solution)/shard_map/all_to_all | solution.py:146
  13.9 0.5 broadcast.908
  14.4 0.7 reduce.1
  15.4 4.0 %collective-permute-start.1 = (f32[2,32,8,3]{2,1,3,0:T(8,128)S(1)}, f32[2,32,8,3]{2,1,3,0:T(8,128)S(1)}, u32[]{:S(2)}, u32[]{:S(2)}) collective-permute-start(f32[2,32,8,3]{2,1,3,0:T(8,128)S(1)} %bitcast.416), channel_id=1, source_target_pairs={{8,0},{16,8},{24,16},{32,24},{40,32},{48,40},{56,48},{64,56},{72,6... | collective-permute-start | bytes 18440 | tf_op jit(solution)/shard_map/ppermute | solution.py:18
  19.5 4.3 %collective-permute-start = (f32[2,32,8,3]{2,1,3,0:T(8,128)S(1)}, f32[2,32,8,3]{2,1,3,0:T(8,128)S(1)}, u32[]{:S(2)}, u32[]{:S(2)}) collective-permute-start(f32[2,32,8,3]{2,1,3,0:T(8,128)S(1)} %bitcast.417), channel_id=1, source_target_pairs={{0,8},{8,16},{16,24},{24,32},{32,40},{40,48},{48,56},{56,64},{64,7... | collective-permute-start | bytes 18440 | tf_op jit(solution)/shard_map/ppermute | solution.py:18
  23.8 0.7 convert_element_type.111
  24.7 0.6 collective-permute-done
  25.8 2.9 %convolution_convert_fusion = bf16[8,32,24,50]{3,2,1,0:T(8,128)(2,1)S(1)} fusion(s32[8,32,8]{2,1,0:T(8,128)S(1)} %copy.148, bf16[8,32,8]{2,1,0:T(8,128)(2,1)S(1)} %copy.147, s32[8,32,8]{2,1,0:T(8,128)S(1)} %copy.146), kind=kOutput, calls=%fused_computation.4 | convolution fusion | flops 5115904 | bytes 634880 | tf_op jit(solution)/shard_map/xyks,xykb->xysb/dot_general | solution.py:92
  31.3 1.3 slice-done
  32.6 0.6 slice-done.1
  33.2 2.6 %fusion = f32[4,4,24,1000,1]{3,2,0,1,4:T(8,128)S(1)} fusion(f32[25,50,1000]{2,1,0:T(8,128)S(1)} %bitcast.420, bf16[25,4,4,24,50]{4,3,2,1,0:T(8,128)(2,1)S(1)} %constant_dynamic-update-slice_fusion), kind=kOutput, calls=%fused_computation | convolution fusion | flops 961249984 | bytes 7496000 | tf_op jit(solution)/shard_map/oxysb,obt->xyst/dot_general | solution.py:164
  36.0 0.3 fusion.48
  36.3 1.2 fusion.47
  39.1 0.3 bitcast_dynamic-update-slice_fusion.18
  39.4 0.3 fusion.13
  39.7 0.3 bitcast_dynamic-update-slice_fusion.17
  40.1 0.3 bitcast_dynamic-update-slice_fusion.16
  40.4 0.3 bitcast_dynamic-update-slice_fusion.15
  40.7 0.3 bitcast_dynamic-update-slice_fusion.14
  41.4 0.3 bitcast_dynamic-update-slice_fusion.13
  41.7 0.3 bitcast_dynamic-update-slice_fusion.12
  42.1 0.3 bitcast_dynamic-update-slice_fusion.11
  42.4 0.3 bitcast_dynamic-update-slice_fusion.10
  42.9 0.3 bitcast_dynamic-update-slice_fusion.9
  43.2 0.3 bitcast_dynamic-update-slice_fusion.8
  43.6 0.3 bitcast_dynamic-update-slice_fusion.7
  43.9 0.3 bitcast_dynamic-update-slice_fusion.6
  44.6 0.3 bitcast_dynamic-update-slice_fusion.5
  44.9 0.3 bitcast_dynamic-update-slice_fusion.4
  45.3 0.5 bitcast_dynamic-update-slice_fusion.3
  45.8 0.3 bitcast_dynamic-update-slice_fusion.2
  46.5 2.0 %multiply_convert_fusion = (bf16[4,4,1024]{2,1,0:T(4,128)(2,1)S(1)}, bf16[4,4,1024]{2,1,0:T(4,128)(2,1)}) fusion(bf16[4,4,1024]{2,1,0:T(4,128)(2,1)S(1)} %copy-done, f32[4,4]{1,0:T(4,128)S(1)} %convert_element_type.111, f32[4,4,1000]{2,1,0:T(4,128)S(1)} %bitcast.391, f32[4,4,1000]{2,1,0:T(4,128)S(1)} %bitcast.392, f32[4,4,1000]{2,1,0:T(4,128)S(1)} %bitcast.393, ...), kind=kLoop, calls=%fused_computation.168 | loop fusion | flops 458752 | bytes 1634368 | tf_op jit(solution)/shard_map/convert_element_type | solution.py:129
  48.5 4.6 %copy-done.1 = bf16[25,4,32,24,50]{4,3,2,1,0:T(8,128)(2,1)} copy-done((bf16[25,4,32,24,50]{4,3,2,1,0:T(8,128)(2,1)}, bf16[25,4,32,24,50]{4,3,2,1,0:T(8,128)(2,1)S(1)}, u32[]{:S(2)}) %copy-start.1) | copy-done | bytes 7680024
  53.1 0.6 constant_dynamic-update-slice_fusion.32
  53.7 0.7 constant_dynamic-update-slice_fusion.31
  54.4 0.7 constant_dynamic-update-slice_fusion.30
  55.1 0.7 constant_dynamic-update-slice_fusion.29
  55.7 0.7 constant_dynamic-update-slice_fusion.28
  56.4 0.7 constant_dynamic-update-slice_fusion.27
  57.1 0.7 constant_dynamic-update-slice_fusion.26
  57.8 0.7 constant_dynamic-update-slice_fusion.25
  58.4 3.4 %all-to-all-start.1 = ((bf16[8,4,4,148]{3,2,1,0:T(4,128)(2,1)}), bf16[8,4,4,148]{3,2,1,0:T(4,128)(2,1)S(1)}, u32[]{:S(2)}, u32[]{:S(2)}) async-start(bf16[8,4,4,148]{3,2,1,0:T(4,128)(2,1)} %constant_dynamic-update-slice_fusion.25), calls=%async_computation.1 | async-start | bytes 131072 | tf_op jit(solution)/shard_map/all_to_all | solution.py:173
  61.8 1.1 bitcast_dynamic-update-slice_fusion.1
  62.9 1.1 bitcast_dynamic-update-slice_fusion
  64.0 2.9 %all-to-all-done.1 = bf16[8,4,4,148]{3,2,1,0:T(4,128)(2,1)S(1)} async-done(((bf16[8,4,4,148]{3,2,1,0:T(4,128)(2,1)}), bf16[8,4,4,148]{3,2,1,0:T(4,128)(2,1)S(1)}, u32[]{:S(2)}, u32[]{:S(2)}) %all-to-all-start.1) | async-done | bytes 37920 | tf_op jit(solution)/shard_map/all_to_all | solution.py:173
  67.1 0.4 slice_bitcast_fusion.1
  68.9 2.6 %stack.359 = bf16[4,32,24,125]{3,2,1,0:T(8,128)(2,1)S(1)} concatenate(bf16[4,32,1,125]{3,2,1,0:T(2,128)(2,1)S(1)} %copy.197, bf16[4,32,1,125]{3,2,1,0:T(2,128)(2,1)S(1)} %copy.198, bf16[4,32,1,125]{3,2,1,0:T(2,128)(2,1)S(1)} %copy.199, bf16[4,32,1,125]{3,2,1,0:T(2,128)(2,1)S(1)} %copy.200, bf16[4,32,1,125]{3,2,1,0:T(2,128)(2,1)S(1)} %copy.201, ...), dimensions={2} | concatenate | bytes 1536000 | tf_op jit(solution)/shard_map/stack | solution.py:123
  71.5 11.9 %convolution_bitcast_fusion = f32[25,50,125]{2,1,0:T(8,128)S(1)} fusion(bf16[25,4,32,24,50]{4,3,2,1,0:T(8,128)(2,1)} %bitcast_dynamic-update-slice_fusion, bf16[4,32,24,125]{3,2,1,0:T(8,128)(2,1)S(1)} %stack.359), kind=kOutput, calls=%fused_computation.6 | convolution fusion | flops 960000000 | bytes 9073000 | tf_op jit(solution)/shard_map/oxysb,xysu->obu/dot_general | solution.py:177
  83.7 1.6 %collective-permute-done.2 = f32[640,125]{1,0:T(8,128)S(1)} collective-permute-done((f32[640,125]{1,0:T(8,128)S(1)}, f32[640,125]{1,0:T(8,128)S(1)}, u32[]{:S(2)}, u32[]{:S(2)}) %collective-permute-start.2) | collective-permute-done | bytes 320032 | tf_op jit(solution)/shard_map/ppermute | solution.py:74
  85.4 4.9 %collective-permute-start.3 = (bf16[320,125]{1,0:T(8,128)(2,1)S(1)}, bf16[320,125]{1,0:T(8,128)(2,1)S(1)}, u32[]{:S(2)}, u32[]{:S(2)}) collective-permute-start(bf16[320,125]{1,0:T(8,128)(2,1)S(1)} %dynamic-slice_convert_fusion), channel_id=1, source_target_pairs={{0,16},{16,0},{1,17},{17,1},{2,18},{18,2},{3,19},{19,3},{4,20},{20... | collective-permute-start | bytes 240008 | tf_op jit(solution)/shard_map/ppermute | solution.py:74
  90.3 2.4 %collective-permute-done.3 = bf16[320,125]{1,0:T(8,128)(2,1)S(1)} collective-permute-done((bf16[320,125]{1,0:T(8,128)(2,1)S(1)}, bf16[320,125]{1,0:T(8,128)(2,1)S(1)}, u32[]{:S(2)}, u32[]{:S(2)}) %collective-permute-start.3) | collective-permute-done | bytes 80032 | tf_op jit(solution)/shard_map/ppermute | solution.py:74
  92.7 18.0 %all_to_all.20 = bf16[8,40,125]{2,1,0:T(8,128)(2,1)S(1)} all-to-all(bf16[8,40,125]{2,1,0:T(8,128)(2,1)S(1)} %bitcast.390), channel_id=1, replica_groups=mesh['pza'=8,'pxh'=2,'pxc'=2,'py'=8] {'pza'}, dimensions={0} | all-to-all | bytes 160000 | tf_op jit(solution)/shard_map/all_to_all | solution.py:76
  110.8 9.8 %all_to_all.21 = bf16[8,40,125]{2,1,0:T(8,128)(2,1)S(1)} all-to-all(bf16[8,40,125]{2,1,0:T(8,128)(2,1)S(1)} %broadcast_in_dim.526), channel_id=1, replica_groups=mesh['pza'=8,'pxh'=2,'pxc'=2,'py'=8] {'pza'}, dimensions={0} | all-to-all | bytes 160000 | tf_op jit(solution)/shard_map/all_to_all | solution.py:79
  120.6 4.7 %collective-permute-done.4 = bf16[320,125]{1,0:T(8,128)(2,1)S(1)} collective-permute-done((bf16[320,125]{1,0:T(8,128)(2,1)S(1)}, bf16[320,125]{1,0:T(8,128)(2,1)S(1)}, u32[]{:S(2)}, u32[]{:S(2)}) %collective-permute-start.4) | collective-permute-done | bytes 80032 | tf_op jit(solution)/shard_map/ppermute | solution.py:81
  125.4 5.0 %collective-permute-start.5 = (bf16[640,125]{1,0:T(8,128)(2,1)S(1)}, bf16[640,125]{1,0:T(8,128)(2,1)S(1)}, u32[]{:S(2)}, u32[]{:S(2)}) collective-permute-start(bf16[640,125]{1,0:T(8,128)(2,1)S(1)} %pad_maximum_fusion.1), channel_id=1, source_target_pairs={{0,8},{8,0},{1,9},{9,1},{2,10},{10,2},{3,11},{11,3},{4,12},{12,4},... | collective-permute-start | bytes 480008 | tf_op jit(solution)/shard_map/ppermute | solution.py:81
  130.5 1.0 collective-permute-done.5
  131.6 0.9 div.10
  (121 shorter events, 8.5 us)
Async XLA Ops:
  2.9 11.0 %all-to-all-start = ((f32[8,1,384]{2,1,0:T(1,128)}), f32[8,1,384]{2,1,0:T(1,128)S(1)}, u32[]{:S(2)}, u32[]{:S(2)}) async-start(f32[8,1,384]{2,1,0:T(1,128)} %reshape.934), calls=%async_computation | async-start | bytes 24576 | tf_op jit(solution)/shard_map/all_to_all | solution.py:146
  15.4 9.2 %collective-permute-start.1 = (f32[2,32,8,3]{2,1,3,0:T(8,128)S(1)}, f32[2,32,8,3]{2,1,3,0:T(8,128)S(1)}, u32[]{:S(2)}, u32[]{:S(2)}) collective-permute-start(f32[2,32,8,3]{2,1,3,0:T(8,128)S(1)} %bitcast.416), channel_id=1, source_target_pairs={{8,0},{16,8},{24,16},{32,24},{40,32},{48,40},{56,48},{64,56},{72,6... | collective-permute-start | bytes 18440 | tf_op jit(solution)/shard_map/ppermute | solution.py:18
  19.5 5.9 %collective-permute-start = (f32[2,32,8,3]{2,1,3,0:T(8,128)S(1)}, f32[2,32,8,3]{2,1,3,0:T(8,128)S(1)}, u32[]{:S(2)}, u32[]{:S(2)}) collective-permute-start(f32[2,32,8,3]{2,1,3,0:T(8,128)S(1)} %bitcast.417), channel_id=1, source_target_pairs={{0,8},{8,16},{16,24},{24,32},{32,40},{40,48},{48,56},{56,64},{64,7... | collective-permute-start | bytes 18440 | tf_op jit(solution)/shard_map/ppermute | solution.py:18
  30.4 2.2 %slice-start = ((s8[5734400]{0:T(1024)(128)(4,1)}), s8[4194304]{0:T(1024)(128)(4,1)S(1)}, s32[]{:S(2)}) async-start(s8[5734400]{0:T(1024)(128)(4,1)} %bitcast.419), calls=%async_computation.4 | async-start | bytes 8388608
  30.8 2.4 %slice-start.1 = ((s8[5734400]{0:T(1024)(128)(4,1)}), s8[1540096]{0:T(1024)(128)(4,1)S(1)}, s32[]{:S(2)}) async-start(s8[5734400]{0:T(1024)(128)(4,1)} %bitcast.419), calls=%async_computation.5 | async-start | bytes 3080192
  45.8 0.8 copy-start
  46.4 6.7 %copy-start.1 = (bf16[25,4,32,24,50]{4,3,2,1,0:T(8,128)(2,1)}, bf16[25,4,32,24,50]{4,3,2,1,0:T(8,128)(2,1)S(1)}, u32[]{:S(2)}) copy-start(bf16[25,4,32,24,50]{4,3,2,1,0:T(8,128)(2,1)S(1)} %fusion.6) | copy-start | bytes 23040004
  58.4 8.5 %all-to-all-start.1 = ((bf16[8,4,4,148]{3,2,1,0:T(4,128)(2,1)}), bf16[8,4,4,148]{3,2,1,0:T(4,128)(2,1)S(1)}, u32[]{:S(2)}, u32[]{:S(2)}) async-start(bf16[8,4,4,148]{3,2,1,0:T(4,128)(2,1)} %constant_dynamic-update-slice_fusion.25), calls=%async_computation.1 | async-start | bytes 131072 | tf_op jit(solution)/shard_map/all_to_all | solution.py:173
  83.5 1.7 %collective-permute-start.2 = (f32[640,125]{1,0:T(8,128)S(1)}, f32[640,125]{1,0:T(8,128)S(1)}, u32[]{:S(2)}, u32[]{:S(2)}) collective-permute-start(f32[640,125]{1,0:T(8,128)S(1)} %pad_dynamic-slice_fusion), channel_id=1, source_target_pairs={{0,8},{8,0},{1,9},{9,1},{2,10},{10,2},{3,11},{11,3},{4,12},{12,4},... | collective-permute-start | bytes 960008 | tf_op jit(solution)/shard_map/ppermute | solution.py:74
  85.4 7.3 %collective-permute-start.3 = (bf16[320,125]{1,0:T(8,128)(2,1)S(1)}, bf16[320,125]{1,0:T(8,128)(2,1)S(1)}, u32[]{:S(2)}, u32[]{:S(2)}) collective-permute-start(bf16[320,125]{1,0:T(8,128)(2,1)S(1)} %dynamic-slice_convert_fusion), channel_id=1, source_target_pairs={{0,16},{16,0},{1,17},{17,1},{2,18},{18,2},{3,19},{19,3},{4,20},{20... | collective-permute-start | bytes 240008 | tf_op jit(solution)/shard_map/ppermute | solution.py:74
  120.6 4.8 %collective-permute-start.4 = (bf16[320,125]{1,0:T(8,128)(2,1)S(1)}, bf16[320,125]{1,0:T(8,128)(2,1)S(1)}, u32[]{:S(2)}, u32[]{:S(2)}) collective-permute-start(bf16[320,125]{1,0:T(8,128)(2,1)S(1)} %bitcast.389), channel_id=1, source_target_pairs={{0,16},{16,0},{1,17},{17,1},{2,18},{18,2},{3,19},{19,3},{4,20},{20... | collective-permute-start | bytes 240008 | tf_op jit(solution)/shard_map/ppermute | solution.py:81
  125.4 6.1 %collective-permute-start.5 = (bf16[640,125]{1,0:T(8,128)(2,1)S(1)}, bf16[640,125]{1,0:T(8,128)(2,1)S(1)}, u32[]{:S(2)}, u32[]{:S(2)}) collective-permute-start(bf16[640,125]{1,0:T(8,128)(2,1)S(1)} %pad_maximum_fusion.1), channel_id=1, source_target_pairs={{0,8},{8,0},{1,9},{9,1},{2,10},{10,2},{3,11},{11,3},{4,12},{12,4},... | collective-permute-start | bytes 480008 | tf_op jit(solution)/shard_map/ppermute | solution.py:81

commit v6 on v4

--- a/solution.py
+++ b/solution.py
@@ -85,6 +85,16 @@
     return jnp.einsum("xyks,xykb->xysb", weighted, bin_hot).astype(jnp.bfloat16)
 
 
+def bin_sum(charge, hit_bins, hit_ticks):
+    total = jnp.zeros(charge.shape[:2] + (SHIFTS, BINS), jnp.float32)
+    ticks = jnp.arange(SHIFTS, dtype=jnp.int32)[:, None]
+    bins = jnp.arange(BINS, dtype=jnp.int32)[None, :]
+    for k in range(charge.shape[2]):
+        hit = (hit_ticks[:, :, k, None, None] == ticks) & (hit_bins[:, :, k, None, None] == bins)
+        total = total + jnp.where(hit, charge[:, :, k, None, None], 0.0)
+    return total.astype(jnp.bfloat16)
+
+
 def gather_offsets(source, rows, cols, count_x, count_y):
     pieces = []
     for row_off in range(-2, 3):
@@ -141,7 +151,7 @@
     above = passed_along(band[tile_x - 2 :], PX, 1)
     below = passed_along(band[:2], PX, -1)
     wide = jnp.concatenate([above, band, below], axis=0)
-    binned = bin_charges(
+    binned = bin_sum(
         wide[..., 0], wide[..., 1].astype(jnp.int32), wide[..., 2].astype(jnp.int32)
     )
     source = jnp.pad(binned, ((0, 0), (2, 2), (0, 0), (0, 0)))
@@ -160,9 +170,10 @@
     prediction = shift_sum(partial_value, ticks)
     resid = residual_of(prediction, measured, active)
 
-    sent = jnp.stack(
-        [resid[:, :, k * share : k * share + span] for k in range(parts_y)], axis=0
-    )
+    room = jnp.pad(resid, ((0, 0), (0, 0), (0, (parts_y + 1) * share - resid.shape[2])))
+    lead = room[:, :, : parts_y * share].reshape(tile_x, tile_y, parts_y, share)
+    rest = room[:, :, share : (parts_y + 1) * share].reshape(tile_x, tile_y, parts_y, share)
+    sent = jnp.moveaxis(jnp.concatenate([lead, rest[..., : span - share]], axis=-1), 2, 0)
     got = lax.all_to_all(sent, "py", 0, 0)
     band_resid = jnp.transpose(got, (1, 0, 2, 3)).reshape(tile_x, width, span)
 

time: 128 us -> 133 us (1.039)
  other arithmetic: 18.4 us -> 30.7 us
  matrix products: 17.4 us -> 13.7 us
  local copies, waits for them, and re-layouts: 24 us -> 20.6 us
    convert_element_type x0 -> x2, other arithmetic: none -> 9.83 us  [the longest x1 9.8 us: bin_sum(): return total.astype(jnp.bfloat16)]
    unnamed x44 -> x37, local copies, waits for them, and re-layouts: 13.5 us -> 7.93 us
    slice x0 -> x4, local copies, waits for them, and re-layouts: none -> 3.52 us  [the longest x1 1.41 us: bin_sum(): hit_bins[:, :, k, None, None] == bins]
    dot_general x1 -> x0, matrix products: 2.89 us -> none  [bin_charges(): return jnp.einsum('xyks,xykb->xysb', weighted, bin_hot).astype(jnp.bfloat16)]
    eq x1 -> x16, other arithmetic: 0.01 us -> 1.61 us  [the longest x8 0.8 us: bin_sum(): hit_ticks[:, :, k, None, None] == ticks]
    unnamed x47 -> x48, other arithmetic: 10.9 us -> 11.5 us
  transfers between devices with their start and end apart: 6 -> 6, of which waited for: 5 -> 5; matrix products, arithmetic and copies ran while one was open for 5% -> 4% of each run, Pallas kernels for 0% -> 0%
where the time goes in v6:
time: 133 us
  blocking collectives  36.3 us (27%)
  other arithmetic  30.7 us (23%)
  starting transfers between devices  21 us (16%)
  local copies, waits for them, and re-layouts  20.6 us (15%)
  matrix products  13.7 us (10%)
  waiting for transfers between devices  8.72 us (7%)
  between operations  1.6 us (1%)
    all_to_all x1, blocking collectives, chip_sum(): got = lax.all_to_all(pieces, 'pxa', 0, 0).astype(jnp.float32)  23.5 us
    all_to_all x1, blocking collectives, chip_sum(): lax.all_to_all(spread, 'pxa', 0, 0).reshape((half,) + value.shape[1:])  12.9 us
    dot_general x1, matrix products, on_device(): jnp.einsum('oxysb,xysu->obu', stacked_band, windows(band_resid, share), p...  11.9 us
    unnamed x48, other arithmetic  11.5 us
    convert_element_type x1, other arithmetic, bin_sum(): return total.astype(jnp.bfloat16)  9.8 us
    ppermute x2, starting transfers between devices, passed_along(): return lax.ppermute(block, axis, route)  8.27 us
    unnamed x37, local copies, waits for them, and re-layouts  7.93 us
    all_to_all x1, starting transfers between devices, on_device(): band = jnp.transpose(lax.all_to_all(spread, 'py', 0, 0), (1, 0, 2, 3, 4))  5.94 us
  transfers between devices with their start and end apart: 6, of which 5 were waited for; matrix products, arithmetic and copies ran while one was open for 4% of the time, Pallas kernels for 0%

profile of v6, /device:TPU:1, one launch (start us, length us, event | category | flops | bytes accessed | tf_op | source)
XLA Modules:
  0.0 132.7 jit_solution(11785230841363894038)
XLA Ops:
  0.6 0.7 convert_bitcast_fusion
  1.3 0.7 broadcast_bitcast_fusion
  2.1 0.8 reshape.1092
  2.9 5.9 %all-to-all-start = ((f32[8,1,384]{2,1,0:T(1,128)}), f32[8,1,384]{2,1,0:T(1,128)S(1)}, u32[]{:S(2)}, u32[]{:S(2)}) async-start(f32[8,1,384]{2,1,0:T(1,128)} %reshape.1092), calls=%async_computation | async-start | bytes 24576 | tf_op jit(solution)/shard_map/all_to_all | solution.py:149
  8.8 0.7 pad_dynamic-slice_fusion.2
  9.6 0.7 pad_dynamic-slice_fusion.3
  10.5 0.9 slice_compare_fusion
  11.4 2.5 %all-to-all-done = f32[8,1,384]{2,1,0:T(1,128)S(1)} async-done(((f32[8,1,384]{2,1,0:T(1,128)}), f32[8,1,384]{2,1,0:T(1,128)S(1)}, u32[]{:S(2)}, u32[]{:S(2)}) %all-to-all-start) | async-done | bytes 12320 | tf_op jit(solution)/shard_map/all_to_all | solution.py:149
  13.9 0.5 broadcast.1056
  14.4 0.7 reduce.49
  15.1 0.3 reshape.1093
  15.4 4.0 %collective-permute-start.1 = (f32[2,32,8,3]{2,1,3,0:T(8,128)S(1)}, f32[2,32,8,3]{2,1,3,0:T(8,128)S(1)}, u32[]{:S(2)}, u32[]{:S(2)}) collective-permute-start(f32[2,32,8,3]{2,1,3,0:T(8,128)S(1)} %bitcast.410), channel_id=1, source_target_pairs={{8,0},{16,8},{24,16},{32,24},{40,32},{48,40},{56,48},{64,56},{72,6... | collective-permute-start | bytes 18440 | tf_op jit(solution)/shard_map/ppermute | solution.py:18
  19.5 4.3 %collective-permute-start = (f32[2,32,8,3]{2,1,3,0:T(8,128)S(1)}, f32[2,32,8,3]{2,1,3,0:T(8,128)S(1)}, u32[]{:S(2)}, u32[]{:S(2)}) collective-permute-start(f32[2,32,8,3]{2,1,3,0:T(8,128)S(1)} %bitcast.411), channel_id=1, source_target_pairs={{0,8},{8,16},{16,24},{24,32},{32,40},{40,48},{48,56},{56,64},{64,7... | collective-permute-start | bytes 18440 | tf_op jit(solution)/shard_map/ppermute | solution.py:18
  23.8 0.7 convert_element_type.111
  24.6 0.8 collective-permute-done
  25.4 0.6 slice_reduce_fusion.21
  26.0 1.4 %slice_reduce_fusion.22 = (s32[8,32]{1,0:T(8,128)S(1)}, s32[8,32]{1,0:T(8,128)S(1)}, s32[8,32]{1,0:T(8,128)S(1)}, s32[8,32]{1,0:T(8,128)S(1)}, s32[8,32]{1,0:T(8...) fusion(s32[8,32,8]{2,1,0:T(8,128)S(1)} %get-tuple-element.54), kind=kLoop, calls=%fused_computation.73 | loop fusion | bytes 16384 | tf_op jit(solution)/shard_map/slice | solution.py:93
  27.6 1.4 %slice_reduce_fusion.23 = (s32[8,32]{1,0:T(8,128)S(1)}, s32[8,32]{1,0:T(8,128)S(1)}, s32[8,32]{1,0:T(8,128)S(1)}, s32[8,32]{1,0:T(8,128)S(1)}, s32[8,32]{1,0:T(8...) fusion(s32[8,32,8]{2,1,0:T(8,128)S(1)} %get-tuple-element.52), kind=kLoop, calls=%fused_computation.76 | loop fusion | bytes 16384 | tf_op jit(solution)/shard_map/slice | solution.py:93
  30.6 9.8 %add_convert_fusion = bf16[8,32,24,50]{3,2,1,0:T(8,128)(2,1)S(1)} fusion(f32[8,32]{1,0:T(8,128)S(1)} %get-tuple-element.19, f32[8,32]{1,0:T(8,128)S(1)} %get-tuple-element.20, f32[8,32]{1,0:T(8,128)S(1)} %get-tuple-element.21, f32[8,32]{1,0:T(8,128)S(1)} %get-tuple-element.22, f32[8,32]{1,0:T(8,128)S(1)} %get-tuple-element.23, ...), kind=kLoop, calls=%fused_computation | loop fusion | flops 7372800 | bytes 774144 | tf_op jit(solution)/shard_map/convert_element_type | solution.py:95
  40.5 0.1 constant_dynamic-update-slice_fusion.23
  43.1 1.3 slice-done
  44.4 0.6 slice-done.1
  44.9 1.8 %fusion.3 = f32[4,4,24,1000]{3,2,1,0:T(8,128)S(1)} fusion(bf16[25,4,4,24,50]{4,3,0,2,1:T(8,128)(2,1)S(1)} %constant_dynamic-update-slice_fusion, f32[25,50,1000]{2,1,0:T(8,128)S(1)} %bitcast.414), kind=kOutput, calls=%fused_computation.4 | convolution fusion | flops 961249984 | bytes 7496000 | tf_op jit(solution)/shard_map/oxysb,obt->xyst/dot_general | solution.py:167
  46.8 0.3 fusion.45
  47.1 1.2 fusion.44
  49.0 0.2 bitcast_dynamic-update-slice_fusion.19
  49.2 0.3 bitcast_dynamic-update-slice_fusion.18
  49.6 0.3 fusion.14
  49.9 0.3 bitcast_dynamic-update-slice_fusion.17
  50.2 0.3 bitcast_dynamic-update-slice_fusion.16
  50.6 0.3 bitcast_dynamic-update-slice_fusion.15
  50.9 0.3 bitcast_dynamic-update-slice_fusion.14
  51.3 0.3 fusion.12
  51.5 0.3 bitcast_dynamic-update-slice_fusion.13
  51.9 0.3 bitcast_dynamic-update-slice_fusion.12
  52.2 0.3 bitcast_dynamic-update-slice_fusion.11
  52.6 0.3 bitcast_dynamic-update-slice_fusion.10
  52.9 0.1 fusion.10
  53.1 0.3 bitcast_dynamic-update-slice_fusion.9
  53.4 0.3 bitcast_dynamic-update-slice_fusion.8
  53.7 0.3 bitcast_dynamic-update-slice_fusion.7
  54.1 0.3 bitcast_dynamic-update-slice_fusion.6
  54.4 0.3 fusion.9
  54.7 0.3 bitcast_dynamic-update-slice_fusion.5
  55.1 0.3 bitcast_dynamic-update-slice_fusion.4
  55.4 0.3 bitcast_dynamic-update-slice_fusion.3
  55.8 0.3 bitcast_dynamic-update-slice_fusion.2
  56.1 0.3 fusion.7
  56.5 2.3 %multiply_convert_fusion = (bf16[4,4,1024]{2,1,0:T(4,128)(2,1)S(1)}, bf16[4,4,1024]{2,1,0:T(4,128)(2,1)}) fusion(bf16[4,4,1024]{2,1,0:T(4,128)(2,1)S(1)} %copy-done, f32[4,4]{1,0:T(4,128)S(1)} %convert_element_type.111, f32[4,4,1000]{2,1,0:T(4,128)S(1)} %bitcast.384, f32[4,4,1000]{2,1,0:T(4,128)S(1)} %bitcast.385, f32[4,4,1000]{2,1,0:T(4,128)S(1)} %bitcast.386, ...), kind=kLoop, calls=%fused_computation.194 | loop fusion | flops 458752 | bytes 1634368 | tf_op jit(solution)/shard_map/convert_element_type | solution.py:132
  58.9 4.3 %copy-done.1 = bf16[25,4,32,24,50]{4,3,2,1,0:T(8,128)(2,1)} copy-done((bf16[25,4,32,24,50]{4,3,2,1,0:T(8,128)(2,1)}, bf16[25,4,32,24,50]{4,3,2,1,0:T(8,128)(2,1)S(1)}, u32[]{:S(2)}) %copy-start.1) | copy-done | bytes 7680024
  63.4 0.7 maximum_bitcast_fusion
  64.1 3.4 %all-to-all-start.1 = ((bf16[8,4,4,148]{3,2,1,0:T(4,128)(2,1)}), bf16[8,4,4,148]{3,2,1,0:T(4,128)(2,1)S(1)}, u32[]{:S(2)}, u32[]{:S(2)}) async-start(bf16[8,4,4,148]{3,2,1,0:T(4,128)(2,1)} %maximum_bitcast_fusion), calls=%async_computation.1 | async-start | bytes 131072 | tf_op jit(solution)/shard_map/all_to_all | solution.py:177
  67.5 1.2 bitcast_dynamic-update-slice_fusion.1
  68.7 1.2 bitcast_dynamic-update-slice_fusion
  69.8 2.8 %all-to-all-done.1 = bf16[8,4,4,148]{3,2,1,0:T(4,128)(2,1)S(1)} async-done(((bf16[8,4,4,148]{3,2,1,0:T(4,128)(2,1)}), bf16[8,4,4,148]{3,2,1,0:T(4,128)(2,1)S(1)}, u32[]{:S(2)}, u32[]{:S(2)}) %all-to-all-start.1) | async-done | bytes 37920 | tf_op jit(solution)/shard_map/all_to_all | solution.py:177
  72.8 0.2 slice_bitcast_fusion.2
  74.5 2.6 %stack.323 = bf16[4,32,24,125]{3,2,1,0:T(8,128)(2,1)S(1)} concatenate(bf16[4,32,1,125]{3,2,1,0:T(2,128)(2,1)S(1)} %copy.2075, bf16[4,32,1,125]{3,2,1,0:T(2,128)(2,1)S(1)} %copy.2076, bf16[4,32,1,125]{3,2,1,0:T(2,128)(2,1)S(1)} %copy.2077, bf16[4,32,1,125]{3,2,1,0:T(2,128)(2,1)S(1)} %copy.2078, bf16[4,32,1,125]{3,2,1,0:T(2,128)(2,1)S(1)} %copy.2079, ...), dimensions={2} | concatenate | bytes 1536000 | tf_op jit(solution)/shard_map/stack | solution.py:126
  77.1 11.9 %convolution_bitcast_fusion = f32[25,50,125]{2,1,0:T(8,128)S(1)} fusion(bf16[25,4,32,24,50]{4,3,2,1,0:T(8,128)(2,1)} %bitcast_dynamic-update-slice_fusion, bf16[4,32,24,125]{3,2,1,0:T(8,128)(2,1)S(1)} %stack.323), kind=kOutput, calls=%fused_computation.5 | convolution fusion | flops 960000000 | bytes 9073000 | tf_op jit(solution)/shard_map/oxysb,xysu->obu/dot_general | solution.py:181
  89.2 1.6 %collective-permute-done.2 = f32[640,125]{1,0:T(8,128)S(1)} collective-permute-done((f32[640,125]{1,0:T(8,128)S(1)}, f32[640,125]{1,0:T(8,128)S(1)}, u32[]{:S(2)}, u32[]{:S(2)}) %collective-permute-start.2) | collective-permute-done | bytes 320032 | tf_op jit(solution)/shard_map/ppermute | solution.py:69
  90.9 23.5 %all_to_all.20 = bf16[16,40,125]{2,1,0:T(8,128)(2,1)S(1)} all-to-all(bf16[16,40,125]{2,1,0:T(8,128)(2,1)S(1)} %bitcast.383), channel_id=1, replica_groups=mesh['pxa'=16,'pxc'=2,'py'=8] {'pxa'}, dimensions={0} | all-to-all | bytes 320000 | tf_op jit(solution)/shard_map/all_to_all | solution.py:71
  114.5 12.9 %all_to_all.21 = bf16[16,40,125]{2,1,0:T(8,128)(2,1)S(1)} all-to-all(bf16[16,40,125]{2,1,0:T(8,128)(2,1)S(1)} %broadcast_in_dim.609), channel_id=1, replica_groups=mesh['pxa'=16,'pxc'=2,'py'=8] {'pxa'}, dimensions={0} | all-to-all | bytes 320000 | tf_op jit(solution)/shard_map/all_to_all | solution.py:74
  127.3 3.4 %collective-permute-start.3 = (bf16[640,125]{1,0:T(8,128)(2,1)S(1)}, bf16[640,125]{1,0:T(8,128)(2,1)S(1)}, u32[]{:S(2)}, u32[]{:S(2)}) collective-permute-start(bf16[640,125]{1,0:T(8,128)(2,1)S(1)} %bitcast.382), channel_id=1, source_target_pairs={{0,8},{8,0},{1,9},{9,1},{2,10},{10,2},{3,11},{11,3},{4,12},{12,4},... | collective-permute-start | bytes 480008 | tf_op jit(solution)/shard_map/ppermute | solution.py:75
  130.7 1.0 collective-permute-done.3
  131.8 0.9 div.10
  (121 shorter events, 7.4 us)
Async XLA Ops:
  2.9 11.0 %all-to-all-start = ((f32[8,1,384]{2,1,0:T(1,128)}), f32[8,1,384]{2,1,0:T(1,128)S(1)}, u32[]{:S(2)}, u32[]{:S(2)}) async-start(f32[8,1,384]{2,1,0:T(1,128)} %reshape.1092), calls=%async_computation | async-start | bytes 24576 | tf_op jit(solution)/shard_map/all_to_all | solution.py:149
  15.4 9.1 %collective-permute-start.1 = (f32[2,32,8,3]{2,1,3,0:T(8,128)S(1)}, f32[2,32,8,3]{2,1,3,0:T(8,128)S(1)}, u32[]{:S(2)}, u32[]{:S(2)}) collective-permute-start(f32[2,32,8,3]{2,1,3,0:T(8,128)S(1)} %bitcast.410), channel_id=1, source_target_pairs={{8,0},{16,8},{24,16},{32,24},{40,32},{48,40},{56,48},{64,56},{72,6... | collective-permute-start | bytes 18440 | tf_op jit(solution)/shard_map/ppermute | solution.py:18
  19.5 5.9 %collective-permute-start = (f32[2,32,8,3]{2,1,3,0:T(8,128)S(1)}, f32[2,32,8,3]{2,1,3,0:T(8,128)S(1)}, u32[]{:S(2)}, u32[]{:S(2)}) collective-permute-start(f32[2,32,8,3]{2,1,3,0:T(8,128)S(1)} %bitcast.411), channel_id=1, source_target_pairs={{0,8},{8,16},{16,24},{24,32},{32,40},{40,48},{48,56},{56,64},{64,7... | collective-permute-start | bytes 18440 | tf_op jit(solution)/shard_map/ppermute | solution.py:18
  42.2 2.2 %slice-start = ((s8[5734400]{0:T(1024)(128)(4,1)}), s8[4194304]{0:T(1024)(128)(4,1)S(1)}, s32[]{:S(2)}) async-start(s8[5734400]{0:T(1024)(128)(4,1)} %bitcast.413), calls=%async_computation.4 | async-start | bytes 8388608
  42.5 2.4 %slice-start.1 = ((s8[5734400]{0:T(1024)(128)(4,1)}), s8[1540096]{0:T(1024)(128)(4,1)S(1)}, s32[]{:S(2)}) async-start(s8[5734400]{0:T(1024)(128)(4,1)} %bitcast.413), calls=%async_computation.5 | async-start | bytes 3080192
  55.8 0.8 copy-start
  56.4 6.7 %copy-start.1 = (bf16[25,4,32,24,50]{4,3,2,1,0:T(8,128)(2,1)}, bf16[25,4,32,24,50]{4,3,2,1,0:T(8,128)(2,1)S(1)}, u32[]{:S(2)}) copy-start(bf16[25,4,32,24,50]{4,3,2,1,0:T(8,128)(2,1)S(1)} %fusion.7) | copy-start | bytes 23040004
  64.1 8.5 %all-to-all-start.1 = ((bf16[8,4,4,148]{3,2,1,0:T(4,128)(2,1)}), bf16[8,4,4,148]{3,2,1,0:T(4,128)(2,1)S(1)}, u32[]{:S(2)}, u32[]{:S(2)}) async-start(bf16[8,4,4,148]{3,2,1,0:T(4,128)(2,1)} %maximum_bitcast_fusion), calls=%async_computation.1 | async-start | bytes 131072 | tf_op jit(solution)/shard_map/all_to_all | solution.py:177
  89.1 1.7 %collective-permute-start.2 = (f32[640,125]{1,0:T(8,128)S(1)}, f32[640,125]{1,0:T(8,128)S(1)}, u32[]{:S(2)}, u32[]{:S(2)}) collective-permute-start(f32[640,125]{1,0:T(8,128)S(1)} %pad_dynamic-slice_fusion), channel_id=1, source_target_pairs={{0,8},{8,0},{1,9},{9,1},{2,10},{10,2},{3,11},{11,3},{4,12},{12,4},... | collective-permute-start | bytes 960008 | tf_op jit(solution)/shard_map/ppermute | solution.py:69
  127.3 4.4 %collective-permute-start.3 = (bf16[640,125]{1,0:T(8,128)(2,1)S(1)}, bf16[640,125]{1,0:T(8,128)(2,1)S(1)}, u32[]{:S(2)}, u32[]{:S(2)}) collective-permute-start(bf16[640,125]{1,0:T(8,128)(2,1)S(1)} %bitcast.382), channel_id=1, source_target_pairs={{0,8},{8,0},{1,9},{9,1},{2,10},{10,2},{3,11},{11,3},{4,12},{12,4},... | collective-permute-start | bytes 480008 | tf_op jit(solution)/shard_map/ppermute | solution.py:75

commit v7 on v4

--- a/solution.py
+++ b/solution.py
@@ -160,9 +160,10 @@
     prediction = shift_sum(partial_value, ticks)
     resid = residual_of(prediction, measured, active)
 
-    sent = jnp.stack(
-        [resid[:, :, k * share : k * share + span] for k in range(parts_y)], axis=0
-    )
+    room = jnp.pad(resid, ((0, 0), (0, 0), (0, (parts_y + 1) * share - resid.shape[2])))
+    lead = room[:, :, : parts_y * share].reshape(tile_x, tile_y, parts_y, share)
+    rest = room[:, :, share : (parts_y + 1) * share].reshape(tile_x, tile_y, parts_y, share)
+    sent = jnp.moveaxis(jnp.concatenate([lead, rest[..., : span - share]], axis=-1), 2, 0)
     got = lax.all_to_all(sent, "py", 0, 0)
     band_resid = jnp.transpose(got, (1, 0, 2, 3)).reshape(tile_x, width, span)
 

time: 128 us -> 123 us (0.961)
  local copies, waits for them, and re-layouts: 24 us -> 20.4 us
    unnamed x44 -> x39, local copies, waits for them, and re-layouts: 13.5 us -> 10.4 us
where the time goes in v7:
time: 123 us
  blocking collectives  36.3 us (30%)
  starting transfers between devices  21 us (17%)
  local copies, waits for them, and re-layouts  20.4 us (17%)
  other arithmetic  18.1 us (15%)
  matrix products  17.4 us (14%)
  waiting for transfers between devices  7.89 us (6%)
  between operations  1.51 us (1%)
    all_to_all x1, blocking collectives, chip_sum(): got = lax.all_to_all(pieces, 'pxa', 0, 0).astype(jnp.float32)  23.5 us
    all_to_all x1, blocking collectives, chip_sum(): lax.all_to_all(spread, 'pxa', 0, 0).reshape((half,) + value.shape[1:])  12.9 us
    dot_general x1, matrix products, on_device(): jnp.einsum('oxysb,xysu->obu', stacked_band, windows(band_resid, share), p...  11.9 us
    unnamed x47, other arithmetic  10.9 us
    unnamed x39, local copies, waits for them, and re-layouts  10.4 us
    ppermute x2, starting transfers between devices, passed_along(): return lax.ppermute(block, axis, route)  8.27 us
    all_to_all x1, starting transfers between devices, on_device(): band = jnp.transpose(lax.all_to_all(spread, 'py', 0, 0), (1, 0, 2, 3, 4))  5.94 us
    another operation x27, local copies, waits for them, and re-layouts, windows(): jnp.stack([resid[:, :, offset:offset + ticks] for offset in range(SHIFTS)...  4.18 us
  transfers between devices with their start and end apart: 6, of which 5 were waited for; matrix products, arithmetic and copies ran while one was open for 5% of the time, Pallas kernels for 0%

profile of v7, /device:TPU:1, one launch (start us, length us, event | category | flops | bytes accessed | tf_op | source)
XLA Modules:
  0.0 122.7 jit_solution(8778441360685993)
XLA Ops:
  0.6 0.7 convert_bitcast_fusion
  1.3 0.7 pad_maximum_fusion.2
  2.1 0.8 reshape.942
  2.9 5.9 %all-to-all-start = ((f32[8,1,384]{2,1,0:T(1,128)}), f32[8,1,384]{2,1,0:T(1,128)S(1)}, u32[]{:S(2)}, u32[]{:S(2)}) async-start(f32[8,1,384]{2,1,0:T(1,128)} %reshape.942), calls=%async_computation | async-start | bytes 24576 | tf_op jit(solution)/shard_map/all_to_all | solution.py:139
  8.8 0.7 pad_dynamic-slice_fusion.2
  9.6 0.7 pad_dynamic-slice_fusion.3
  10.5 0.9 slice_compare_fusion
  11.4 2.5 %all-to-all-done = f32[8,1,384]{2,1,0:T(1,128)S(1)} async-done(((f32[8,1,384]{2,1,0:T(1,128)}), f32[8,1,384]{2,1,0:T(1,128)S(1)}, u32[]{:S(2)}, u32[]{:S(2)}) %all-to-all-start) | async-done | bytes 12320 | tf_op jit(solution)/shard_map/all_to_all | solution.py:139
  13.9 0.5 broadcast.910
  14.4 0.7 reduce.1
  15.1 0.3 reshape.943
  15.4 4.0 %collective-permute-start.1 = (f32[2,32,8,3]{2,1,3,0:T(8,128)S(1)}, f32[2,32,8,3]{2,1,3,0:T(8,128)S(1)}, u32[]{:S(2)}, u32[]{:S(2)}) collective-permute-start(f32[2,32,8,3]{2,1,3,0:T(8,128)S(1)} %bitcast.390), channel_id=1, source_target_pairs={{8,0},{16,8},{24,16},{32,24},{40,32},{48,40},{56,48},{64,56},{72,6... | collective-permute-start | bytes 18440 | tf_op jit(solution)/shard_map/ppermute | solution.py:18
  19.5 4.3 %collective-permute-start = (f32[2,32,8,3]{2,1,3,0:T(8,128)S(1)}, f32[2,32,8,3]{2,1,3,0:T(8,128)S(1)}, u32[]{:S(2)}, u32[]{:S(2)}) collective-permute-start(f32[2,32,8,3]{2,1,3,0:T(8,128)S(1)} %bitcast.391), channel_id=1, source_target_pairs={{0,8},{8,16},{16,24},{24,32},{32,40},{40,48},{48,56},{56,64},{64,7... | collective-permute-start | bytes 18440 | tf_op jit(solution)/shard_map/ppermute | solution.py:18
  23.8 0.7 convert_element_type.107
  24.8 0.5 collective-permute-done
  25.8 2.9 %convolution_convert_fusion = bf16[8,32,24,50]{3,2,1,0:T(8,128)(2,1)S(1)} fusion(s32[8,32,8]{2,1,0:T(8,128)S(1)} %copy.1539, bf16[8,32,8]{2,1,0:T(8,128)(2,1)S(1)} %copy.1538, s32[8,32,8]{2,1,0:T(8,128)S(1)} %copy.1537), kind=kOutput, calls=%fused_computation.3 | convolution fusion | flops 5115904 | bytes 634880 | tf_op jit(solution)/shard_map/xyks,xykb->xysb/dot_general | solution.py:85
  29.2 0.1 constant_dynamic-update-slice_fusion.19
  29.5 0.1 constant_dynamic-update-slice_fusion.16
  31.3 1.3 %slice-done = s8[4194304]{0:T(1024)(128)(4,1)S(1)} async-done(((s8[5734400]{0:T(1024)(128)(4,1)}), s8[4194304]{0:T(1024)(128)(4,1)S(1)}, s32[]{:S(2)}) %slice-start) | async-done | bytes 4194328
  32.6 0.6 slice-done.1
  33.2 2.6 %fusion = f32[4,4,24,1000,1]{3,2,1,0,4:T(8,128)S(1)} fusion(bf16[25,4,4,24,50]{4,3,2,1,0:T(8,128)(2,1)S(1)} %constant_dynamic-update-slice_fusion, f32[25,50,1000]{2,1,0:T(8,128)S(1)} %bitcast.394), kind=kOutput, calls=%fused_computation | convolution fusion | flops 961249984 | bytes 7496000 | tf_op jit(solution)/shard_map/oxysb,obt->xyst/dot_general | solution.py:157
  35.8 0.2 copy.1674
  36.0 0.3 fusion.48
  36.3 1.2 fusion.47
  38.8 0.2 bitcast_dynamic-update-slice_fusion.19
  39.1 0.3 bitcast_dynamic-update-slice_fusion.18
  39.4 0.3 fusion.12
  39.7 0.3 bitcast_dynamic-update-slice_fusion.17
  40.0 0.3 bitcast_dynamic-update-slice_fusion.16
  40.4 0.3 bitcast_dynamic-update-slice_fusion.15
  40.7 0.3 bitcast_dynamic-update-slice_fusion.14
  41.1 0.3 fusion.10
  41.4 0.3 bitcast_dynamic-update-slice_fusion.13
  41.7 0.3 bitcast_dynamic-update-slice_fusion.12
  42.1 0.3 bitcast_dynamic-update-slice_fusion.11
  42.4 0.3 bitcast_dynamic-update-slice_fusion.10
  42.8 0.1 fusion.8
  42.9 0.3 bitcast_dynamic-update-slice_fusion.9
  43.2 0.3 bitcast_dynamic-update-slice_fusion.8
  43.6 0.3 bitcast_dynamic-update-slice_fusion.7
  43.9 0.3 bitcast_dynamic-update-slice_fusion.6
  44.3 0.3 fusion.7
  44.6 0.3 bitcast_dynamic-update-slice_fusion.5
  44.9 0.3 bitcast_dynamic-update-slice_fusion.4
  45.3 0.5 bitcast_dynamic-update-slice_fusion.3
  45.8 0.3 bitcast_dynamic-update-slice_fusion.2
  46.1 0.3 fusion.5
  46.5 1.0 multiply_convert_fusion
  47.7 5.4 %copy-done.1 = bf16[25,4,32,24,50]{4,3,2,1,0:T(8,128)(2,1)} copy-done((bf16[25,4,32,24,50]{4,3,2,1,0:T(8,128)(2,1)}, bf16[25,4,32,24,50]{4,3,2,1,0:T(8,128)(2,1)S(1)}, u32[]{:S(2)}) %copy-start.1) | copy-done | bytes 7680024
  53.4 0.7 maximum_bitcast_fusion
  54.1 3.4 %all-to-all-start.1 = ((bf16[8,4,4,148]{3,2,1,0:T(4,128)(2,1)}), bf16[8,4,4,148]{3,2,1,0:T(4,128)(2,1)S(1)}, u32[]{:S(2)}, u32[]{:S(2)}) async-start(bf16[8,4,4,148]{3,2,1,0:T(4,128)(2,1)} %maximum_bitcast_fusion), calls=%async_computation.1 | async-start | bytes 131072 | tf_op jit(solution)/shard_map/all_to_all | solution.py:167
  57.5 1.1 bitcast_dynamic-update-slice_fusion.1
  58.6 1.1 bitcast_dynamic-update-slice_fusion
  59.7 2.9 %all-to-all-done.1 = bf16[8,4,4,148]{3,2,1,0:T(4,128)(2,1)S(1)} async-done(((bf16[8,4,4,148]{3,2,1,0:T(4,128)(2,1)}), bf16[8,4,4,148]{3,2,1,0:T(4,128)(2,1)S(1)}, u32[]{:S(2)}, u32[]{:S(2)}) %all-to-all-start.1) | async-done | bytes 37920 | tf_op jit(solution)/shard_map/all_to_all | solution.py:167
  62.8 0.2 slice_bitcast_fusion.1
  64.5 2.6 %stack.323 = bf16[4,32,24,125]{3,2,1,0:T(8,128)(2,1)S(1)} concatenate(bf16[4,32,1,125]{3,2,1,0:T(2,128)(2,1)S(1)} %copy.1569, bf16[4,32,1,125]{3,2,1,0:T(2,128)(2,1)S(1)} %copy.1570, bf16[4,32,1,125]{3,2,1,0:T(2,128)(2,1)S(1)} %copy.1571, bf16[4,32,1,125]{3,2,1,0:T(2,128)(2,1)S(1)} %copy.1572, bf16[4,32,1,125]{3,2,1,0:T(2,128)(2,1)S(1)} %copy.1573, ...), dimensions={2} | concatenate | bytes 1536000 | tf_op jit(solution)/shard_map/stack | solution.py:116
  67.0 11.9 %convolution_bitcast_fusion = f32[25,50,125]{2,1,0:T(8,128)S(1)} fusion(bf16[25,4,32,24,50]{4,3,2,1,0:T(8,128)(2,1)} %bitcast_dynamic-update-slice_fusion, bf16[4,32,24,125]{3,2,1,0:T(8,128)(2,1)S(1)} %stack.323), kind=kOutput, calls=%fused_computation.5 | convolution fusion | flops 960000000 | bytes 9073000 | tf_op jit(solution)/shard_map/oxysb,xysu->obu/dot_general | solution.py:171
  79.2 1.6 %collective-permute-done.2 = f32[640,125]{1,0:T(8,128)S(1)} collective-permute-done((f32[640,125]{1,0:T(8,128)S(1)}, f32[640,125]{1,0:T(8,128)S(1)}, u32[]{:S(2)}, u32[]{:S(2)}) %collective-permute-start.2) | collective-permute-done | bytes 320032 | tf_op jit(solution)/shard_map/ppermute | solution.py:69
  80.9 23.5 %all_to_all.20 = bf16[16,40,125]{2,1,0:T(8,128)(2,1)S(1)} all-to-all(bf16[16,40,125]{2,1,0:T(8,128)(2,1)S(1)} %bitcast.363), channel_id=1, replica_groups=mesh['pxa'=16,'pxc'=2,'py'=8] {'pxa'}, dimensions={0} | all-to-all | bytes 320000 | tf_op jit(solution)/shard_map/all_to_all | solution.py:71
  104.4 12.9 %all_to_all.21 = bf16[16,40,125]{2,1,0:T(8,128)(2,1)S(1)} all-to-all(bf16[16,40,125]{2,1,0:T(8,128)(2,1)S(1)} %broadcast_in_dim.526), channel_id=1, replica_groups=mesh['pxa'=16,'pxc'=2,'py'=8] {'pxa'}, dimensions={0} | all-to-all | bytes 320000 | tf_op jit(solution)/shard_map/all_to_all | solution.py:74
  117.3 3.4 %collective-permute-start.3 = (bf16[640,125]{1,0:T(8,128)(2,1)S(1)}, bf16[640,125]{1,0:T(8,128)(2,1)S(1)}, u32[]{:S(2)}, u32[]{:S(2)}) collective-permute-start(bf16[640,125]{1,0:T(8,128)(2,1)S(1)} %bitcast.362), channel_id=1, source_target_pairs={{0,8},{8,0},{1,9},{9,1},{2,10},{10,2},{3,11},{11,3},{4,12},{12,4},... | collective-permute-start | bytes 480008 | tf_op jit(solution)/shard_map/ppermute | solution.py:75
  120.7 0.6 copy.1594
  121.3 0.4 collective-permute-done.3
  121.8 0.9 div.10
  (114 shorter events, 6.9 us)
Async XLA Ops:
  2.9 11.0 %all-to-all-start = ((f32[8,1,384]{2,1,0:T(1,128)}), f32[8,1,384]{2,1,0:T(1,128)S(1)}, u32[]{:S(2)}, u32[]{:S(2)}) async-start(f32[8,1,384]{2,1,0:T(1,128)} %reshape.942), calls=%async_computation | async-start | bytes 24576 | tf_op jit(solution)/shard_map/all_to_all | solution.py:139
  15.4 9.3 %collective-permute-start.1 = (f32[2,32,8,3]{2,1,3,0:T(8,128)S(1)}, f32[2,32,8,3]{2,1,3,0:T(8,128)S(1)}, u32[]{:S(2)}, u32[]{:S(2)}) collective-permute-start(f32[2,32,8,3]{2,1,3,0:T(8,128)S(1)} %bitcast.390), channel_id=1, source_target_pairs={{8,0},{16,8},{24,16},{32,24},{40,32},{48,40},{56,48},{64,56},{72,6... | collective-permute-start | bytes 18440 | tf_op jit(solution)/shard_map/ppermute | solution.py:18
  19.5 5.9 %collective-permute-start = (f32[2,32,8,3]{2,1,3,0:T(8,128)S(1)}, f32[2,32,8,3]{2,1,3,0:T(8,128)S(1)}, u32[]{:S(2)}, u32[]{:S(2)}) collective-permute-start(f32[2,32,8,3]{2,1,3,0:T(8,128)S(1)} %bitcast.391), channel_id=1, source_target_pairs={{0,8},{8,16},{16,24},{24,32},{32,40},{40,48},{48,56},{56,64},{64,7... | collective-permute-start | bytes 18440 | tf_op jit(solution)/shard_map/ppermute | solution.py:18
  30.4 2.2 %slice-start = ((s8[5734400]{0:T(1024)(128)(4,1)}), s8[4194304]{0:T(1024)(128)(4,1)S(1)}, s32[]{:S(2)}) async-start(s8[5734400]{0:T(1024)(128)(4,1)} %bitcast.393), calls=%async_computation.4 | async-start | bytes 8388608
  30.8 2.4 %slice-start.1 = ((s8[5734400]{0:T(1024)(128)(4,1)}), s8[1540096]{0:T(1024)(128)(4,1)S(1)}, s32[]{:S(2)}) async-start(s8[5734400]{0:T(1024)(128)(4,1)} %bitcast.393), calls=%async_computation.5 | async-start | bytes 3080192
  45.8 0.8 copy-start
  46.4 6.7 %copy-start.1 = (bf16[25,4,32,24,50]{4,3,2,1,0:T(8,128)(2,1)}, bf16[25,4,32,24,50]{4,3,2,1,0:T(8,128)(2,1)S(1)}, u32[]{:S(2)}) copy-start(bf16[25,4,32,24,50]{4,3,2,1,0:T(8,128)(2,1)S(1)} %fusion.5) | copy-start | bytes 23040004
  54.1 8.5 %all-to-all-start.1 = ((bf16[8,4,4,148]{3,2,1,0:T(4,128)(2,1)}), bf16[8,4,4,148]{3,2,1,0:T(4,128)(2,1)S(1)}, u32[]{:S(2)}, u32[]{:S(2)}) async-start(bf16[8,4,4,148]{3,2,1,0:T(4,128)(2,1)} %maximum_bitcast_fusion), calls=%async_computation.1 | async-start | bytes 131072 | tf_op jit(solution)/shard_map/all_to_all | solution.py:167
  79.1 1.7 %collective-permute-start.2 = (f32[640,125]{1,0:T(8,128)S(1)}, f32[640,125]{1,0:T(8,128)S(1)}, u32[]{:S(2)}, u32[]{:S(2)}) collective-permute-start(f32[640,125]{1,0:T(8,128)S(1)} %pad_dynamic-slice_fusion), channel_id=1, source_target_pairs={{0,8},{8,0},{1,9},{9,1},{2,10},{10,2},{3,11},{11,3},{4,12},{12,4},... | collective-permute-start | bytes 960008 | tf_op jit(solution)/shard_map/ppermute | solution.py:69
  117.3 4.4 %collective-permute-start.3 = (bf16[640,125]{1,0:T(8,128)(2,1)S(1)}, bf16[640,125]{1,0:T(8,128)(2,1)S(1)}, u32[]{:S(2)}, u32[]{:S(2)}) collective-permute-start(bf16[640,125]{1,0:T(8,128)(2,1)S(1)} %bitcast.362), channel_id=1, source_target_pairs={{0,8},{8,0},{1,9},{9,1},{2,10},{10,2},{3,11},{11,3},{4,12},{12,4},... | collective-permute-start | bytes 480008 | tf_op jit(solution)/shard_map/ppermute | solution.py:75

commit v8 on v7

--- a/solution.py
+++ b/solution.py
@@ -168,14 +168,15 @@
     band_resid = jnp.transpose(got, (1, 0, 2, 3)).reshape(tile_x, width, span)
 
     stacked_band = gather_offsets(source, rows_wide, cols_all, tile_x, width)
-    gradient = jnp.einsum(
-        "oxysb,xysu->obu",
-        stacked_band,
-        windows(band_resid, share),
-        preferred_element_type=jnp.float32,
-    )
-    flat = gradient.reshape(-1, share)
-    summed = chip_sum(flat).reshape(gradient.shape)
+    shifted = windows(band_resid, share)
+    group = (stacked_band.shape[0] + 1) // 2
+    sums = []
+    for part in (stacked_band[:group], stacked_band[group:]):
+        gradient = jnp.einsum(
+            "oxysb,xysu->obu", part, shifted, preferred_element_type=jnp.float32
+        )
+        sums.append(chip_sum(gradient.reshape(-1, share)).reshape(gradient.shape))
+    summed = jnp.concatenate(sums, axis=0)
     return (prediction.astype(jnp.bfloat16), summed / 16)
 
 

time: 123 us -> 152 us (1.24)
  blocking collectives: 36.3 us -> 0 us
  waiting for transfers between devices: 7.89 us -> 40.1 us
  starting transfers between devices: 21 us -> 51.2 us
    all_to_all x2 -> x0, blocking collectives: 36.3 us -> none  [the longest x1 23.5 us: chip_sum(): got = lax.all_to_all(pieces, 'pxa', 0, 0).astype(jnp.float32)]
    all_to_all x0 -> x4, waiting for transfers between devices: none -> 33.4 us  [the longest x2 18.7 us: chip_sum(): got = lax.all_to_all(pieces, 'pxa', 0, 0).astype(jnp.float32)]
    all_to_all x0 -> x4, starting transfers between devices: none -> 23.4 us  [the longest x2 16.4 us: chip_sum(): got = lax.all_to_all(pieces, 'pxa', 0, 0).astype(jnp.float32)]
    ppermute x1 -> x2, starting transfers between devices: 3.36 us -> 9.51 us  [chip_sum(): theirs = lax.ppermute(ours, 'pxc', swap)]
    unnamed x39 -> x40, local copies, waits for them, and re-layouts: 10.4 us -> 8.53 us
    ppermute x1 -> x2, waiting for transfers between devices: 1.61 us -> 0.01 us  [chip_sum(): part = keep + lax.ppermute(send, 'pxc', swap)]
    dot_general x1 -> x2, matrix products: 11.9 us -> 13 us  [on_device(): jnp.einsum('oxysb,xysu->obu', part, shifted, preferred_element_type=jnp.f...]
    unnamed x47 -> x46, other arithmetic: 10.9 us -> 10.6 us
  transfers between devices with their start and end apart: 6 -> 12, of which waited for: 5 -> 8; matrix products, arithmetic and copies ran while one was open for 5% -> 10% of each run, Pallas kernels for 0% -> 0%
where the time goes in v8:
time: 152 us; the launch traced here: 151 us
  starting transfers between devices  51.2 us (34%)
  waiting for transfers between devices  40.1 us (26%)
  local copies, waits for them, and re-layouts  20.5 us (13%)
  other arithmetic  19.1 us (13%)
  matrix products  18.5 us (12%)
  between operations  1.6 us (1%)
    all_to_all x2, waiting for transfers between devices, chip_sum(): got = lax.all_to_all(pieces, 'pxa', 0, 0).astype(jnp.float32)  18.7 us
    all_to_all x2, starting transfers between devices, chip_sum(): got = lax.all_to_all(pieces, 'pxa', 0, 0).astype(jnp.float32)  16.4 us
    all_to_all x2, waiting for transfers between devices, chip_sum(): lax.all_to_all(spread, 'pxa', 0, 0).reshape((half,) + value.shape[1:])  14.7 us
    dot_general x2, matrix products, on_device(): jnp.einsum('oxysb,xysu->obu', part, shifted, preferred_element_type=jnp.f...  13 us
    unnamed x46, other arithmetic  10.6 us
    ppermute x2, starting transfers between devices, chip_sum(): theirs = lax.ppermute(ours, 'pxc', swap)  9.51 us
    unnamed x40, local copies, waits for them, and re-layouts  8.53 us
    ppermute x2, starting transfers between devices, passed_along(): return lax.ppermute(block, axis, route)  8.27 us
  transfers between devices with their start and end apart: 12, of which 8 were waited for; matrix products, arithmetic and copies ran while one was open for 10% of the time, Pallas kernels for 0%

profile of v8, /device:TPU:1, one launch (start us, length us, event | category | flops | bytes accessed | tf_op | source)
XLA Modules:
  0.0 150.9 jit_solution(12684615166179178401)
XLA Ops:
  0.6 0.7 convert_bitcast_fusion
  1.3 0.7 pad_maximum_fusion.3
  2.1 0.8 reshape.961
  2.9 5.9 %all-to-all-start = ((f32[8,1,384]{2,1,0:T(1,128)}), f32[8,1,384]{2,1,0:T(1,128)S(1)}, u32[]{:S(2)}, u32[]{:S(2)}) async-start(f32[8,1,384]{2,1,0:T(1,128)} %reshape.961), calls=%async_computation | async-start | bytes 24576 | tf_op jit(solution)/shard_map/all_to_all | solution.py:139
  8.8 0.7 pad_dynamic-slice_fusion.4
  9.6 0.7 pad_dynamic-slice_fusion.5
  10.5 0.9 slice_compare_fusion.2
  11.4 2.5 %all-to-all-done = f32[8,1,384]{2,1,0:T(1,128)S(1)} async-done(((f32[8,1,384]{2,1,0:T(1,128)}), f32[8,1,384]{2,1,0:T(1,128)S(1)}, u32[]{:S(2)}, u32[]{:S(2)}) %all-to-all-start) | async-done | bytes 12320 | tf_op jit(solution)/shard_map/all_to_all | solution.py:139
  13.9 0.5 broadcast.911
  14.4 0.7 reduce.2
  15.4 4.0 %collective-permute-start.1 = (f32[2,32,8,3]{2,1,3,0:T(8,128)S(1)}, f32[2,32,8,3]{2,1,3,0:T(8,128)S(1)}, u32[]{:S(2)}, u32[]{:S(2)}) collective-permute-start(f32[2,32,8,3]{2,1,3,0:T(8,128)S(1)} %bitcast.394), channel_id=1, source_target_pairs={{8,0},{16,8},{24,16},{32,24},{40,32},{48,40},{56,48},{64,56},{72,6... | collective-permute-start | bytes 18440 | tf_op jit(solution)/shard_map/ppermute | solution.py:18
  19.5 4.3 %collective-permute-start = (f32[2,32,8,3]{2,1,3,0:T(8,128)S(1)}, f32[2,32,8,3]{2,1,3,0:T(8,128)S(1)}, u32[]{:S(2)}, u32[]{:S(2)}) collective-permute-start(f32[2,32,8,3]{2,1,3,0:T(8,128)S(1)} %bitcast.395), channel_id=1, source_target_pairs={{0,8},{8,16},{16,24},{24,32},{32,40},{40,48},{48,56},{56,64},{64,7... | collective-permute-start | bytes 18440 | tf_op jit(solution)/shard_map/ppermute | solution.py:18
  23.8 0.7 convert_element_type.116
  24.8 0.5 collective-permute-done
  25.8 2.9 %convolution_convert_fusion = bf16[8,32,24,50]{3,2,1,0:T(8,128)(2,1)S(1)} fusion(s32[8,32,8]{2,1,0:T(8,128)S(1)} %copy.1554, bf16[8,32,8]{2,1,0:T(8,128)(2,1)S(1)} %copy.1553, s32[8,32,8]{2,1,0:T(8,128)S(1)} %copy.1552), kind=kOutput, calls=%fused_computation.3 | convolution fusion | flops 5115904 | bytes 634880 | tf_op jit(solution)/shard_map/xyks,xykb->xysb/dot_general | solution.py:85
  31.3 1.3 slice-done
  32.6 0.6 slice-done.1
  33.2 2.6 %fusion = f32[4,4,24,1000,1]{3,2,1,0,4:T(8,128)S(1)} fusion(bf16[25,4,4,24,50]{4,3,2,1,0:T(8,128)(2,1)S(1)} %constant_dynamic-update-slice_fusion, f32[25,50,1000]{2,1,0:T(8,128)S(1)} %bitcast.398), kind=kOutput, calls=%fused_computation | convolution fusion | flops 961249984 | bytes 7496000 | tf_op jit(solution)/shard_map/oxysb,obt->xyst/dot_general | solution.py:157
  36.3 1.2 fusion.50
  39.1 0.3 bitcast_dynamic-update-slice_fusion.18
  39.7 0.3 bitcast_dynamic-update-slice_fusion.17
  40.1 0.3 bitcast_dynamic-update-slice_fusion.16
  40.4 0.3 bitcast_dynamic-update-slice_fusion.15
  40.7 0.3 bitcast_dynamic-update-slice_fusion.14
  41.4 0.3 bitcast_dynamic-update-slice_fusion.13
  41.7 0.3 bitcast_dynamic-update-slice_fusion.12
  42.4 0.3 bitcast_dynamic-update-slice_fusion.10
  42.8 0.3 fusion.8
  43.1 0.3 bitcast_dynamic-update-slice_fusion.8
  43.5 0.3 bitcast_dynamic-update-slice_fusion.7
  43.8 0.3 bitcast_dynamic-update-slice_fusion.6
  44.5 0.3 bitcast_dynamic-update-slice_fusion.5
  44.8 0.3 bitcast_dynamic-update-slice_fusion.4
  45.2 0.5 bitcast_dynamic-update-slice_fusion.3
  45.7 1.3 copy-done.1
  47.0 0.3 bitcast_dynamic-update-slice_fusion.2
  47.8 1.0 multiply_convert_fusion
  48.9 2.3 %copy-done = bf16[12,4,32,24,50]{4,3,2,1,0:T(8,128)(2,1)} copy-done((bf16[12,4,32,24,50]{4,3,2,1,0:T(8,128)(2,1)}, bf16[12,4,32,24,50]{4,3,2,1,0:T(8,128)(2,1)S(1)}, u32[]{:S(2)}) %copy-start) | copy-done | bytes 3686424
  51.5 0.7 maximum_bitcast_fusion
  52.3 3.4 %all-to-all-start.1 = ((bf16[8,4,4,148]{3,2,1,0:T(4,128)(2,1)}), bf16[8,4,4,148]{3,2,1,0:T(4,128)(2,1)S(1)}, u32[]{:S(2)}, u32[]{:S(2)}) async-start(bf16[8,4,4,148]{3,2,1,0:T(4,128)(2,1)} %maximum_bitcast_fusion), calls=%async_computation.1 | async-start | bytes 131072 | tf_op jit(solution)/shard_map/all_to_all | solution.py:167
  55.6 1.1 bitcast_dynamic-update-slice_fusion.1
  56.8 1.1 bitcast_dynamic-update-slice_fusion
  57.9 2.8 %all-to-all-done.1 = bf16[8,4,4,148]{3,2,1,0:T(4,128)(2,1)S(1)} async-done(((bf16[8,4,4,148]{3,2,1,0:T(4,128)(2,1)}), bf16[8,4,4,148]{3,2,1,0:T(4,128)(2,1)S(1)}, u32[]{:S(2)}, u32[]{:S(2)}) %all-to-all-start.1) | async-done | bytes 37920 | tf_op jit(solution)/shard_map/all_to_all | solution.py:167
  62.6 2.6 %stack.314 = bf16[4,32,24,125]{3,2,1,0:T(8,128)(2,1)S(1)} concatenate(bf16[4,32,1,125]{3,2,1,0:T(2,128)(2,1)S(1)} %copy.1584, bf16[4,32,1,125]{3,2,1,0:T(2,128)(2,1)S(1)} %copy.1585, bf16[4,32,1,125]{3,2,1,0:T(2,128)(2,1)S(1)} %copy.1586, bf16[4,32,1,125]{3,2,1,0:T(2,128)(2,1)S(1)} %copy.1587, bf16[4,32,1,125]{3,2,1,0:T(2,128)(2,1)S(1)} %copy.1588, ...), dimensions={2} | concatenate | bytes 1536000 | tf_op jit(solution)/shard_map/stack | solution.py:116
  65.2 6.3 %convolution_bitcast_fusion.1 = f32[12,50,125]{2,1,0:T(8,128)S(1)} fusion(bf16[12,4,32,24,50]{4,3,2,1,0:T(8,128)(2,1)} %bitcast_dynamic-update-slice_fusion, bf16[4,32,24,125]{3,2,1,0:T(8,128)(2,1)S(1)} %stack.314), kind=kOutput, calls=%fused_computation.6 | convolution fusion | flops 460800000 | bytes 4754400 | tf_op jit(solution)/shard_map/oxysb,xysu->obu/dot_general | solution.py:175
  71.7 6.7 %convolution_bitcast_fusion = f32[13,50,125]{2,1,0:T(8,128)S(1)} fusion(bf16[13,4,32,24,50]{4,3,2,1,0:T(8,128)(2,1)} %copy-done.1, bf16[4,32,24,125]{3,2,1,0:T(8,128)(2,1)S(1)} %stack.314), kind=kOutput, calls=%fused_computation.5 | convolution fusion | flops 499200000 | bytes 5086600 | tf_op jit(solution)/shard_map/oxysb,xysu->obu/dot_general | solution.py:175
  78.4 0.6 collective-permute-start.2
  79.1 0.7 convert_element_type.121
  79.7 12.9 %all-to-all-start.4 = ((bf16[16,19,125]{2,1,0:T(8,128)(2,1)}), bf16[16,19,125]{2,1,0:T(8,128)(2,1)S(1)}, u32[]{:S(2)}, u32[]{:S(2)}) async-start(bf16[16,19,125]{2,1,0:T(8,128)(2,1)} %convert_element_type.121), calls=%async_computation.4 | async-start | bytes 196608 | tf_op jit(solution)/shard_map/all_to_all | solution.py:71
  92.7 0.7 convert_element_type.119
  93.4 9.0 %all-to-all-done.4 = bf16[16,19,125]{2,1,0:T(8,128)(2,1)S(1)} async-done(((bf16[16,19,125]{2,1,0:T(8,128)(2,1)}), bf16[16,19,125]{2,1,0:T(8,128)(2,1)S(1)}, u32[]{:S(2)}, u32[]{:S(2)}) %all-to-all-start.4) | async-done | bytes 76032 | tf_op jit(solution)/shard_map/all_to_all | solution.py:71
  102.3 3.5 %all-to-all-start.2 = ((bf16[16,21,125]{2,1,0:T(8,128)(2,1)}), bf16[16,21,125]{2,1,0:T(8,128)(2,1)S(1)}, u32[]{:S(2)}, u32[]{:S(2)}) async-start(bf16[16,21,125]{2,1,0:T(8,128)(2,1)} %convert_element_type.119), calls=%async_computation.2 | async-start | bytes 196608 | tf_op jit(solution)/shard_map/all_to_all | solution.py:71
  105.9 9.7 %all-to-all-done.2 = bf16[16,21,125]{2,1,0:T(8,128)(2,1)S(1)} async-done(((bf16[16,21,125]{2,1,0:T(8,128)(2,1)}), bf16[16,21,125]{2,1,0:T(8,128)(2,1)S(1)}, u32[]{:S(2)}, u32[]{:S(2)}) %all-to-all-start.2) | async-done | bytes 84032 | tf_op jit(solution)/shard_map/all_to_all | solution.py:71
  115.6 0.7 broadcast_in_dim.533
  116.3 3.5 %all-to-all-start.5 = ((bf16[16,19,125]{2,1,0:T(8,128)(2,1)}), bf16[16,19,125]{2,1,0:T(8,128)(2,1)S(1)}, u32[]{:S(2)}, u32[]{:S(2)}) async-start(bf16[16,19,125]{2,1,0:T(8,128)(2,1)} %broadcast_in_dim.533), calls=%async_computation.5 | async-start | bytes 196608 | tf_op jit(solution)/shard_map/all_to_all | solution.py:74
  119.8 9.8 %all-to-all-done.5 = bf16[16,19,125]{2,1,0:T(8,128)(2,1)S(1)} async-done(((bf16[16,19,125]{2,1,0:T(8,128)(2,1)}), bf16[16,19,125]{2,1,0:T(8,128)(2,1)S(1)}, u32[]{:S(2)}, u32[]{:S(2)}) %all-to-all-start.5) | async-done | bytes 76032 | tf_op jit(solution)/shard_map/all_to_all | solution.py:74
  129.6 0.7 broadcast_in_dim.520
  130.3 3.5 %all-to-all-start.3 = ((bf16[16,21,125]{2,1,0:T(8,128)(2,1)}), bf16[16,21,125]{2,1,0:T(8,128)(2,1)S(1)}, u32[]{:S(2)}, u32[]{:S(2)}) async-start(bf16[16,21,125]{2,1,0:T(8,128)(2,1)} %broadcast_in_dim.520), calls=%async_computation.3 | async-start | bytes 196608 | tf_op jit(solution)/shard_map/all_to_all | solution.py:74
  133.8 4.2 %collective-permute-start.5 = (bf16[304,125]{1,0:T(8,128)(2,1)S(1)}, bf16[304,125]{1,0:T(8,128)(2,1)S(1)}, u32[]{:S(2)}, u32[]{:S(2)}) collective-permute-start(bf16[304,125]{1,0:T(8,128)(2,1)S(1)} %reshape.954), channel_id=1, source_target_pairs={{0,8},{8,0},{1,9},{9,1},{2,10},{10,2},{3,11},{11,3},{4,12},{12,4},... | collective-permute-start | bytes 228008 | tf_op jit(solution)/shard_map/ppermute | solution.py:75
  138.0 0.6 copy.1610
  138.6 4.9 %all-to-all-done.3 = bf16[16,21,125]{2,1,0:T(8,128)(2,1)S(1)} async-done(((bf16[16,21,125]{2,1,0:T(8,128)(2,1)}), bf16[16,21,125]{2,1,0:T(8,128)(2,1)S(1)}, u32[]{:S(2)}, u32[]{:S(2)}) %all-to-all-start.3) | async-done | bytes 84032 | tf_op jit(solution)/shard_map/all_to_all | solution.py:74
  143.6 5.3 %collective-permute-start.3 = (bf16[336,125]{1,0:T(8,128)(2,1)S(1)}, bf16[336,125]{1,0:T(8,128)(2,1)S(1)}, u32[]{:S(2)}, u32[]{:S(2)}) collective-permute-start(bf16[336,125]{1,0:T(8,128)(2,1)S(1)} %reshape.951), channel_id=1, source_target_pairs={{0,8},{8,0},{1,9},{9,1},{2,10},{10,2},{3,11},{11,3},{4,12},{12,4},... | collective-permute-start | bytes 252008 | tf_op jit(solution)/shard_map/ppermute | solution.py:75
  149.0 0.8 collective-permute-done.3
  150.0 0.9 convert_multiply_fusion
  (139 shorter events, 10.0 us)
Async XLA Ops:
  2.9 11.0 %all-to-all-start = ((f32[8,1,384]{2,1,0:T(1,128)}), f32[8,1,384]{2,1,0:T(1,128)S(1)}, u32[]{:S(2)}, u32[]{:S(2)}) async-start(f32[8,1,384]{2,1,0:T(1,128)} %reshape.961), calls=%async_computation | async-start | bytes 24576 | tf_op jit(solution)/shard_map/all_to_all | solution.py:139
  15.4 9.3 %collective-permute-start.1 = (f32[2,32,8,3]{2,1,3,0:T(8,128)S(1)}, f32[2,32,8,3]{2,1,3,0:T(8,128)S(1)}, u32[]{:S(2)}, u32[]{:S(2)}) collective-permute-start(f32[2,32,8,3]{2,1,3,0:T(8,128)S(1)} %bitcast.394), channel_id=1, source_target_pairs={{8,0},{16,8},{24,16},{32,24},{40,32},{48,40},{56,48},{64,56},{72,6... | collective-permute-start | bytes 18440 | tf_op jit(solution)/shard_map/ppermute | solution.py:18
  19.5 5.9 %collective-permute-start = (f32[2,32,8,3]{2,1,3,0:T(8,128)S(1)}, f32[2,32,8,3]{2,1,3,0:T(8,128)S(1)}, u32[]{:S(2)}, u32[]{:S(2)}) collective-permute-start(f32[2,32,8,3]{2,1,3,0:T(8,128)S(1)} %bitcast.395), channel_id=1, source_target_pairs={{0,8},{8,16},{16,24},{24,32},{32,40},{40,48},{48,56},{56,64},{64,7... | collective-permute-start | bytes 18440 | tf_op jit(solution)/shard_map/ppermute | solution.py:18
  30.4 2.2 %slice-start = ((s8[5734400]{0:T(1024)(128)(4,1)}), s8[4194304]{0:T(1024)(128)(4,1)S(1)}, s32[]{:S(2)}) async-start(s8[5734400]{0:T(1024)(128)(4,1)} %bitcast.397), calls=%async_computation.6 | async-start | bytes 8388608
  30.8 2.4 %slice-start.1 = ((s8[5734400]{0:T(1024)(128)(4,1)}), s8[1540096]{0:T(1024)(128)(4,1)S(1)}, s32[]{:S(2)}) async-start(s8[5734400]{0:T(1024)(128)(4,1)} %bitcast.397), calls=%async_computation.7 | async-start | bytes 3080192
  43.1 3.9 %copy-start.1 = (bf16[13,4,32,24,50]{4,3,2,1,0:T(8,128)(2,1)}, bf16[13,4,32,24,50]{4,3,2,1,0:T(8,128)(2,1)S(1)}, u32[]{:S(2)}) copy-start(bf16[13,4,32,24,50]{4,3,2,1,0:T(8,128)(2,1)S(1)} %get-tuple-element.30) | copy-start | bytes 11980804
  47.0 0.8 copy-start.2
  47.7 3.6 %copy-start = (bf16[12,4,32,24,50]{4,3,2,1,0:T(8,128)(2,1)}, bf16[12,4,32,24,50]{4,3,2,1,0:T(8,128)(2,1)S(1)}, u32[]{:S(2)}) copy-start(bf16[12,4,32,24,50]{4,3,2,1,0:T(8,128)(2,1)S(1)} %fusion.5) | copy-start | bytes 11059204
  52.3 8.5 %all-to-all-start.1 = ((bf16[8,4,4,148]{3,2,1,0:T(4,128)(2,1)}), bf16[8,4,4,148]{3,2,1,0:T(4,128)(2,1)S(1)}, u32[]{:S(2)}, u32[]{:S(2)}) async-start(bf16[8,4,4,148]{3,2,1,0:T(4,128)(2,1)} %maximum_bitcast_fusion), calls=%async_computation.1 | async-start | bytes 131072 | tf_op jit(solution)/shard_map/all_to_all | solution.py:167
  71.6 7.5 %collective-permute-start.4 = (f32[304,125]{1,0:T(8,128)S(1)}, f32[304,125]{1,0:T(8,128)S(1)}, u32[]{:S(2)}, u32[]{:S(2)}) collective-permute-start(f32[304,125]{1,0:T(8,128)S(1)} %pad_dynamic-slice_fusion.2), channel_id=1, source_target_pairs={{0,8},{8,0},{1,9},{9,1},{2,10},{10,2},{3,11},{11,3},{4,12},{12,4},... | collective-permute-start | bytes 456008 | tf_op jit(solution)/shard_map/ppermute | solution.py:69
  78.4 14.2 %collective-permute-start.2 = (f32[336,125]{1,0:T(8,128)S(1)}, f32[336,125]{1,0:T(8,128)S(1)}, u32[]{:S(2)}, u32[]{:S(2)}) collective-permute-start(f32[336,125]{1,0:T(8,128)S(1)} %pad_dynamic-slice_fusion), channel_id=1, source_target_pairs={{0,8},{8,0},{1,9},{9,1},{2,10},{10,2},{3,11},{11,3},{4,12},{12,4},... | collective-permute-start | bytes 504008 | tf_op jit(solution)/shard_map/ppermute | solution.py:69
  79.7 22.6 %all-to-all-start.4 = ((bf16[16,19,125]{2,1,0:T(8,128)(2,1)}), bf16[16,19,125]{2,1,0:T(8,128)(2,1)S(1)}, u32[]{:S(2)}, u32[]{:S(2)}) async-start(bf16[16,19,125]{2,1,0:T(8,128)(2,1)} %convert_element_type.121), calls=%async_computation.4 | async-start | bytes 196608 | tf_op jit(solution)/shard_map/all_to_all | solution.py:71
  102.3 13.3 %all-to-all-start.2 = ((bf16[16,21,125]{2,1,0:T(8,128)(2,1)}), bf16[16,21,125]{2,1,0:T(8,128)(2,1)S(1)}, u32[]{:S(2)}, u32[]{:S(2)}) async-start(bf16[16,21,125]{2,1,0:T(8,128)(2,1)} %convert_element_type.119), calls=%async_computation.2 | async-start | bytes 196608 | tf_op jit(solution)/shard_map/all_to_all | solution.py:71
  116.3 13.4 %all-to-all-start.5 = ((bf16[16,19,125]{2,1,0:T(8,128)(2,1)}), bf16[16,19,125]{2,1,0:T(8,128)(2,1)S(1)}, u32[]{:S(2)}, u32[]{:S(2)}) async-start(bf16[16,19,125]{2,1,0:T(8,128)(2,1)} %broadcast_in_dim.533), calls=%async_computation.5 | async-start | bytes 196608 | tf_op jit(solution)/shard_map/all_to_all | solution.py:74
  130.3 13.3 %all-to-all-start.3 = ((bf16[16,21,125]{2,1,0:T(8,128)(2,1)}), bf16[16,21,125]{2,1,0:T(8,128)(2,1)S(1)}, u32[]{:S(2)}, u32[]{:S(2)}) async-start(bf16[16,21,125]{2,1,0:T(8,128)(2,1)} %broadcast_in_dim.520), calls=%async_computation.3 | async-start | bytes 196608 | tf_op jit(solution)/shard_map/all_to_all | solution.py:74
  133.8 15.1 %collective-permute-start.5 = (bf16[304,125]{1,0:T(8,128)(2,1)S(1)}, bf16[304,125]{1,0:T(8,128)(2,1)S(1)}, u32[]{:S(2)}, u32[]{:S(2)}) collective-permute-start(bf16[304,125]{1,0:T(8,128)(2,1)S(1)} %reshape.954), channel_id=1, source_target_pairs={{0,8},{8,0},{1,9},{9,1},{2,10},{10,2},{3,11},{11,3},{4,12},{12,4},... | collective-permute-start | bytes 228008 | tf_op jit(solution)/shard_map/ppermute | solution.py:75
  143.6 6.3 %collective-permute-start.3 = (bf16[336,125]{1,0:T(8,128)(2,1)S(1)}, bf16[336,125]{1,0:T(8,128)(2,1)S(1)}, u32[]{:S(2)}, u32[]{:S(2)}) collective-permute-start(bf16[336,125]{1,0:T(8,128)(2,1)S(1)} %reshape.951), channel_id=1, source_target_pairs={{0,8},{8,0},{1,9},{9,1},{2,10},{10,2},{3,11},{11,3},{4,12},{12,4},... | collective-permute-start | bytes 252008 | tf_op jit(solution)/shard_map/ppermute | solution.py:75

commit v9 on v7

--- a/solution.py
+++ b/solution.py
@@ -151,9 +151,8 @@
     )
     cols_all = jnp.pad(col_module, 2, constant_values=-1)
 
-    own_source = lax.dynamic_slice_in_dim(source, col_start, tile_y + 4, 1)
-    own_cols = lax.dynamic_slice_in_dim(cols_all, col_start, tile_y + 4, 0)
-    stacked = gather_offsets(own_source, rows_wide, own_cols, tile_x, tile_y)
+    stacked_band = gather_offsets(source, rows_wide, cols_all, tile_x, width)
+    stacked = lax.dynamic_slice_in_dim(stacked_band, col_start, tile_y, 2)
     partial_value = jnp.einsum(
         "oxysb,obt->xyst", stacked, weights, preferred_element_type=jnp.float32
     )
@@ -167,7 +166,6 @@
     got = lax.all_to_all(sent, "py", 0, 0)
     band_resid = jnp.transpose(got, (1, 0, 2, 3)).reshape(tile_x, width, span)
 
-    stacked_band = gather_offsets(source, rows_wide, cols_all, tile_x, width)
     gradient = jnp.einsum(
         "oxysb,xysu->obu",
         stacked_band,

time: 123 us -> 115 us (0.935)
  local copies, waits for them, and re-layouts: 20.4 us -> 12.3 us
  waiting for transfers between devices: 7.89 us -> 14.9 us
  other arithmetic: 18.1 us -> 13.9 us
  blocking collectives: 36.3 us -> 34.1 us
    unnamed x39 -> x38, local copies, waits for them, and re-layouts: 10.4 us -> 2.97 us
    ppermute x2, waiting for transfers between devices: 0.52 us -> 4.41 us  [passed_along(): return lax.ppermute(block, axis, route)]
    unnamed x47 -> x24, other arithmetic: 10.9 us -> 7.53 us
    all_to_all x1, blocking collectives: 23.5 us -> 21.2 us  [chip_sum(): got = lax.all_to_all(pieces, 'pxa', 0, 0).astype(jnp.float32)]
    all_to_all x1, waiting for transfers between devices: 2.86 us -> 5.12 us  [on_device(): got = lax.all_to_all(sent, 'py', 0, 0)]
  transfers between devices with their start and end apart: 6 -> 6, of which waited for: 5 -> 5; matrix products, arithmetic and copies ran while one was open for 5% -> 3% of each run, Pallas kernels for 0% -> 0%
where the time goes in v9:
time: 115 us
  blocking collectives  34.1 us (30%)
  starting transfers between devices  20.7 us (18%)
  matrix products  17.4 us (15%)
  waiting for transfers between devices  14.9 us (13%)
  other arithmetic  13.9 us (12%)
  local copies, waits for them, and re-layouts  12.3 us (11%)
  between operations  1.55 us (1%)
    all_to_all x1, blocking collectives, chip_sum(): got = lax.all_to_all(pieces, 'pxa', 0, 0).astype(jnp.float32)  21.2 us
    all_to_all x1, blocking collectives, chip_sum(): lax.all_to_all(spread, 'pxa', 0, 0).reshape((half,) + value.shape[1:])  12.9 us
    dot_general x1, matrix products, on_device(): jnp.einsum('oxysb,xysu->obu', stacked_band, windows(band_resid, share), p...  11.9 us
    ppermute x2, starting transfers between devices, passed_along(): return lax.ppermute(block, axis, route)  8.27 us
    unnamed x24, other arithmetic  7.53 us
    all_to_all x1, starting transfers between devices, on_device(): band = jnp.transpose(lax.all_to_all(spread, 'py', 0, 0), (1, 0, 2, 3, 4))  5.94 us
    all_to_all x1, waiting for transfers between devices, on_device(): got = lax.all_to_all(sent, 'py', 0, 0)  5.12 us
    ppermute x2, waiting for transfers between devices, passed_along(): return lax.ppermute(block, axis, route)  4.41 us
  transfers between devices with their start and end apart: 6, of which 5 were waited for; matrix products, arithmetic and copies ran while one was open for 3% of the time, Pallas kernels for 0%

profile of v9, /device:TPU:1, one launch (start us, length us, event | category | flops | bytes accessed | tf_op | source)
XLA Modules:
  0.0 114.9 jit_solution(945687265127936210)
XLA Ops:
  0.6 0.7 convert_bitcast_fusion
  1.3 0.7 pad_maximum_fusion.2
  2.1 0.8 reshape.496
  2.9 5.9 %all-to-all-start = ((f32[8,1,384]{2,1,0:T(1,128)}), f32[8,1,384]{2,1,0:T(1,128)S(1)}, u32[]{:S(2)}, u32[]{:S(2)}) async-start(f32[8,1,384]{2,1,0:T(1,128)} %reshape.496), calls=%async_computation | async-start | bytes 24576 | tf_op jit(solution)/shard_map/all_to_all | solution.py:139
  8.8 0.7 pad_dynamic-slice_fusion.2
  9.6 0.9 slice_compare_fusion.3
  10.6 3.3 %all-to-all-done = f32[8,1,384]{2,1,0:T(1,128)S(1)} async-done(((f32[8,1,384]{2,1,0:T(1,128)}), f32[8,1,384]{2,1,0:T(1,128)S(1)}, u32[]{:S(2)}, u32[]{:S(2)}) %all-to-all-start) | async-done | bytes 12320 | tf_op jit(solution)/shard_map/all_to_all | solution.py:139
  13.9 0.5 broadcast.494
  14.4 0.7 reduce.1
  15.1 0.3 reshape.497
  15.4 6.3 %collective-permute-start = (f32[2,32,8,3]{2,1,3,0:T(8,128)S(1)}, f32[2,32,8,3]{2,1,3,0:T(8,128)S(1)}, u32[]{:S(2)}, u32[]{:S(2)}) collective-permute-start(f32[2,32,8,3]{2,1,3,0:T(8,128)S(1)} %bitcast.289), channel_id=1, source_target_pairs={{0,8},{8,16},{16,24},{24,32},{32,40},{40,48},{48,56},{56,64},{64,7... | collective-permute-start | bytes 18440 | tf_op jit(solution)/shard_map/ppermute | solution.py:18
  21.8 1.9 %collective-permute-start.1 = (f32[2,32,8,3]{2,1,3,0:T(8,128)S(1)}, f32[2,32,8,3]{2,1,3,0:T(8,128)S(1)}, u32[]{:S(2)}, u32[]{:S(2)}) collective-permute-start(f32[2,32,8,3]{2,1,3,0:T(8,128)S(1)} %bitcast.290), channel_id=1, source_target_pairs={{8,0},{16,8},{24,16},{32,24},{40,32},{48,40},{56,48},{64,56},{72,6... | collective-permute-start | bytes 18440 | tf_op jit(solution)/shard_map/ppermute | solution.py:18
  23.8 0.7 convert_element_type.107
  24.5 0.1 copy.1565
  24.6 0.1 copy.1535
  24.8 4.4 %collective-permute-done.1 = f32[2,32,8,3]{2,1,3,0:T(8,128)S(1)} collective-permute-done((f32[2,32,8,3]{2,1,3,0:T(8,128)S(1)}, f32[2,32,8,3]{2,1,3,0:T(8,128)S(1)}, u32[]{:S(2)}, u32[]{:S(2)}) %collective-permute-start.1) | collective-permute-done | bytes 6176 | tf_op jit(solution)/shard_map/ppermute | solution.py:18
  29.6 0.1 copy.1538
  29.7 2.9 %convolution_convert_fusion = bf16[8,32,24,50]{3,2,1,0:T(8,128)(2,1)S(1)} fusion(s32[8,32,8]{2,1,0:T(8,128)S(1)} %copy.1539, bf16[8,32,8]{2,1,0:T(8,128)(2,1)S(1)} %copy.1538, s32[8,32,8]{2,1,0:T(8,128)S(1)} %copy.1537), kind=kOutput, calls=%fused_computation.4 | convolution fusion | flops 5115904 | bytes 634880 | tf_op jit(solution)/shard_map/xyks,xykb->xysb/dot_general | solution.py:85
  32.6 0.2 bitcast_dynamic-update-slice_fusion.19
  32.8 0.3 bitcast_dynamic-update-slice_fusion.18
  33.2 0.3 fusion.13
  33.5 0.3 bitcast_dynamic-update-slice_fusion.17
  33.8 0.3 bitcast_dynamic-update-slice_fusion.16
  34.2 0.3 bitcast_dynamic-update-slice_fusion.15
  34.5 0.3 bitcast_dynamic-update-slice_fusion.14
  34.9 0.3 fusion.11
  35.2 0.3 bitcast_dynamic-update-slice_fusion.13
  35.5 0.3 bitcast_dynamic-update-slice_fusion.12
  35.9 0.3 bitcast_dynamic-update-slice_fusion.11
  36.2 0.3 bitcast_dynamic-update-slice_fusion.10
  36.6 0.1 fusion.9
  36.7 0.3 bitcast_dynamic-update-slice_fusion.9
  37.0 0.3 bitcast_dynamic-update-slice_fusion.8
  37.4 0.3 bitcast_dynamic-update-slice_fusion.7
  37.8 0.3 bitcast_dynamic-update-slice_fusion.6
  38.1 0.3 fusion.8
  38.4 0.3 bitcast_dynamic-update-slice_fusion.5
  38.7 0.3 bitcast_dynamic-update-slice_fusion.4
  39.1 0.3 bitcast_dynamic-update-slice_fusion.3
  39.5 0.3 bitcast_dynamic-update-slice_fusion.2
  39.8 0.3 fusion.6
  40.1 0.3 bitcast_dynamic-update-slice_fusion.1
  40.5 0.3 bitcast_dynamic-update-slice_fusion
  40.8 2.6 %fusion = f32[4,4,24,1000,1]{3,2,1,0,4:T(8,128)S(1)} fusion(f32[25,50,1000]{2,1,0:T(8,128)S(1)} %bitcast.293, bf16[25,4,32,24,50]{4,3,2,1,0:T(8,128)(2,1)S(1)} %bitcast_dynamic-update-slice_fusion, s32[]{:T(128)S(6)} %select_n.123), kind=kOutput, calls=%fused_computation | convolution fusion | flops 961249984 | bytes 9728004 | tf_op jit(solution)/shard_map/oxysb,obt->xyst/dot_general | solution.py:156
  43.5 0.2 copy.1674
  43.7 1.2 %fusion.25 = (f32[4,4,1,1000]{3,2,1,0:T(1,128)S(1)}, f32[4,4,1,1000]{3,2,1,0:T(1,128)S(1)}, f32[4,4,1,1000]{3,2,1,0:T(1,128)S(1)}, f32[4,4,1,1000]{3,2,1,0:T(1,1...) fusion(f32[4,4,24,1000]{3,2,1,0:T(8,128)S(1)} %bitcast.257), kind=kLoop, calls=%fused_computation.145 | loop fusion | bytes 2432000 | tf_op jit(solution)/shard_map/slice | solution.py:110
  44.9 0.3 fusion.26
  46.5 1.2 %multiply_convert_fusion = (bf16[4,4,1024]{2,0,1:T(4,128)(2,1)S(1)}, bf16[4,4,1024]{2,0,1:T(4,128)(2,1)S(1)}) fusion(bf16[4,4,1024]{2,1,0:T(4,128)(2,1)S(1)} %copy-done, f32[4,4]{0,1:T(4,128)S(1)} %copy.1565, f32[4,4,1000]{2,0,1:T(4,128)S(1)} %bitcast.263, f32[4,4,1000]{2,0,1:T(4,128)S(1)} %bitcast.283, f32[4,4,1000]{2,0,1:T(4,128)S(1)} %bitcast.264, ...), kind=kLoop, calls=%fused_computation.83 | loop fusion | flops 458752 | bytes 1634368 | tf_op jit(solution)/shard_map/convert_element_type | solution.py:122
  47.8 0.1 reshape.487
  47.9 0.1 reshape.488
  48.1 0.7 maximum_bitcast_fusion
  48.8 3.4 %all-to-all-start.1 = ((bf16[8,4,4,148]{3,2,1,0:T(4,128)(2,1)}), bf16[8,4,4,148]{3,2,1,0:T(4,128)(2,1)S(1)}, u32[]{:S(2)}, u32[]{:S(2)}) async-start(bf16[8,4,4,148]{3,2,1,0:T(4,128)(2,1)} %maximum_bitcast_fusion), calls=%async_computation.1 | async-start | bytes 131072 | tf_op jit(solution)/shard_map/all_to_all | solution.py:166
  52.2 5.1 %all-to-all-done.1 = bf16[8,4,4,148]{3,2,1,0:T(4,128)(2,1)S(1)} async-done(((bf16[8,4,4,148]{3,2,1,0:T(4,128)(2,1)}), bf16[8,4,4,148]{3,2,1,0:T(4,128)(2,1)S(1)}, u32[]{:S(2)}, u32[]{:S(2)}) %all-to-all-start.1) | async-done | bytes 37920 | tf_op jit(solution)/shard_map/all_to_all | solution.py:166
  57.4 0.2 slice_bitcast_fusion.1
  57.6 0.1 slice_bitcast_fusion.20
  59.2 2.6 %stack.219 = bf16[4,32,24,125]{3,2,1,0:T(8,128)(2,1)S(1)} concatenate(bf16[4,32,1,125]{3,2,1,0:T(2,128)(2,1)S(1)} %copy.1569, bf16[4,32,1,125]{3,2,1,0:T(2,128)(2,1)S(1)} %copy.1570, bf16[4,32,1,125]{3,2,1,0:T(2,128)(2,1)S(1)} %copy.1571, bf16[4,32,1,125]{3,2,1,0:T(2,128)(2,1)S(1)} %copy.1572, bf16[4,32,1,125]{3,2,1,0:T(2,128)(2,1)S(1)} %copy.1573, ...), dimensions={2} | concatenate | bytes 1536000 | tf_op jit(solution)/shard_map/stack | solution.py:116
  61.8 11.9 %convolution_bitcast_fusion = f32[25,50,125]{2,1,0:T(8,128)S(1)} fusion(bf16[25,4,32,24,50]{4,3,2,1,0:T(8,128)(2,1)} %copy-done.1, bf16[4,32,24,125]{3,2,1,0:T(8,128)(2,1)S(1)} %stack.219), kind=kOutput, calls=%fused_computation.6 | convolution fusion | flops 960000000 | bytes 9073000 | tf_op jit(solution)/shard_map/oxysb,xysu->obu/dot_general | solution.py:169
  73.9 1.6 %collective-permute-done.2 = f32[640,125]{1,0:T(8,128)S(1)} collective-permute-done((f32[640,125]{1,0:T(8,128)S(1)}, f32[640,125]{1,0:T(8,128)S(1)}, u32[]{:S(2)}, u32[]{:S(2)}) %collective-permute-start.2) | collective-permute-done | bytes 320032 | tf_op jit(solution)/shard_map/ppermute | solution.py:69
  75.6 21.2 %all_to_all.20 = bf16[16,40,125]{2,1,0:T(8,128)(2,1)S(1)} all-to-all(bf16[16,40,125]{2,1,0:T(8,128)(2,1)S(1)} %bitcast.262), channel_id=1, replica_groups=mesh['pxa'=16,'pxc'=2,'py'=8] {'pxa'}, dimensions={0} | all-to-all | bytes 320000 | tf_op jit(solution)/shard_map/all_to_all | solution.py:71
  96.9 12.9 %all_to_all.21 = bf16[16,40,125]{2,1,0:T(8,128)(2,1)S(1)} all-to-all(bf16[16,40,125]{2,1,0:T(8,128)(2,1)S(1)} %broadcast_in_dim.272), channel_id=1, replica_groups=mesh['pxa'=16,'pxc'=2,'py'=8] {'pxa'}, dimensions={0} | all-to-all | bytes 320000 | tf_op jit(solution)/shard_map/all_to_all | solution.py:74
  109.8 3.0 %collective-permute-start.3 = (bf16[640,125]{1,0:T(8,128)(2,1)S(1)}, bf16[640,125]{1,0:T(8,128)(2,1)S(1)}, u32[]{:S(2)}, u32[]{:S(2)}) collective-permute-start(bf16[640,125]{1,0:T(8,128)(2,1)S(1)} %bitcast.261), channel_id=1, source_target_pairs={{0,8},{8,0},{1,9},{9,1},{2,10},{10,2},{3,11},{11,3},{4,12},{12,4},... | collective-permute-start | bytes 480008 | tf_op jit(solution)/shard_map/ppermute | solution.py:75
  112.8 0.6 copy.1594
  113.5 0.4 collective-permute-done.3
  114.0 0.9 div.10
  (87 shorter events, 3.7 us)
Async XLA Ops:
  2.9 11.0 %all-to-all-start = ((f32[8,1,384]{2,1,0:T(1,128)}), f32[8,1,384]{2,1,0:T(1,128)S(1)}, u32[]{:S(2)}, u32[]{:S(2)}) async-start(f32[8,1,384]{2,1,0:T(1,128)} %reshape.496), calls=%async_computation | async-start | bytes 24576 | tf_op jit(solution)/shard_map/all_to_all | solution.py:139
  15.4 9.3 %collective-permute-start = (f32[2,32,8,3]{2,1,3,0:T(8,128)S(1)}, f32[2,32,8,3]{2,1,3,0:T(8,128)S(1)}, u32[]{:S(2)}, u32[]{:S(2)}) collective-permute-start(f32[2,32,8,3]{2,1,3,0:T(8,128)S(1)} %bitcast.289), channel_id=1, source_target_pairs={{0,8},{8,16},{16,24},{24,32},{32,40},{40,48},{48,56},{56,64},{64,7... | collective-permute-start | bytes 18440 | tf_op jit(solution)/shard_map/ppermute | solution.py:18
  21.8 7.4 %collective-permute-start.1 = (f32[2,32,8,3]{2,1,3,0:T(8,128)S(1)}, f32[2,32,8,3]{2,1,3,0:T(8,128)S(1)}, u32[]{:S(2)}, u32[]{:S(2)}) collective-permute-start(f32[2,32,8,3]{2,1,3,0:T(8,128)S(1)} %bitcast.290), channel_id=1, source_target_pairs={{8,0},{16,8},{24,16},{32,24},{40,32},{48,40},{56,48},{64,56},{72,6... | collective-permute-start | bytes 18440 | tf_op jit(solution)/shard_map/ppermute | solution.py:18
  34.9 5.9 %slice-start = ((s8[5734400]{0:T(1024)(128)(4,1)}), s8[4194304]{0:T(1024)(128)(4,1)S(1)}, s32[]{:S(2)}) async-start(s8[5734400]{0:T(1024)(128)(4,1)} %bitcast.292), calls=%async_computation.4 | async-start | bytes 8388608
  37.7 3.1 %slice-start.1 = ((s8[5734400]{0:T(1024)(128)(4,1)}), s8[1540096]{0:T(1024)(128)(4,1)S(1)}, s32[]{:S(2)}) async-start(s8[5734400]{0:T(1024)(128)(4,1)} %bitcast.292), calls=%async_computation.5 | async-start | bytes 3080192
  39.1 7.4 %copy-start = (bf16[4,4,1024]{2,1,0:T(4,128)(2,1)S(1)}, bf16[4,4,1024]{2,1,0:T(4,128)(2,1)}, u32[]{:S(2)}) copy-start(bf16[4,4,1024]{2,1,0:T(4,128)(2,1)} %param.13) | copy-start | bytes 98308
  40.8 7.0 %copy-start.1 = (bf16[25,4,32,24,50]{4,3,2,1,0:T(8,128)(2,1)}, bf16[25,4,32,24,50]{4,3,2,1,0:T(8,128)(2,1)S(1)}, u32[]{:S(2)}) copy-start(bf16[25,4,32,24,50]{4,3,2,1,0:T(8,128)(2,1)S(1)} %bitcast_dynamic-update-slice_fusion) | copy-start | bytes 23040004
  48.8 8.5 %all-to-all-start.1 = ((bf16[8,4,4,148]{3,2,1,0:T(4,128)(2,1)}), bf16[8,4,4,148]{3,2,1,0:T(4,128)(2,1)S(1)}, u32[]{:S(2)}, u32[]{:S(2)}) async-start(bf16[8,4,4,148]{3,2,1,0:T(4,128)(2,1)} %maximum_bitcast_fusion), calls=%async_computation.1 | async-start | bytes 131072 | tf_op jit(solution)/shard_map/all_to_all | solution.py:166
  73.8 1.7 %collective-permute-start.2 = (f32[640,125]{1,0:T(8,128)S(1)}, f32[640,125]{1,0:T(8,128)S(1)}, u32[]{:S(2)}, u32[]{:S(2)}) collective-permute-start(f32[640,125]{1,0:T(8,128)S(1)} %pad_dynamic-slice_fusion), channel_id=1, source_target_pairs={{0,8},{8,0},{1,9},{9,1},{2,10},{10,2},{3,11},{11,3},{4,12},{12,4},... | collective-permute-start | bytes 960008 | tf_op jit(solution)/shard_map/ppermute | solution.py:69
  109.8 4.1 %collective-permute-start.3 = (bf16[640,125]{1,0:T(8,128)(2,1)S(1)}, bf16[640,125]{1,0:T(8,128)(2,1)S(1)}, u32[]{:S(2)}, u32[]{:S(2)}) collective-permute-start(bf16[640,125]{1,0:T(8,128)(2,1)S(1)} %bitcast.261), channel_id=1, source_target_pairs={{0,8},{8,0},{1,9},{9,1},{2,10},{10,2},{3,11},{11,3},{4,12},{12,4},... | collective-permute-start | bytes 480008 | tf_op jit(solution)/shard_map/ppermute | solution.py:75

commit v10 on v9

--- a/solution.py
+++ b/solution.py
@@ -116,6 +116,12 @@
     return jnp.stack([resid[:, :, offset : offset + ticks] for offset in range(SHIFTS)], axis=2)
 
 
+def toeplitz(resid, ticks):
+    length = resid.shape[2]
+    tiled = jnp.tile(resid, (1, 1, SHIFTS + 1))[:, :, : SHIFTS * (length + 1)]
+    return tiled.reshape(resid.shape[:2] + (SHIFTS, length + 1))[..., :ticks]
+
+
 def residual_of(prediction, measured, active):
     return (
         (prediction - measured.astype(jnp.float32)) * active.astype(jnp.float32)[..., None]
@@ -169,7 +175,7 @@
     gradient = jnp.einsum(
         "oxysb,xysu->obu",
         stacked_band,
-        windows(band_resid, share),
+        toeplitz(band_resid, share),
         preferred_element_type=jnp.float32,
     )
     flat = gradient.reshape(-1, share)

time: 115 us -> 116 us (level)
    reshape x1, local copies, waits for them, and re-layouts: 0.04 us -> 2.33 us  [toeplitz(): return tiled.reshape(resid.shape[:2] + (SHIFTS, length + 1))[..., :ticks]]
    another operation x27 -> x3, local copies, waits for them, and re-layouts: 4.18 us -> 2.42 us  [toeplitz(): tiled = jnp.tile(resid, (1, 1, SHIFTS + 1))[:, :, :SHIFTS * (length + 1)]]
    unnamed x38 -> x37, local copies, waits for them, and re-layouts: 2.97 us -> 2.33 us
  transfers between devices with their start and end apart: 6 -> 6, of which waited for: 5 -> 5; matrix products, arithmetic and copies ran while one was open for 3% -> 2% of each run, Pallas kernels for 0% -> 0%
where the time goes in v10:
time: 116 us
  blocking collectives  34.1 us (29%)
  starting transfers between devices  20.7 us (18%)
  matrix products  17.4 us (15%)
  waiting for transfers between devices  15.6 us (13%)
  other arithmetic  14.4 us (12%)
  local copies, waits for them, and re-layouts  12.1 us (10%)
  between operations  1.36 us (1%)
    all_to_all x1, blocking collectives, chip_sum(): got = lax.all_to_all(pieces, 'pxa', 0, 0).astype(jnp.float32)  21.2 us
    all_to_all x1, blocking collectives, chip_sum(): lax.all_to_all(spread, 'pxa', 0, 0).reshape((half,) + value.shape[1:])  12.9 us
    dot_general x1, matrix products, on_device(): jnp.einsum('oxysb,xysu->obu', stacked_band, toeplitz(band_resid, share),...  11.8 us
    ppermute x2, starting transfers between devices, passed_along(): return lax.ppermute(block, axis, route)  8.27 us
    unnamed x24, other arithmetic  7.53 us
    all_to_all x1, starting transfers between devices, on_device(): band = jnp.transpose(lax.all_to_all(spread, 'py', 0, 0), (1, 0, 2, 3, 4))  5.94 us
    all_to_all x1, waiting for transfers between devices, on_device(): got = lax.all_to_all(sent, 'py', 0, 0)  5.12 us
    ppermute x2, waiting for transfers between devices, passed_along(): return lax.ppermute(block, axis, route)  4.51 us
  transfers between devices with their start and end apart: 6, of which 5 were waited for; matrix products, arithmetic and copies ran while one was open for 2% of the time, Pallas kernels for 0%

profile of v10, /device:TPU:1, one launch (start us, length us, event | category | flops | bytes accessed | tf_op | source)
XLA Modules:
  0.0 115.7 jit_solution(7030841855136142222)
XLA Ops:
  0.6 0.7 convert_bitcast_fusion
  1.3 0.7 pad_maximum_fusion.2
  2.1 0.8 reshape.500
  2.9 5.9 %all-to-all-start = ((f32[8,1,384]{2,1,0:T(1,128)}), f32[8,1,384]{2,1,0:T(1,128)S(1)}, u32[]{:S(2)}, u32[]{:S(2)}) async-start(f32[8,1,384]{2,1,0:T(1,128)} %reshape.500), calls=%async_computation | async-start | bytes 24576 | tf_op jit(solution)/shard_map/all_to_all | solution.py:145
  8.8 0.7 pad_dynamic-slice_fusion.2
  9.6 0.9 slice_compare_fusion.3
  10.6 3.3 %all-to-all-done = f32[8,1,384]{2,1,0:T(1,128)S(1)} async-done(((f32[8,1,384]{2,1,0:T(1,128)}), f32[8,1,384]{2,1,0:T(1,128)S(1)}, u32[]{:S(2)}, u32[]{:S(2)}) %all-to-all-start) | async-done | bytes 12320 | tf_op jit(solution)/shard_map/all_to_all | solution.py:145
  13.9 0.5 broadcast.496
  14.4 0.7 reduce.1
  15.1 0.3 reshape.501
  15.4 6.3 %collective-permute-start = (f32[2,32,8,3]{2,1,3,0:T(8,128)S(1)}, f32[2,32,8,3]{2,1,3,0:T(8,128)S(1)}, u32[]{:S(2)}, u32[]{:S(2)}) collective-permute-start(f32[2,32,8,3]{2,1,3,0:T(8,128)S(1)} %bitcast.239), channel_id=1, source_target_pairs={{0,8},{8,16},{16,24},{24,32},{32,40},{40,48},{48,56},{56,64},{64,7... | collective-permute-start | bytes 18440 | tf_op jit(solution)/shard_map/ppermute | solution.py:18
  21.8 1.9 %collective-permute-start.1 = (f32[2,32,8,3]{2,1,3,0:T(8,128)S(1)}, f32[2,32,8,3]{2,1,3,0:T(8,128)S(1)}, u32[]{:S(2)}, u32[]{:S(2)}) collective-permute-start(f32[2,32,8,3]{2,1,3,0:T(8,128)S(1)} %bitcast.240), channel_id=1, source_target_pairs={{8,0},{16,8},{24,16},{32,24},{40,32},{48,40},{56,48},{64,56},{72,6... | collective-permute-start | bytes 18440 | tf_op jit(solution)/shard_map/ppermute | solution.py:18
  23.8 0.7 convert_element_type.107
  24.5 0.1 copy.102
  24.7 4.5 %collective-permute-done.1 = f32[2,32,8,3]{2,1,3,0:T(8,128)S(1)} collective-permute-done((f32[2,32,8,3]{2,1,3,0:T(8,128)S(1)}, f32[2,32,8,3]{2,1,3,0:T(8,128)S(1)}, u32[]{:S(2)}, u32[]{:S(2)}) %collective-permute-start.1) | collective-permute-done | bytes 6176 | tf_op jit(solution)/shard_map/ppermute | solution.py:18
  29.5 0.1 copy.106
  29.6 0.1 copy.105
  29.7 2.9 %convolution_convert_fusion = bf16[8,32,24,50]{3,2,1,0:T(8,128)(2,1)S(1)} fusion(s32[8,32,8]{2,1,0:T(8,128)S(1)} %copy.106, bf16[8,32,8]{2,1,0:T(8,128)(2,1)S(1)} %copy.105, s32[8,32,8]{2,1,0:T(8,128)S(1)} %copy.104), kind=kOutput, calls=%fused_computation.4 | convolution fusion | flops 5115904 | bytes 634880 | tf_op jit(solution)/shard_map/xyks,xykb->xysb/dot_general | solution.py:85
  32.6 0.2 bitcast_dynamic-update-slice_fusion.19
  32.8 0.3 bitcast_dynamic-update-slice_fusion.18
  33.2 0.3 fusion.13
  33.5 0.3 bitcast_dynamic-update-slice_fusion.17
  33.8 0.3 bitcast_dynamic-update-slice_fusion.16
  34.2 0.3 bitcast_dynamic-update-slice_fusion.15
  34.5 0.3 bitcast_dynamic-update-slice_fusion.14
  34.9 0.3 fusion.11
  35.2 0.3 bitcast_dynamic-update-slice_fusion.13
  35.5 0.3 bitcast_dynamic-update-slice_fusion.12
  35.9 0.3 bitcast_dynamic-update-slice_fusion.11
  36.2 0.3 bitcast_dynamic-update-slice_fusion.10
  36.6 0.1 fusion.9
  36.7 0.3 bitcast_dynamic-update-slice_fusion.9
  37.0 0.3 bitcast_dynamic-update-slice_fusion.8
  37.4 0.3 bitcast_dynamic-update-slice_fusion.7
  37.8 0.3 bitcast_dynamic-update-slice_fusion.6
  38.1 0.3 fusion.8
  38.4 0.3 bitcast_dynamic-update-slice_fusion.5
  38.7 0.3 bitcast_dynamic-update-slice_fusion.4
  39.1 0.3 bitcast_dynamic-update-slice_fusion.3
  39.5 0.3 bitcast_dynamic-update-slice_fusion.2
  39.8 0.3 fusion.6
  40.1 0.3 bitcast_dynamic-update-slice_fusion.1
  40.5 0.3 bitcast_dynamic-update-slice_fusion
  40.8 2.6 %fusion = f32[4,4,24,1000,1]{3,2,0,1,4:T(8,128)S(1)} fusion(f32[25,50,1000]{2,1,0:T(8,128)S(1)} %bitcast.243, bf16[25,4,32,24,50]{4,3,2,1,0:T(8,128)(2,1)S(1)} %bitcast_dynamic-update-slice_fusion, s32[]{:T(128)S(6)} %select_n.123), kind=kOutput, calls=%fused_computation | convolution fusion | flops 961249984 | bytes 9728004 | tf_op jit(solution)/shard_map/oxysb,obt->xyst/dot_general | solution.py:162
  43.5 0.2 copy.214
  43.6 1.2 %fusion.23 = (f32[4,4,1,1000]{3,2,0,1:T(1,128)S(1)}, f32[4,4,1,1000]{3,2,0,1:T(1,128)S(1)}, f32[4,4,1,1000]{3,2,0,1:T(1,128)S(1)}, f32[4,4,1,1000]{3,2,0,1:T(1,1...) fusion(f32[4,4,24,1000]{3,2,0,1:T(8,128)S(1)} %bitcast.207), kind=kLoop, calls=%fused_computation.121 | loop fusion | bytes 2432000 | tf_op jit(solution)/shard_map/slice | solution.py:110
  44.9 0.3 fusion.24
  46.5 1.7 %multiply_convert_fusion = (bf16[4,4,1024]{2,1,0:T(4,128)(2,1)S(1)}, bf16[4,4,1024]{2,1,0:T(4,128)(2,1)}) fusion(bf16[4,4,1024]{2,1,0:T(4,128)(2,1)S(1)} %copy-done, f32[4,4]{1,0:T(4,128)S(1)} %convert_element_type.107, f32[4,4,1000]{2,1,0:T(4,128)S(1)} %bitcast.213, f32[4,4,1000]{2,1,0:T(4,128)S(1)} %bitcast.233, f32[4,4,1000]{2,1,0:T(4,128)S(1)} %bitcast.214, ...), kind=kLoop, calls=%fused_computation.83 | loop fusion | flops 458752 | bytes 1634368 | tf_op jit(solution)/shard_map/convert_element_type | solution.py:128
  48.3 0.1 reshape.491
  48.4 0.1 reshape.492
  48.5 0.7 maximum_bitcast_fusion
  49.3 3.4 %all-to-all-start.1 = ((bf16[8,4,4,148]{3,1,2,0:T(4,128)(2,1)}), bf16[8,4,4,148]{3,1,2,0:T(4,128)(2,1)S(1)}, u32[]{:S(2)}, u32[]{:S(2)}) async-start(bf16[8,4,4,148]{3,1,2,0:T(4,128)(2,1)} %maximum_bitcast_fusion), calls=%async_computation.1 | async-start | bytes 131072 | tf_op jit(solution)/shard_map/all_to_all | solution.py:172
  52.6 5.1 %all-to-all-done.1 = bf16[8,4,4,148]{3,1,2,0:T(4,128)(2,1)S(1)} async-done(((bf16[8,4,4,148]{3,1,2,0:T(4,128)(2,1)}), bf16[8,4,4,148]{3,1,2,0:T(4,128)(2,1)S(1)}, u32[]{:S(2)}, u32[]{:S(2)}) %all-to-all-start.1) | async-done | bytes 37920 | tf_op jit(solution)/shard_map/all_to_all | solution.py:172
  57.8 0.2 tile.11
  57.9 2.3 %tile.12 = bf16[4,32,3700]{2,1,0:T(8,128)(2,1)S(1)} reshape(bf16[4,32,25,148]{3,2,1,0:T(8,128)(2,1)S(1)} %tile.11) | data formatting | bytes 1894400 | tf_op jit(solution)/shard_map/tile | solution.py:121
  60.3 2.3 %reshape.493 = bf16[4,32,24,149]{3,2,1,0:T(8,128)(2,1)S(1)} reshape(bf16[4,32,3576]{2,1,0:T(8,128)(2,1)S(1)} %slice.417) | data formatting | bytes 1830912 | tf_op jit(solution)/shard_map/reshape | solution.py:122
  62.6 11.8 %convolution_bitcast_fusion = f32[25,50,125]{2,1,0:T(8,128)S(1)} fusion(bf16[25,4,32,24,50]{4,3,2,1,0:T(8,128)(2,1)} %copy-done.1, bf16[4,32,24,149]{3,2,1,0:T(8,128)(2,1)S(1)} %reshape.493), kind=kOutput, calls=%fused_computation.6 | convolution fusion | flops 960000000 | bytes 9091432 | tf_op jit(solution)/shard_map/oxysb,xysu->obu/dot_general | solution.py:175
  74.6 0.1 collective-permute-start.2
  74.7 1.6 %collective-permute-done.2 = f32[640,125]{1,0:T(8,128)S(1)} collective-permute-done((f32[640,125]{1,0:T(8,128)S(1)}, f32[640,125]{1,0:T(8,128)S(1)}, u32[]{:S(2)}, u32[]{:S(2)}) %collective-permute-start.2) | collective-permute-done | bytes 320032 | tf_op jit(solution)/shard_map/ppermute | solution.py:69
  76.4 21.2 %all_to_all.20 = bf16[16,40,125]{2,1,0:T(8,128)(2,1)S(1)} all-to-all(bf16[16,40,125]{2,1,0:T(8,128)(2,1)S(1)} %bitcast.212), channel_id=1, replica_groups=mesh['pxa'=16,'pxc'=2,'py'=8] {'pxa'}, dimensions={0} | all-to-all | bytes 320000 | tf_op jit(solution)/shard_map/all_to_all | solution.py:71
  97.6 12.9 %all_to_all.21 = bf16[16,40,125]{2,1,0:T(8,128)(2,1)S(1)} all-to-all(bf16[16,40,125]{2,1,0:T(8,128)(2,1)S(1)} %broadcast_in_dim.272), channel_id=1, replica_groups=mesh['pxa'=16,'pxc'=2,'py'=8] {'pxa'}, dimensions={0} | all-to-all | bytes 320000 | tf_op jit(solution)/shard_map/all_to_all | solution.py:74
  110.6 3.0 %collective-permute-start.3 = (bf16[640,125]{1,0:T(8,128)(2,1)S(1)}, bf16[640,125]{1,0:T(8,128)(2,1)S(1)}, u32[]{:S(2)}, u32[]{:S(2)}) collective-permute-start(bf16[640,125]{1,0:T(8,128)(2,1)S(1)} %bitcast.211), channel_id=1, source_target_pairs={{0,8},{8,0},{1,9},{9,1},{2,10},{10,2},{3,11},{11,3},{4,12},{12,4},... | collective-permute-start | bytes 480008 | tf_op jit(solution)/shard_map/ppermute | solution.py:75
  113.6 1.0 collective-permute-done.3
  114.8 0.9 div.10
  (61 shorter events, 2.3 us)
Async XLA Ops:
  2.9 11.0 %all-to-all-start = ((f32[8,1,384]{2,1,0:T(1,128)}), f32[8,1,384]{2,1,0:T(1,128)S(1)}, u32[]{:S(2)}, u32[]{:S(2)}) async-start(f32[8,1,384]{2,1,0:T(1,128)} %reshape.500), calls=%async_computation | async-start | bytes 24576 | tf_op jit(solution)/shard_map/all_to_all | solution.py:145
  15.4 9.2 %collective-permute-start = (f32[2,32,8,3]{2,1,3,0:T(8,128)S(1)}, f32[2,32,8,3]{2,1,3,0:T(8,128)S(1)}, u32[]{:S(2)}, u32[]{:S(2)}) collective-permute-start(f32[2,32,8,3]{2,1,3,0:T(8,128)S(1)} %bitcast.239), channel_id=1, source_target_pairs={{0,8},{8,16},{16,24},{24,32},{32,40},{40,48},{48,56},{56,64},{64,7... | collective-permute-start | bytes 18440 | tf_op jit(solution)/shard_map/ppermute | solution.py:18
  21.8 7.4 %collective-permute-start.1 = (f32[2,32,8,3]{2,1,3,0:T(8,128)S(1)}, f32[2,32,8,3]{2,1,3,0:T(8,128)S(1)}, u32[]{:S(2)}, u32[]{:S(2)}) collective-permute-start(f32[2,32,8,3]{2,1,3,0:T(8,128)S(1)} %bitcast.240), channel_id=1, source_target_pairs={{8,0},{16,8},{24,16},{32,24},{40,32},{48,40},{56,48},{64,56},{72,6... | collective-permute-start | bytes 18440 | tf_op jit(solution)/shard_map/ppermute | solution.py:18
  34.9 5.9 %slice-start = ((s8[5734400]{0:T(1024)(128)(4,1)}), s8[4194304]{0:T(1024)(128)(4,1)S(1)}, s32[]{:S(2)}) async-start(s8[5734400]{0:T(1024)(128)(4,1)} %bitcast.242), calls=%async_computation.4 | async-start | bytes 8388608
  37.7 3.1 %slice-start.1 = ((s8[5734400]{0:T(1024)(128)(4,1)}), s8[1540096]{0:T(1024)(128)(4,1)S(1)}, s32[]{:S(2)}) async-start(s8[5734400]{0:T(1024)(128)(4,1)} %bitcast.242), calls=%async_computation.5 | async-start | bytes 3080192
  39.1 7.4 %copy-start = (bf16[4,4,1024]{2,1,0:T(4,128)(2,1)S(1)}, bf16[4,4,1024]{2,1,0:T(4,128)(2,1)}, u32[]{:S(2)}) copy-start(bf16[4,4,1024]{2,1,0:T(4,128)(2,1)} %param.13) | copy-start | bytes 98308
  40.8 7.4 %copy-start.1 = (bf16[25,4,32,24,50]{4,3,2,1,0:T(8,128)(2,1)}, bf16[25,4,32,24,50]{4,3,2,1,0:T(8,128)(2,1)S(1)}, u32[]{:S(2)}) copy-start(bf16[25,4,32,24,50]{4,3,2,1,0:T(8,128)(2,1)S(1)} %bitcast_dynamic-update-slice_fusion) | copy-start | bytes 23040004
  49.3 8.5 %all-to-all-start.1 = ((bf16[8,4,4,148]{3,1,2,0:T(4,128)(2,1)}), bf16[8,4,4,148]{3,1,2,0:T(4,128)(2,1)S(1)}, u32[]{:S(2)}, u32[]{:S(2)}) async-start(bf16[8,4,4,148]{3,1,2,0:T(4,128)(2,1)} %maximum_bitcast_fusion), calls=%async_computation.1 | async-start | bytes 131072 | tf_op jit(solution)/shard_map/all_to_all | solution.py:172
  74.6 1.7 %collective-permute-start.2 = (f32[640,125]{1,0:T(8,128)S(1)}, f32[640,125]{1,0:T(8,128)S(1)}, u32[]{:S(2)}, u32[]{:S(2)}) collective-permute-start(f32[640,125]{1,0:T(8,128)S(1)} %pad_dynamic-slice_fusion), channel_id=1, source_target_pairs={{0,8},{8,0},{1,9},{9,1},{2,10},{10,2},{3,11},{11,3},{4,12},{12,4},... | collective-permute-start | bytes 960008 | tf_op jit(solution)/shard_map/ppermute | solution.py:69
  110.6 4.1 %collective-permute-start.3 = (bf16[640,125]{1,0:T(8,128)(2,1)S(1)}, bf16[640,125]{1,0:T(8,128)(2,1)S(1)}, u32[]{:S(2)}, u32[]{:S(2)}) collective-permute-start(bf16[640,125]{1,0:T(8,128)(2,1)S(1)} %bitcast.211), channel_id=1, source_target_pairs={{0,8},{8,0},{1,9},{9,1},{2,10},{10,2},{3,11},{11,3},{4,12},{12,4},... | collective-permute-start | bytes 480008 | tf_op jit(solution)/shard_map/ppermute | solution.py:75

commit v11 on v9

--- a/solution.py
+++ b/solution.py
@@ -2,6 +2,7 @@
 import jax.numpy as jnp
 from jax import lax
 from jax.sharding import PartitionSpec as P
+from jax.experimental.layout import Layout, with_layout_constraint
 
 BINS = 50
 SHIFTS = 24
@@ -151,10 +152,15 @@
     )
     cols_all = jnp.pad(col_module, 2, constant_values=-1)
 
-    stacked_band = gather_offsets(source, rows_wide, cols_all, tile_x, width)
-    stacked = lax.dynamic_slice_in_dim(stacked_band, col_start, tile_y, 2)
+    stacked_band = with_layout_constraint(
+        jnp.transpose(
+            gather_offsets(source, rows_wide, cols_all, tile_x, width), (0, 1, 3, 2, 4)
+        ),
+        Layout(major_to_minor=(0, 1, 2, 3, 4)),
+    )
+    stacked = lax.dynamic_slice_in_dim(stacked_band, col_start, tile_y, 3)
     partial_value = jnp.einsum(
-        "oxysb,obt->xyst", stacked, weights, preferred_element_type=jnp.float32
+        "oxsyb,obt->xyst", stacked, weights, preferred_element_type=jnp.float32
     )
     prediction = shift_sum(partial_value, ticks)
     resid = residual_of(prediction, measured, active)
@@ -167,7 +173,7 @@
     band_resid = jnp.transpose(got, (1, 0, 2, 3)).reshape(tile_x, width, span)
 
     gradient = jnp.einsum(
-        "oxysb,xysu->obu",
+        "oxsyb,xysu->obu",
         stacked_band,
         windows(band_resid, share),
         preferred_element_type=jnp.float32,

time: 115 us -> 117 us (1.017)
  other arithmetic: 13.9 us -> 15.5 us
    another operation x27 -> x1, local copies, waits for them, and re-layouts: 4.18 us -> 0.09 us  [windows(): jnp.stack([resid[:, :, offset:offset + ticks] for offset in range(SHIFTS)...]
    unnamed x38 -> x60, local copies, waits for them, and re-layouts: 2.97 us -> 5.23 us
    dynamic_slice x0 -> x1, local copies, waits for them, and re-layouts: none -> 1.47 us  [on_device(): stacked = lax.dynamic_slice_in_dim(stacked_band, col_start, tile_y, 3)]
    unnamed x24, other arithmetic: 7.53 us -> 8.75 us
  transfers between devices with their start and end apart: 6 -> 6, of which waited for: 5 -> 5; matrix products, arithmetic and copies ran while one was open for 3% -> 2% of each run, Pallas kernels for 0% -> 0%
where the time goes in v11:
time: 117 us; the launch traced here: 116 us
  blocking collectives  34.1 us (29%)
  starting transfers between devices  20.7 us (18%)
  matrix products  16.7 us (14%)
  waiting for transfers between devices  15.6 us (13%)
  other arithmetic  15.5 us (13%)
  local copies, waits for them, and re-layouts  12.1 us (10%)
  between operations  1.35 us (1%)
    all_to_all x1, blocking collectives, chip_sum(): got = lax.all_to_all(pieces, 'pxa', 0, 0).astype(jnp.float32)  21.2 us
    all_to_all x1, blocking collectives, chip_sum(): lax.all_to_all(spread, 'pxa', 0, 0).reshape((half,) + value.shape[1:])  12.9 us
    dot_general x1, matrix products, on_device(): jnp.einsum('oxsyb,xysu->obu', stacked_band, windows(band_resid, share), p...  11.9 us
    unnamed x24, other arithmetic  8.75 us
    ppermute x2, starting transfers between devices, passed_along(): return lax.ppermute(block, axis, route)  8.27 us
    all_to_all x1, starting transfers between devices, on_device(): band = jnp.transpose(lax.all_to_all(spread, 'py', 0, 0), (1, 0, 2, 3, 4))  5.94 us
    unnamed x60, local copies, waits for them, and re-layouts  5.23 us
    all_to_all x1, waiting for transfers between devices, on_device(): got = lax.all_to_all(sent, 'py', 0, 0)  5.12 us
  transfers between devices with their start and end apart: 6, of which 5 were waited for; matrix products, arithmetic and copies ran while one was open for 2% of the time, Pallas kernels for 0%

profile of v11, /device:TPU:1, one launch (start us, length us, event | category | flops | bytes accessed | tf_op | source)
XLA Modules:
  0.0 116.1 jit_solution(18386999406709500646)
XLA Ops:
  0.6 0.7 convert_bitcast_fusion
  1.3 0.7 pad_maximum_fusion.2
  2.1 0.8 reshape.496
  2.9 5.9 %all-to-all-start = ((f32[8,1,384]{2,1,0:T(1,128)}), f32[8,1,384]{2,1,0:T(1,128)S(1)}, u32[]{:S(2)}, u32[]{:S(2)}) async-start(f32[8,1,384]{2,1,0:T(1,128)} %reshape.496), calls=%async_computation | async-start | bytes 24576 | tf_op jit(solution)/shard_map/all_to_all | solution.py:140
  8.8 0.7 pad_dynamic-slice_fusion.2
  9.6 0.9 slice_compare_fusion.3
  10.6 3.3 %all-to-all-done = f32[8,1,384]{2,1,0:T(1,128)S(1)} async-done(((f32[8,1,384]{2,1,0:T(1,128)}), f32[8,1,384]{2,1,0:T(1,128)S(1)}, u32[]{:S(2)}, u32[]{:S(2)}) %all-to-all-start) | async-done | bytes 12320 | tf_op jit(solution)/shard_map/all_to_all | solution.py:140
  13.9 0.5 broadcast.494
  14.4 0.7 reduce.1
  15.1 0.3 reshape.497
  15.4 6.3 %collective-permute-start = (f32[2,32,8,3]{2,1,3,0:T(8,128)S(1)}, f32[2,32,8,3]{2,1,3,0:T(8,128)S(1)}, u32[]{:S(2)}, u32[]{:S(2)}) collective-permute-start(f32[2,32,8,3]{2,1,3,0:T(8,128)S(1)} %bitcast.400), channel_id=1, source_target_pairs={{0,8},{8,16},{16,24},{24,32},{32,40},{40,48},{48,56},{56,64},{64,7... | collective-permute-start | bytes 18440 | tf_op jit(solution)/shard_map/ppermute | solution.py:19
  21.8 1.9 %collective-permute-start.1 = (f32[2,32,8,3]{2,1,3,0:T(8,128)S(1)}, f32[2,32,8,3]{2,1,3,0:T(8,128)S(1)}, u32[]{:S(2)}, u32[]{:S(2)}) collective-permute-start(f32[2,32,8,3]{2,1,3,0:T(8,128)S(1)} %bitcast.401), channel_id=1, source_target_pairs={{8,0},{16,8},{24,16},{32,24},{40,32},{48,40},{56,48},{64,56},{72,6... | collective-permute-start | bytes 18440 | tf_op jit(solution)/shard_map/ppermute | solution.py:19
  23.8 0.7 convert_element_type.107
  24.5 0.1 copy.73
  24.7 4.5 %collective-permute-done.1 = f32[2,32,8,3]{2,1,3,0:T(8,128)S(1)} collective-permute-done((f32[2,32,8,3]{2,1,3,0:T(8,128)S(1)}, f32[2,32,8,3]{2,1,3,0:T(8,128)S(1)}, u32[]{:S(2)}, u32[]{:S(2)}) %collective-permute-start.1) | collective-permute-done | bytes 6176 | tf_op jit(solution)/shard_map/ppermute | solution.py:19
  29.5 0.1 copy.77
  29.6 0.1 copy.76
  29.7 2.9 %fusion.9 = bf16[8,32,24,50]{3,2,1,0:T(8,128)(2,1)S(1)} fusion(s32[8,32,8]{2,1,0:T(8,128)S(1)} %copy.77, bf16[8,32,8]{2,1,0:T(8,128)(2,1)S(1)} %copy.76, s32[8,32,8]{2,1,0:T(8,128)S(1)} %copy.75), kind=kOutput, calls=%fused_computation.28 | convolution fusion | flops 5115904 | bytes 634880 | tf_op jit(solution)/shard_map/xyks,xykb->xysb/dot_general | solution.py:86
  32.6 0.3 copy.188
  32.9 0.3 fusion.13
  33.2 0.4 fusion.16
  33.6 0.3 fusion.79
  33.9 0.4 fusion.19
  34.3 0.4 fusion.22
  34.8 0.4 fusion.25
  35.2 0.4 fusion.28
  35.6 0.3 fusion.77
  35.8 0.4 fusion.31
  36.3 0.4 fusion.34
  36.7 0.4 fusion.37
  37.1 0.4 fusion.40
  37.5 0.1 fusion.75
  37.6 0.4 fusion.43
  38.0 0.4 fusion.46
  38.4 0.4 fusion.49
  38.8 0.4 fusion.52
  39.2 0.3 fusion.74
  39.5 0.4 fusion.55
  40.0 0.4 fusion.58
  40.4 0.4 fusion.61
  40.8 0.4 fusion.64
  41.2 0.3 fusion.72
  41.5 0.4 fusion.67
  41.9 0.4 fusion.70
  42.4 1.5 %constant_dynamic-slice_fusion = bf16[25,4,24,4,50]{4,3,2,1,0:T(4,128)(2,1)S(1)} fusion(bf16[25,4,24,32,50]{4,3,2,1,0:T(8,128)(2,1)S(1)} %bitcast.373, s32[]{:T(128)S(6)} %select_n.123), kind=kLoop, calls=%fused_computation.220 | loop fusion | bytes 1920004 | tf_op jit(solution)/shard_map/dynamic_slice | solution.py:161
  43.9 1.9 %fusion.4 = f32[4,4,24,1000]{3,2,1,0:T(8,128)S(1)} fusion(f32[25,50,1000]{2,1,0:T(8,128)S(1)} %bitcast.404, bf16[25,4,24,4,50]{4,3,2,1,0:T(4,128)(2,1)S(1)} %constant_dynamic-slice_fusion), kind=kOutput, calls=%fused_computation.5 | convolution fusion | flops 961249984 | bytes 7496000 | tf_op jit(solution)/shard_map/oxsyb,obt->xyst/dot_general | solution.py:162
  45.7 1.4 %fusion.91 = (f32[4,4,1,1000]{3,2,1,0:T(1,128)S(1)}, f32[4,4,1,1000]{3,2,1,0:T(1,128)S(1)}, f32[4,4,1,1000]{3,2,1,0:T(1,128)S(1)}, f32[4,4,1,1000]{3,2,1,0:T(1,1...) fusion(f32[4,4,24,1000]{3,2,1,0:T(8,128)S(1)} %fusion.4), kind=kLoop, calls=%fused_computation.231 | loop fusion | bytes 2432000 | tf_op jit(solution)/shard_map/slice | solution.py:111
  47.1 0.3 fusion.92
  47.5 1.5 %copy-done = bf16[25,4,32,24,50]{4,2,3,1,0:T(8,128)(2,1)} copy-done((bf16[25,4,32,24,50]{4,2,3,1,0:T(8,128)(2,1)}, bf16[25,4,32,24,50]{4,2,3,1,0:T(8,128)(2,1)S(1)}, u32[]{:S(2)}) %copy-start) | copy-done | bytes 7680024
  49.7 1.5 %multiply_convert_fusion = (bf16[4,4,1024]{2,1,0:T(4,128)(2,1)S(1)}, bf16[4,4,1024]{2,1,0:T(4,128)(2,1)}) fusion(bf16[4,4,1024]{2,1,0:T(4,128)(2,1)S(1)} %copy-done.1, f32[4,4]{1,0:T(4,128)S(1)} %convert_element_type.107, f32[4,4,1000]{2,1,0:T(4,128)S(1)} %bitcast.397, f32[4,4,1000]{2,1,0:T(4,128)S(1)} %bitcast.393, f32[4,4,1000]{2,1,0:T(4,128)S(1)} %bitcast.374, ...), kind=kLoop, calls=%fused_computation.168 | loop fusion | flops 458752 | bytes 1634368 | tf_op jit(solution)/shard_map/convert_element_type | solution.py:123
  51.3 0.1 reshape.487
  51.4 0.1 reshape.488
  51.5 0.7 maximum_bitcast_fusion
  52.3 3.4 %all-to-all-start.1 = ((bf16[8,4,4,148]{3,2,1,0:T(4,128)(2,1)}), bf16[8,4,4,148]{3,2,1,0:T(4,128)(2,1)S(1)}, u32[]{:S(2)}, u32[]{:S(2)}) async-start(bf16[8,4,4,148]{3,2,1,0:T(4,128)(2,1)} %maximum_bitcast_fusion), calls=%async_computation.1 | async-start | bytes 131072 | tf_op jit(solution)/shard_map/all_to_all | solution.py:172
  55.6 5.1 %all-to-all-done.1 = bf16[8,4,4,148]{3,2,1,0:T(4,128)(2,1)S(1)} async-done(((bf16[8,4,4,148]{3,2,1,0:T(4,128)(2,1)}), bf16[8,4,4,148]{3,2,1,0:T(4,128)(2,1)S(1)}, u32[]{:S(2)}, u32[]{:S(2)}) %all-to-all-start.1) | async-done | bytes 37920 | tf_op jit(solution)/shard_map/all_to_all | solution.py:172
  63.0 11.9 %convolution_bitcast_fusion = f32[25,50,125]{2,1,0:T(8,128)S(1)} fusion(bf16[4,32,24,125]{3,1,2,0:T(8,128)(2,1)S(1)} %constant_dynamic-update-slice_fusion, bf16[25,4,32,24,50]{4,2,3,1,0:T(8,128)(2,1)} %copy-done), kind=kOutput, calls=%fused_computation.6 | convolution fusion | flops 960000000 | bytes 9073000 | tf_op jit(solution)/shard_map/oxsyb,xysu->obu/dot_general | solution.py:175
  75.0 0.1 collective-permute-start.2
  75.1 1.6 %collective-permute-done.2 = f32[640,125]{1,0:T(8,128)S(1)} collective-permute-done((f32[640,125]{1,0:T(8,128)S(1)}, f32[640,125]{1,0:T(8,128)S(1)}, u32[]{:S(2)}, u32[]{:S(2)}) %collective-permute-start.2) | collective-permute-done | bytes 320032 | tf_op jit(solution)/shard_map/ppermute | solution.py:70
  76.7 0.1 fusion.86
  76.8 21.2 %all_to_all.20 = bf16[16,40,125]{2,1,0:T(8,128)(2,1)S(1)} all-to-all(bf16[16,40,125]{2,1,0:T(8,128)(2,1)S(1)} %bitcast.372), channel_id=1, replica_groups=mesh['pxa'=16,'pxc'=2,'py'=8] {'pxa'}, dimensions={0} | all-to-all | bytes 320000 | tf_op jit(solution)/shard_map/all_to_all | solution.py:72
  98.1 12.9 %all_to_all.21 = bf16[16,40,125]{2,1,0:T(8,128)(2,1)S(1)} all-to-all(bf16[16,40,125]{2,1,0:T(8,128)(2,1)S(1)} %broadcast_in_dim.272), channel_id=1, replica_groups=mesh['pxa'=16,'pxc'=2,'py'=8] {'pxa'}, dimensions={0} | all-to-all | bytes 320000 | tf_op jit(solution)/shard_map/all_to_all | solution.py:75
  111.0 3.0 %collective-permute-start.3 = (bf16[640,125]{1,0:T(8,128)(2,1)S(1)}, bf16[640,125]{1,0:T(8,128)(2,1)S(1)}, u32[]{:S(2)}, u32[]{:S(2)}) collective-permute-start(bf16[640,125]{1,0:T(8,128)(2,1)S(1)} %bitcast.371), channel_id=1, source_target_pairs={{0,8},{8,0},{1,9},{9,1},{2,10},{10,2},{3,11},{11,3},{4,12},{12,4},... | collective-permute-start | bytes 480008 | tf_op jit(solution)/shard_map/ppermute | solution.py:76
  114.0 1.0 collective-permute-done.3
  115.2 0.9 div.10
  (82 shorter events, 3.6 us)
Async XLA Ops:
  2.9 11.0 %all-to-all-start = ((f32[8,1,384]{2,1,0:T(1,128)}), f32[8,1,384]{2,1,0:T(1,128)S(1)}, u32[]{:S(2)}, u32[]{:S(2)}) async-start(f32[8,1,384]{2,1,0:T(1,128)} %reshape.496), calls=%async_computation | async-start | bytes 24576 | tf_op jit(solution)/shard_map/all_to_all | solution.py:140
  15.4 9.2 %collective-permute-start = (f32[2,32,8,3]{2,1,3,0:T(8,128)S(1)}, f32[2,32,8,3]{2,1,3,0:T(8,128)S(1)}, u32[]{:S(2)}, u32[]{:S(2)}) collective-permute-start(f32[2,32,8,3]{2,1,3,0:T(8,128)S(1)} %bitcast.400), channel_id=1, source_target_pairs={{0,8},{8,16},{16,24},{24,32},{32,40},{40,48},{48,56},{56,64},{64,7... | collective-permute-start | bytes 18440 | tf_op jit(solution)/shard_map/ppermute | solution.py:19
  21.8 7.4 %collective-permute-start.1 = (f32[2,32,8,3]{2,1,3,0:T(8,128)S(1)}, f32[2,32,8,3]{2,1,3,0:T(8,128)S(1)}, u32[]{:S(2)}, u32[]{:S(2)}) collective-permute-start(f32[2,32,8,3]{2,1,3,0:T(8,128)S(1)} %bitcast.401), channel_id=1, source_target_pairs={{8,0},{16,8},{24,16},{32,24},{40,32},{48,40},{56,48},{64,56},{72,6... | collective-permute-start | bytes 18440 | tf_op jit(solution)/shard_map/ppermute | solution.py:19
  36.3 7.6 %slice-start = ((s8[5734400]{0:T(1024)(128)(4,1)}), s8[4194304]{0:T(1024)(128)(4,1)S(1)}, s32[]{:S(2)}) async-start(s8[5734400]{0:T(1024)(128)(4,1)} %bitcast.403), calls=%async_computation.4 | async-start | bytes 8388608
  39.5 4.3 %slice-start.1 = ((s8[5734400]{0:T(1024)(128)(4,1)}), s8[1540096]{0:T(1024)(128)(4,1)S(1)}, s32[]{:S(2)}) async-start(s8[5734400]{0:T(1024)(128)(4,1)} %bitcast.403), calls=%async_computation.5 | async-start | bytes 3080192
  41.2 8.4 %copy-start.1 = (bf16[4,4,1024]{2,1,0:T(4,128)(2,1)S(1)}, bf16[4,4,1024]{2,1,0:T(4,128)(2,1)}, u32[]{:S(2)}) copy-start(bf16[4,4,1024]{2,1,0:T(4,128)(2,1)} %param.13) | copy-start | bytes 98308
  42.3 6.7 %copy-start = (bf16[25,4,32,24,50]{4,2,3,1,0:T(8,128)(2,1)}, bf16[25,4,32,24,50]{4,2,3,1,0:T(8,128)(2,1)S(1)}, u32[]{:S(2)}) copy-start(bf16[25,4,32,24,50]{4,2,3,1,0:T(8,128)(2,1)S(1)} %fusion.70) | copy-start | bytes 23040004
  52.3 8.5 %all-to-all-start.1 = ((bf16[8,4,4,148]{3,2,1,0:T(4,128)(2,1)}), bf16[8,4,4,148]{3,2,1,0:T(4,128)(2,1)S(1)}, u32[]{:S(2)}, u32[]{:S(2)}) async-start(bf16[8,4,4,148]{3,2,1,0:T(4,128)(2,1)} %maximum_bitcast_fusion), calls=%async_computation.1 | async-start | bytes 131072 | tf_op jit(solution)/shard_map/all_to_all | solution.py:172
  75.0 1.7 %collective-permute-start.2 = (f32[640,125]{1,0:T(8,128)S(1)}, f32[640,125]{1,0:T(8,128)S(1)}, u32[]{:S(2)}, u32[]{:S(2)}) collective-permute-start(f32[640,125]{1,0:T(8,128)S(1)} %pad_dynamic-slice_fusion), channel_id=1, source_target_pairs={{0,8},{8,0},{1,9},{9,1},{2,10},{10,2},{3,11},{11,3},{4,12},{12,4},... | collective-permute-start | bytes 960008 | tf_op jit(solution)/shard_map/ppermute | solution.py:70
  111.0 4.1 %collective-permute-start.3 = (bf16[640,125]{1,0:T(8,128)(2,1)S(1)}, bf16[640,125]{1,0:T(8,128)(2,1)S(1)}, u32[]{:S(2)}, u32[]{:S(2)}) collective-permute-start(bf16[640,125]{1,0:T(8,128)(2,1)S(1)} %bitcast.371), channel_id=1, source_target_pairs={{0,8},{8,0},{1,9},{9,1},{2,10},{10,2},{3,11},{11,3},{4,12},{12,4},... | collective-permute-start | bytes 480008 | tf_op jit(solution)/shard_map/ppermute | solution.py:76

commit v12 on v9

--- a/solution.py
+++ b/solution.py
@@ -66,7 +66,7 @@
     half = unit * count
     keep = lax.dynamic_slice_in_dim(buf, core * half, half, 0)
     send = lax.dynamic_slice_in_dim(buf, (1 - core) * half, half, 0)
-    part = keep + lax.ppermute(send, "pxc", swap)
+    part = keep + lax.ppermute(send.astype(jnp.bfloat16), "pxc", swap).astype(jnp.float32)
     pieces = part.reshape((count, unit) + value.shape[1:]).astype(jnp.bfloat16)
     got = lax.all_to_all(pieces, "pxa", 0, 0).astype(jnp.float32)
     mine = jnp.sum(got, axis=0).astype(jnp.bfloat16)

time: 115 us -> 115 us (level)
  no operation moved by 1% of the time
where the time goes in v12:
time: 115 us
  blocking collectives  34.1 us (30%)
  starting transfers between devices  20.8 us (18%)
  matrix products  17.4 us (15%)
  waiting for transfers between devices  14.6 us (13%)
  other arithmetic  13.9 us (12%)
  local copies, waits for them, and re-layouts  12.3 us (11%)
  between operations  1.55 us (1%)
    all_to_all x1, blocking collectives, chip_sum(): got = lax.all_to_all(pieces, 'pxa', 0, 0).astype(jnp.float32)  21.2 us
    all_to_all x1, blocking collectives, chip_sum(): lax.all_to_all(spread, 'pxa', 0, 0).reshape((half,) + value.shape[1:])  12.9 us
    dot_general x1, matrix products, on_device(): jnp.einsum('oxysb,xysu->obu', stacked_band, windows(band_resid, share), p...  11.9 us
    ppermute x2, starting transfers between devices, passed_along(): return lax.ppermute(block, axis, route)  8.27 us
    unnamed x24, other arithmetic  7.53 us
    all_to_all x1, starting transfers between devices, on_device(): band = jnp.transpose(lax.all_to_all(spread, 'py', 0, 0), (1, 0, 2, 3, 4))  5.94 us
    all_to_all x1, waiting for transfers between devices, on_device(): got = lax.all_to_all(sent, 'py', 0, 0)  5.12 us
    ppermute x2, waiting for transfers between devices, passed_along(): return lax.ppermute(block, axis, route)  4.41 us
  transfers between devices with their start and end apart: 6, of which 5 were waited for; matrix products, arithmetic and copies ran while one was open for 3% of the time, Pallas kernels for 0%

profile of v12, /device:TPU:1, one launch (start us, length us, event | category | flops | bytes accessed | tf_op | source)
XLA Modules:
  0.0 114.7 jit_solution(2488876082577478681)
XLA Ops:
  0.6 0.7 convert_bitcast_fusion
  1.3 0.7 pad_maximum_fusion.2
  2.1 0.8 reshape.496
  2.9 5.9 %all-to-all-start = ((f32[8,1,384]{2,1,0:T(1,128)}), f32[8,1,384]{2,1,0:T(1,128)S(1)}, u32[]{:S(2)}, u32[]{:S(2)}) async-start(f32[8,1,384]{2,1,0:T(1,128)} %reshape.496), calls=%async_computation | async-start | bytes 24576 | tf_op jit(solution)/shard_map/all_to_all | solution.py:139
  8.8 0.7 pad_dynamic-slice_fusion.2
  9.6 0.9 slice_compare_fusion.3
  10.6 3.3 %all-to-all-done = f32[8,1,384]{2,1,0:T(1,128)S(1)} async-done(((f32[8,1,384]{2,1,0:T(1,128)}), f32[8,1,384]{2,1,0:T(1,128)S(1)}, u32[]{:S(2)}, u32[]{:S(2)}) %all-to-all-start) | async-done | bytes 12320 | tf_op jit(solution)/shard_map/all_to_all | solution.py:139
  13.9 0.5 broadcast.494
  14.4 0.7 reduce.1
  15.1 0.3 reshape.497
  15.4 6.3 %collective-permute-start = (f32[2,32,8,3]{2,1,3,0:T(8,128)S(1)}, f32[2,32,8,3]{2,1,3,0:T(8,128)S(1)}, u32[]{:S(2)}, u32[]{:S(2)}) collective-permute-start(f32[2,32,8,3]{2,1,3,0:T(8,128)S(1)} %bitcast.289), channel_id=1, source_target_pairs={{0,8},{8,16},{16,24},{24,32},{32,40},{40,48},{48,56},{56,64},{64,7... | collective-permute-start | bytes 18440 | tf_op jit(solution)/shard_map/ppermute | solution.py:18
  21.8 1.9 %collective-permute-start.1 = (f32[2,32,8,3]{2,1,3,0:T(8,128)S(1)}, f32[2,32,8,3]{2,1,3,0:T(8,128)S(1)}, u32[]{:S(2)}, u32[]{:S(2)}) collective-permute-start(f32[2,32,8,3]{2,1,3,0:T(8,128)S(1)} %bitcast.290), channel_id=1, source_target_pairs={{8,0},{16,8},{24,16},{32,24},{40,32},{48,40},{56,48},{64,56},{72,6... | collective-permute-start | bytes 18440 | tf_op jit(solution)/shard_map/ppermute | solution.py:18
  23.8 0.7 convert_element_type.113
  24.5 0.1 copy.1565
  24.6 0.1 copy.1535
  24.8 4.4 %collective-permute-done.1 = f32[2,32,8,3]{2,1,3,0:T(8,128)S(1)} collective-permute-done((f32[2,32,8,3]{2,1,3,0:T(8,128)S(1)}, f32[2,32,8,3]{2,1,3,0:T(8,128)S(1)}, u32[]{:S(2)}, u32[]{:S(2)}) %collective-permute-start.1) | collective-permute-done | bytes 6176 | tf_op jit(solution)/shard_map/ppermute | solution.py:18
  29.6 0.1 copy.1538
  29.7 2.9 %convolution_convert_fusion = bf16[8,32,24,50]{3,2,1,0:T(8,128)(2,1)S(1)} fusion(s32[8,32,8]{2,1,0:T(8,128)S(1)} %copy.1539, bf16[8,32,8]{2,1,0:T(8,128)(2,1)S(1)} %copy.1538, s32[8,32,8]{2,1,0:T(8,128)S(1)} %copy.1537), kind=kOutput, calls=%fused_computation.4 | convolution fusion | flops 5115904 | bytes 634880 | tf_op jit(solution)/shard_map/xyks,xykb->xysb/dot_general | solution.py:85
  32.6 0.2 bitcast_dynamic-update-slice_fusion.19
  32.8 0.3 bitcast_dynamic-update-slice_fusion.18
  33.2 0.3 fusion.13
  33.5 0.3 bitcast_dynamic-update-slice_fusion.17
  33.8 0.3 bitcast_dynamic-update-slice_fusion.16
  34.2 0.3 bitcast_dynamic-update-slice_fusion.15
  34.5 0.3 bitcast_dynamic-update-slice_fusion.14
  34.9 0.3 fusion.11
  35.2 0.3 bitcast_dynamic-update-slice_fusion.13
  35.5 0.3 bitcast_dynamic-update-slice_fusion.12
  35.9 0.3 bitcast_dynamic-update-slice_fusion.11
  36.2 0.3 bitcast_dynamic-update-slice_fusion.10
  36.6 0.1 fusion.9
  36.7 0.3 bitcast_dynamic-update-slice_fusion.9
  37.0 0.3 bitcast_dynamic-update-slice_fusion.8
  37.4 0.3 bitcast_dynamic-update-slice_fusion.7
  37.8 0.3 bitcast_dynamic-update-slice_fusion.6
  38.1 0.3 fusion.8
  38.4 0.3 bitcast_dynamic-update-slice_fusion.5
  38.7 0.3 bitcast_dynamic-update-slice_fusion.4
  39.1 0.3 bitcast_dynamic-update-slice_fusion.3
  39.5 0.3 bitcast_dynamic-update-slice_fusion.2
  39.8 0.3 fusion.6
  40.1 0.3 bitcast_dynamic-update-slice_fusion.1
  40.5 0.3 bitcast_dynamic-update-slice_fusion
  40.8 2.6 %fusion = f32[4,4,24,1000,1]{3,2,1,0,4:T(8,128)S(1)} fusion(f32[25,50,1000]{2,1,0:T(8,128)S(1)} %bitcast.293, bf16[25,4,32,24,50]{4,3,2,1,0:T(8,128)(2,1)S(1)} %bitcast_dynamic-update-slice_fusion, s32[]{:T(128)S(6)} %select_n.123), kind=kOutput, calls=%fused_computation | convolution fusion | flops 961249984 | bytes 9728004 | tf_op jit(solution)/shard_map/oxysb,obt->xyst/dot_general | solution.py:156
  43.5 0.2 copy.1674
  43.7 1.2 %fusion.26 = (f32[4,4,1,1000]{3,2,1,0:T(1,128)S(1)}, f32[4,4,1,1000]{3,2,1,0:T(1,128)S(1)}, f32[4,4,1,1000]{3,2,1,0:T(1,128)S(1)}, f32[4,4,1,1000]{3,2,1,0:T(1,1...) fusion(f32[4,4,24,1000]{3,2,1,0:T(8,128)S(1)} %bitcast.257), kind=kLoop, calls=%fused_computation.146 | loop fusion | bytes 2432000 | tf_op jit(solution)/shard_map/slice | solution.py:110
  44.9 0.3 fusion.27
  46.5 1.2 %multiply_convert_fusion = (bf16[4,4,1024]{2,0,1:T(4,128)(2,1)S(1)}, bf16[4,4,1024]{2,0,1:T(4,128)(2,1)S(1)}) fusion(bf16[4,4,1024]{2,1,0:T(4,128)(2,1)S(1)} %copy-done, f32[4,4]{0,1:T(4,128)S(1)} %copy.1565, f32[4,4,1000]{2,0,1:T(4,128)S(1)} %bitcast.263, f32[4,4,1000]{2,0,1:T(4,128)S(1)} %bitcast.283, f32[4,4,1000]{2,0,1:T(4,128)S(1)} %bitcast.264, ...), kind=kLoop, calls=%fused_computation.84 | loop fusion | flops 458752 | bytes 1634368 | tf_op jit(solution)/shard_map/convert_element_type | solution.py:122
  47.8 0.1 reshape.487
  47.9 0.1 reshape.488
  48.1 0.7 maximum_bitcast_fusion
  48.8 3.4 %all-to-all-start.1 = ((bf16[8,4,4,148]{3,2,1,0:T(4,128)(2,1)}), bf16[8,4,4,148]{3,2,1,0:T(4,128)(2,1)S(1)}, u32[]{:S(2)}, u32[]{:S(2)}) async-start(bf16[8,4,4,148]{3,2,1,0:T(4,128)(2,1)} %maximum_bitcast_fusion), calls=%async_computation.1 | async-start | bytes 131072 | tf_op jit(solution)/shard_map/all_to_all | solution.py:166
  52.2 5.1 %all-to-all-done.1 = bf16[8,4,4,148]{3,2,1,0:T(4,128)(2,1)S(1)} async-done(((bf16[8,4,4,148]{3,2,1,0:T(4,128)(2,1)}), bf16[8,4,4,148]{3,2,1,0:T(4,128)(2,1)S(1)}, u32[]{:S(2)}, u32[]{:S(2)}) %all-to-all-start.1) | async-done | bytes 37920 | tf_op jit(solution)/shard_map/all_to_all | solution.py:166
  57.4 0.2 slice_bitcast_fusion.1
  57.6 0.1 slice_bitcast_fusion.20
  59.2 2.6 %stack.219 = bf16[4,32,24,125]{3,2,1,0:T(8,128)(2,1)S(1)} concatenate(bf16[4,32,1,125]{3,2,1,0:T(2,128)(2,1)S(1)} %copy.1569, bf16[4,32,1,125]{3,2,1,0:T(2,128)(2,1)S(1)} %copy.1570, bf16[4,32,1,125]{3,2,1,0:T(2,128)(2,1)S(1)} %copy.1571, bf16[4,32,1,125]{3,2,1,0:T(2,128)(2,1)S(1)} %copy.1572, bf16[4,32,1,125]{3,2,1,0:T(2,128)(2,1)S(1)} %copy.1573, ...), dimensions={2} | concatenate | bytes 1536000 | tf_op jit(solution)/shard_map/stack | solution.py:116
  61.8 11.9 %convolution_bitcast_fusion = f32[25,50,125]{2,1,0:T(8,128)S(1)} fusion(bf16[25,4,32,24,50]{4,3,2,1,0:T(8,128)(2,1)} %copy-done.1, bf16[4,32,24,125]{3,2,1,0:T(8,128)(2,1)S(1)} %stack.219), kind=kOutput, calls=%fused_computation.6 | convolution fusion | flops 960000000 | bytes 9073000 | tf_op jit(solution)/shard_map/oxysb,xysu->obu/dot_general | solution.py:169
  73.9 1.4 %collective-permute-done.2 = bf16[640,125]{1,0:T(8,128)(2,1)S(1)} collective-permute-done((bf16[640,125]{1,0:T(8,128)(2,1)S(1)}, bf16[640,125]{1,0:T(8,128)(2,1)S(1)}, u32[]{:S(2)}, u32[]{:S(2)}) %collective-permute-start.2) | collective-permute-done | bytes 160032 | tf_op jit(solution)/shard_map/ppermute | solution.py:69
  75.4 21.2 %all_to_all.20 = bf16[16,40,125]{2,1,0:T(8,128)(2,1)S(1)} all-to-all(bf16[16,40,125]{2,1,0:T(8,128)(2,1)S(1)} %bitcast.261), channel_id=1, replica_groups=mesh['pxa'=16,'pxc'=2,'py'=8] {'pxa'}, dimensions={0} | all-to-all | bytes 320000 | tf_op jit(solution)/shard_map/all_to_all | solution.py:71
  96.6 12.9 %all_to_all.21 = bf16[16,40,125]{2,1,0:T(8,128)(2,1)S(1)} all-to-all(bf16[16,40,125]{2,1,0:T(8,128)(2,1)S(1)} %broadcast_in_dim.272), channel_id=1, replica_groups=mesh['pxa'=16,'pxc'=2,'py'=8] {'pxa'}, dimensions={0} | all-to-all | bytes 320000 | tf_op jit(solution)/shard_map/all_to_all | solution.py:74
  109.5 3.1 %collective-permute-start.3 = (bf16[640,125]{1,0:T(8,128)(2,1)S(1)}, bf16[640,125]{1,0:T(8,128)(2,1)S(1)}, u32[]{:S(2)}, u32[]{:S(2)}) collective-permute-start(bf16[640,125]{1,0:T(8,128)(2,1)S(1)} %bitcast.262), channel_id=1, source_target_pairs={{0,8},{8,0},{1,9},{9,1},{2,10},{10,2},{3,11},{11,3},{4,12},{12,4},... | collective-permute-start | bytes 480008 | tf_op jit(solution)/shard_map/ppermute | solution.py:75
  112.7 0.6 copy.1594
  113.3 0.4 collective-permute-done.3
  113.8 0.9 div.10
  (87 shorter events, 3.8 us)
Async XLA Ops:
  2.9 11.0 %all-to-all-start = ((f32[8,1,384]{2,1,0:T(1,128)}), f32[8,1,384]{2,1,0:T(1,128)S(1)}, u32[]{:S(2)}, u32[]{:S(2)}) async-start(f32[8,1,384]{2,1,0:T(1,128)} %reshape.496), calls=%async_computation | async-start | bytes 24576 | tf_op jit(solution)/shard_map/all_to_all | solution.py:139
  15.4 9.3 %collective-permute-start = (f32[2,32,8,3]{2,1,3,0:T(8,128)S(1)}, f32[2,32,8,3]{2,1,3,0:T(8,128)S(1)}, u32[]{:S(2)}, u32[]{:S(2)}) collective-permute-start(f32[2,32,8,3]{2,1,3,0:T(8,128)S(1)} %bitcast.289), channel_id=1, source_target_pairs={{0,8},{8,16},{16,24},{24,32},{32,40},{40,48},{48,56},{56,64},{64,7... | collective-permute-start | bytes 18440 | tf_op jit(solution)/shard_map/ppermute | solution.py:18
  21.8 7.4 %collective-permute-start.1 = (f32[2,32,8,3]{2,1,3,0:T(8,128)S(1)}, f32[2,32,8,3]{2,1,3,0:T(8,128)S(1)}, u32[]{:S(2)}, u32[]{:S(2)}) collective-permute-start(f32[2,32,8,3]{2,1,3,0:T(8,128)S(1)} %bitcast.290), channel_id=1, source_target_pairs={{8,0},{16,8},{24,16},{32,24},{40,32},{48,40},{56,48},{64,56},{72,6... | collective-permute-start | bytes 18440 | tf_op jit(solution)/shard_map/ppermute | solution.py:18
  34.9 5.9 %slice-start = ((s8[5734400]{0:T(1024)(128)(4,1)}), s8[4194304]{0:T(1024)(128)(4,1)S(1)}, s32[]{:S(2)}) async-start(s8[5734400]{0:T(1024)(128)(4,1)} %bitcast.292), calls=%async_computation.4 | async-start | bytes 8388608
  37.7 3.1 %slice-start.1 = ((s8[5734400]{0:T(1024)(128)(4,1)}), s8[1540096]{0:T(1024)(128)(4,1)S(1)}, s32[]{:S(2)}) async-start(s8[5734400]{0:T(1024)(128)(4,1)} %bitcast.292), calls=%async_computation.5 | async-start | bytes 3080192
  39.1 7.4 %copy-start = (bf16[4,4,1024]{2,1,0:T(4,128)(2,1)S(1)}, bf16[4,4,1024]{2,1,0:T(4,128)(2,1)}, u32[]{:S(2)}) copy-start(bf16[4,4,1024]{2,1,0:T(4,128)(2,1)} %param.13) | copy-start | bytes 98308
  40.8 7.0 %copy-start.1 = (bf16[25,4,32,24,50]{4,3,2,1,0:T(8,128)(2,1)}, bf16[25,4,32,24,50]{4,3,2,1,0:T(8,128)(2,1)S(1)}, u32[]{:S(2)}) copy-start(bf16[25,4,32,24,50]{4,3,2,1,0:T(8,128)(2,1)S(1)} %bitcast_dynamic-update-slice_fusion) | copy-start | bytes 23040004
  48.8 8.5 %all-to-all-start.1 = ((bf16[8,4,4,148]{3,2,1,0:T(4,128)(2,1)}), bf16[8,4,4,148]{3,2,1,0:T(4,128)(2,1)S(1)}, u32[]{:S(2)}, u32[]{:S(2)}) async-start(bf16[8,4,4,148]{3,2,1,0:T(4,128)(2,1)} %maximum_bitcast_fusion), calls=%async_computation.1 | async-start | bytes 131072 | tf_op jit(solution)/shard_map/all_to_all | solution.py:166
  73.8 1.5 %collective-permute-start.2 = (bf16[640,125]{1,0:T(8,128)(2,1)S(1)}, bf16[640,125]{1,0:T(8,128)(2,1)S(1)}, u32[]{:S(2)}, u32[]{:S(2)}) collective-permute-start(bf16[640,125]{1,0:T(8,128)(2,1)S(1)} %fusion.21), channel_id=1, source_target_pairs={{0,8},{8,0},{1,9},{9,1},{2,10},{10,2},{3,11},{11,3},{4,12},{12,4},... | collective-permute-start | bytes 480008 | tf_op jit(solution)/shard_map/ppermute | solution.py:69
  109.5 4.2 %collective-permute-start.3 = (bf16[640,125]{1,0:T(8,128)(2,1)S(1)}, bf16[640,125]{1,0:T(8,128)(2,1)S(1)}, u32[]{:S(2)}, u32[]{:S(2)}) collective-permute-start(bf16[640,125]{1,0:T(8,128)(2,1)S(1)} %bitcast.262), channel_id=1, source_target_pairs={{0,8},{8,0},{1,9},{9,1},{2,10},{10,2},{3,11},{11,3},{4,12},{12,4},... | collective-permute-start | bytes 480008 | tf_op jit(solution)/shard_map/ppermute | solution.py:75

commit v13 on v9

--- a/solution.py
+++ b/solution.py
@@ -69,7 +69,7 @@
     part = keep + lax.ppermute(send, "pxc", swap)
     pieces = part.reshape((count, unit) + value.shape[1:]).astype(jnp.bfloat16)
     got = lax.all_to_all(pieces, "pxa", 0, 0).astype(jnp.float32)
-    mine = jnp.sum(got, axis=0).astype(jnp.bfloat16)
+    mine = (jnp.sum(got, axis=0) * (1.0 / 16)).astype(jnp.bfloat16)
     spread = jnp.broadcast_to(mine[None], pieces.shape)
     ours = lax.all_to_all(spread, "pxa", 0, 0).reshape((half,) + value.shape[1:])
     theirs = lax.ppermute(ours, "pxc", swap)
@@ -174,7 +174,7 @@
     )
     flat = gradient.reshape(-1, share)
     summed = chip_sum(flat).reshape(gradient.shape)
-    return (prediction.astype(jnp.bfloat16), summed / 16)
+    return (prediction.astype(jnp.bfloat16), summed)
 
 
 def solution(mesh):

time: 115 us -> 115 us (level)
  no operation moved by 1% of the time
where the time goes in v13:
time: 115 us
  blocking collectives  34.1 us (30%)
  starting transfers between devices  20.7 us (18%)
  matrix products  17.4 us (15%)
  waiting for transfers between devices  14.9 us (13%)
  other arithmetic  13.9 us (12%)
  local copies, waits for them, and re-layouts  12.3 us (11%)
  between operations  1.56 us (1%)
    all_to_all x1, blocking collectives, chip_sum(): got = lax.all_to_all(pieces, 'pxa', 0, 0).astype(jnp.float32)  21.2 us
    all_to_all x1, blocking collectives, chip_sum(): lax.all_to_all(spread, 'pxa', 0, 0).reshape((half,) + value.shape[1:])  12.9 us
    dot_general x1, matrix products, on_device(): jnp.einsum('oxysb,xysu->obu', stacked_band, windows(band_resid, share), p...  11.9 us
    ppermute x2, starting transfers between devices, passed_along(): return lax.ppermute(block, axis, route)  8.27 us
    unnamed x24, other arithmetic  7.53 us
    all_to_all x1, starting transfers between devices, on_device(): band = jnp.transpose(lax.all_to_all(spread, 'py', 0, 0), (1, 0, 2, 3, 4))  5.94 us
    all_to_all x1, waiting for transfers between devices, on_device(): got = lax.all_to_all(sent, 'py', 0, 0)  5.12 us
    ppermute x2, waiting for transfers between devices, passed_along(): return lax.ppermute(block, axis, route)  4.41 us
  transfers between devices with their start and end apart: 6, of which 5 were waited for; matrix products, arithmetic and copies ran while one was open for 3% of the time, Pallas kernels for 0%

profile of v13, /device:TPU:1, one launch (start us, length us, event | category | flops | bytes accessed | tf_op | source)
XLA Modules:
  0.0 114.9 jit_solution(16095337049040284153)
XLA Ops:
  0.6 0.7 convert_bitcast_fusion
  1.3 0.7 pad_maximum_fusion.2
  2.1 0.8 reshape.507
  2.9 5.9 %all-to-all-start = ((f32[8,1,384]{2,1,0:T(1,128)}), f32[8,1,384]{2,1,0:T(1,128)S(1)}, u32[]{:S(2)}, u32[]{:S(2)}) async-start(f32[8,1,384]{2,1,0:T(1,128)} %reshape.507), calls=%async_computation | async-start | bytes 24576 | tf_op jit(solution)/shard_map/all_to_all | solution.py:139
  8.8 0.7 pad_dynamic-slice_fusion.2
  9.6 0.9 slice_compare_fusion.3
  10.6 3.3 %all-to-all-done = f32[8,1,384]{2,1,0:T(1,128)S(1)} async-done(((f32[8,1,384]{2,1,0:T(1,128)}), f32[8,1,384]{2,1,0:T(1,128)S(1)}, u32[]{:S(2)}, u32[]{:S(2)}) %all-to-all-start) | async-done | bytes 12320 | tf_op jit(solution)/shard_map/all_to_all | solution.py:139
  13.9 0.5 broadcast.494
  14.4 0.7 reduce
  15.1 0.3 reshape.508
  15.4 6.3 %collective-permute-start = (f32[2,32,8,3]{2,1,3,0:T(8,128)S(1)}, f32[2,32,8,3]{2,1,3,0:T(8,128)S(1)}, u32[]{:S(2)}, u32[]{:S(2)}) collective-permute-start(f32[2,32,8,3]{2,1,3,0:T(8,128)S(1)} %bitcast.289), channel_id=1, source_target_pairs={{0,8},{8,16},{16,24},{24,32},{32,40},{40,48},{48,56},{56,64},{64,7... | collective-permute-start | bytes 18440 | tf_op jit(solution)/shard_map/ppermute | solution.py:18
  21.8 1.9 %collective-permute-start.1 = (f32[2,32,8,3]{2,1,3,0:T(8,128)S(1)}, f32[2,32,8,3]{2,1,3,0:T(8,128)S(1)}, u32[]{:S(2)}, u32[]{:S(2)}) collective-permute-start(f32[2,32,8,3]{2,1,3,0:T(8,128)S(1)} %bitcast.290), channel_id=1, source_target_pairs={{8,0},{16,8},{24,16},{32,24},{40,32},{48,40},{56,48},{64,56},{72,6... | collective-permute-start | bytes 18440 | tf_op jit(solution)/shard_map/ppermute | solution.py:18
  23.8 0.7 convert_element_type.113
  24.5 0.1 copy.1565
  24.6 0.1 copy.1535
  24.8 4.4 %collective-permute-done.1 = f32[2,32,8,3]{2,1,3,0:T(8,128)S(1)} collective-permute-done((f32[2,32,8,3]{2,1,3,0:T(8,128)S(1)}, f32[2,32,8,3]{2,1,3,0:T(8,128)S(1)}, u32[]{:S(2)}, u32[]{:S(2)}) %collective-permute-start.1) | collective-permute-done | bytes 6176 | tf_op jit(solution)/shard_map/ppermute | solution.py:18
  29.6 0.1 copy.1538
  29.7 2.9 %convolution_convert_fusion = bf16[8,32,24,50]{3,2,1,0:T(8,128)(2,1)S(1)} fusion(s32[8,32,8]{2,1,0:T(8,128)S(1)} %copy.1539, bf16[8,32,8]{2,1,0:T(8,128)(2,1)S(1)} %copy.1538, s32[8,32,8]{2,1,0:T(8,128)S(1)} %copy.1537), kind=kOutput, calls=%fused_computation.4 | convolution fusion | flops 5115904 | bytes 634880 | tf_op jit(solution)/shard_map/xyks,xykb->xysb/dot_general | solution.py:85
  32.6 0.2 bitcast_dynamic-update-slice_fusion.19
  32.8 0.3 bitcast_dynamic-update-slice_fusion.18
  33.2 0.3 fusion.13
  33.5 0.3 bitcast_dynamic-update-slice_fusion.17
  33.8 0.3 bitcast_dynamic-update-slice_fusion.16
  34.2 0.3 bitcast_dynamic-update-slice_fusion.15
  34.5 0.3 bitcast_dynamic-update-slice_fusion.14
  34.9 0.3 fusion.11
  35.2 0.3 bitcast_dynamic-update-slice_fusion.13
  35.5 0.3 bitcast_dynamic-update-slice_fusion.12
  35.9 0.3 bitcast_dynamic-update-slice_fusion.11
  36.2 0.3 bitcast_dynamic-update-slice_fusion.10
  36.6 0.1 fusion.9
  36.7 0.3 bitcast_dynamic-update-slice_fusion.9
  37.0 0.3 bitcast_dynamic-update-slice_fusion.8
  37.4 0.3 bitcast_dynamic-update-slice_fusion.7
  37.8 0.3 bitcast_dynamic-update-slice_fusion.6
  38.1 0.3 fusion.8
  38.4 0.3 bitcast_dynamic-update-slice_fusion.5
  38.7 0.3 bitcast_dynamic-update-slice_fusion.4
  39.1 0.3 bitcast_dynamic-update-slice_fusion.3
  39.5 0.3 bitcast_dynamic-update-slice_fusion.2
  39.8 0.3 fusion.6
  40.1 0.3 bitcast_dynamic-update-slice_fusion.1
  40.5 0.3 bitcast_dynamic-update-slice_fusion
  40.8 2.6 %fusion = f32[4,4,24,1000,1]{3,2,1,0,4:T(8,128)S(1)} fusion(f32[25,50,1000]{2,1,0:T(8,128)S(1)} %bitcast.293, bf16[25,4,32,24,50]{4,3,2,1,0:T(8,128)(2,1)S(1)} %bitcast_dynamic-update-slice_fusion, s32[]{:T(128)S(6)} %select_n.123), kind=kOutput, calls=%fused_computation | convolution fusion | flops 961249984 | bytes 9728004 | tf_op jit(solution)/shard_map/oxysb,obt->xyst/dot_general | solution.py:156
  43.5 0.2 copy.1674
  43.7 1.2 %fusion.26 = (f32[4,4,1,1000]{3,2,1,0:T(1,128)S(1)}, f32[4,4,1,1000]{3,2,1,0:T(1,128)S(1)}, f32[4,4,1,1000]{3,2,1,0:T(1,128)S(1)}, f32[4,4,1,1000]{3,2,1,0:T(1,1...) fusion(f32[4,4,24,1000]{3,2,1,0:T(8,128)S(1)} %bitcast.257), kind=kLoop, calls=%fused_computation.147 | loop fusion | bytes 2432000 | tf_op jit(solution)/shard_map/slice | solution.py:110
  44.9 0.3 fusion.27
  46.5 1.2 %multiply_convert_fusion = (bf16[4,4,1024]{2,0,1:T(4,128)(2,1)S(1)}, bf16[4,4,1024]{2,0,1:T(4,128)(2,1)S(1)}) fusion(bf16[4,4,1024]{2,1,0:T(4,128)(2,1)S(1)} %copy-done, f32[4,4]{0,1:T(4,128)S(1)} %copy.1565, f32[4,4,1000]{2,0,1:T(4,128)S(1)} %bitcast.263, f32[4,4,1000]{2,0,1:T(4,128)S(1)} %bitcast.283, f32[4,4,1000]{2,0,1:T(4,128)S(1)} %bitcast.264, ...), kind=kLoop, calls=%fused_computation.84 | loop fusion | flops 458752 | bytes 1634368 | tf_op jit(solution)/shard_map/convert_element_type | solution.py:122
  47.8 0.1 reshape.493
  47.9 0.1 reshape.494
  48.1 0.7 maximum_bitcast_fusion
  48.8 3.4 %all-to-all-start.1 = ((bf16[8,4,4,148]{3,2,1,0:T(4,128)(2,1)}), bf16[8,4,4,148]{3,2,1,0:T(4,128)(2,1)S(1)}, u32[]{:S(2)}, u32[]{:S(2)}) async-start(bf16[8,4,4,148]{3,2,1,0:T(4,128)(2,1)} %maximum_bitcast_fusion), calls=%async_computation.1 | async-start | bytes 131072 | tf_op jit(solution)/shard_map/all_to_all | solution.py:166
  52.2 5.1 %all-to-all-done.1 = bf16[8,4,4,148]{3,2,1,0:T(4,128)(2,1)S(1)} async-done(((bf16[8,4,4,148]{3,2,1,0:T(4,128)(2,1)}), bf16[8,4,4,148]{3,2,1,0:T(4,128)(2,1)S(1)}, u32[]{:S(2)}, u32[]{:S(2)}) %all-to-all-start.1) | async-done | bytes 37920 | tf_op jit(solution)/shard_map/all_to_all | solution.py:166
  57.4 0.2 slice_bitcast_fusion.1
  57.6 0.1 slice_bitcast_fusion.20
  59.2 2.6 %stack.219 = bf16[4,32,24,125]{3,2,1,0:T(8,128)(2,1)S(1)} concatenate(bf16[4,32,1,125]{3,2,1,0:T(2,128)(2,1)S(1)} %copy.1569, bf16[4,32,1,125]{3,2,1,0:T(2,128)(2,1)S(1)} %copy.1570, bf16[4,32,1,125]{3,2,1,0:T(2,128)(2,1)S(1)} %copy.1571, bf16[4,32,1,125]{3,2,1,0:T(2,128)(2,1)S(1)} %copy.1572, bf16[4,32,1,125]{3,2,1,0:T(2,128)(2,1)S(1)} %copy.1573, ...), dimensions={2} | concatenate | bytes 1536000 | tf_op jit(solution)/shard_map/stack | solution.py:116
  61.8 11.9 %convolution_bitcast_fusion = f32[25,50,125]{2,1,0:T(8,128)S(1)} fusion(bf16[25,4,32,24,50]{4,3,2,1,0:T(8,128)(2,1)} %copy-done.1, bf16[4,32,24,125]{3,2,1,0:T(8,128)(2,1)S(1)} %stack.219), kind=kOutput, calls=%fused_computation.6 | convolution fusion | flops 960000000 | bytes 9073000 | tf_op jit(solution)/shard_map/oxysb,xysu->obu/dot_general | solution.py:169
  73.9 1.6 %collective-permute-done.2 = f32[640,125]{1,0:T(8,128)S(1)} collective-permute-done((f32[640,125]{1,0:T(8,128)S(1)}, f32[640,125]{1,0:T(8,128)S(1)}, u32[]{:S(2)}, u32[]{:S(2)}) %collective-permute-start.2) | collective-permute-done | bytes 320032 | tf_op jit(solution)/shard_map/ppermute | solution.py:69
  75.6 21.2 %all_to_all.20 = bf16[16,40,125]{2,1,0:T(8,128)(2,1)S(1)} all-to-all(bf16[16,40,125]{2,1,0:T(8,128)(2,1)S(1)} %bitcast.262), channel_id=1, replica_groups=mesh['pxa'=16,'pxc'=2,'py'=8] {'pxa'}, dimensions={0} | all-to-all | bytes 320000 | tf_op jit(solution)/shard_map/all_to_all | solution.py:71
  96.9 12.9 %all_to_all.21 = bf16[16,40,125]{2,1,0:T(8,128)(2,1)S(1)} all-to-all(bf16[16,40,125]{2,1,0:T(8,128)(2,1)S(1)} %broadcast_in_dim.272), channel_id=1, replica_groups=mesh['pxa'=16,'pxc'=2,'py'=8] {'pxa'}, dimensions={0} | all-to-all | bytes 320000 | tf_op jit(solution)/shard_map/all_to_all | solution.py:74
  109.8 3.0 %collective-permute-start.3 = (bf16[640,125]{1,0:T(8,128)(2,1)S(1)}, bf16[640,125]{1,0:T(8,128)(2,1)S(1)}, u32[]{:S(2)}, u32[]{:S(2)}) collective-permute-start(bf16[640,125]{1,0:T(8,128)(2,1)S(1)} %bitcast.261), channel_id=1, source_target_pairs={{0,8},{8,0},{1,9},{9,1},{2,10},{10,2},{3,11},{11,3},{4,12},{12,4},... | collective-permute-start | bytes 480008 | tf_op jit(solution)/shard_map/ppermute | solution.py:75
  112.9 0.6 copy.1594
  113.5 0.4 collective-permute-done.3
  114.0 0.9 reshape.501
  (88 shorter events, 3.7 us)
Async XLA Ops:
  2.9 11.0 %all-to-all-start = ((f32[8,1,384]{2,1,0:T(1,128)}), f32[8,1,384]{2,1,0:T(1,128)S(1)}, u32[]{:S(2)}, u32[]{:S(2)}) async-start(f32[8,1,384]{2,1,0:T(1,128)} %reshape.507), calls=%async_computation | async-start | bytes 24576 | tf_op jit(solution)/shard_map/all_to_all | solution.py:139
  15.4 9.3 %collective-permute-start = (f32[2,32,8,3]{2,1,3,0:T(8,128)S(1)}, f32[2,32,8,3]{2,1,3,0:T(8,128)S(1)}, u32[]{:S(2)}, u32[]{:S(2)}) collective-permute-start(f32[2,32,8,3]{2,1,3,0:T(8,128)S(1)} %bitcast.289), channel_id=1, source_target_pairs={{0,8},{8,16},{16,24},{24,32},{32,40},{40,48},{48,56},{56,64},{64,7... | collective-permute-start | bytes 18440 | tf_op jit(solution)/shard_map/ppermute | solution.py:18
  21.8 7.4 %collective-permute-start.1 = (f32[2,32,8,3]{2,1,3,0:T(8,128)S(1)}, f32[2,32,8,3]{2,1,3,0:T(8,128)S(1)}, u32[]{:S(2)}, u32[]{:S(2)}) collective-permute-start(f32[2,32,8,3]{2,1,3,0:T(8,128)S(1)} %bitcast.290), channel_id=1, source_target_pairs={{8,0},{16,8},{24,16},{32,24},{40,32},{48,40},{56,48},{64,56},{72,6... | collective-permute-start | bytes 18440 | tf_op jit(solution)/shard_map/ppermute | solution.py:18
  34.9 5.9 %slice-start = ((s8[5734400]{0:T(1024)(128)(4,1)}), s8[4194304]{0:T(1024)(128)(4,1)S(1)}, s32[]{:S(2)}) async-start(s8[5734400]{0:T(1024)(128)(4,1)} %bitcast.292), calls=%async_computation.4 | async-start | bytes 8388608
  37.7 3.1 %slice-start.1 = ((s8[5734400]{0:T(1024)(128)(4,1)}), s8[1540096]{0:T(1024)(128)(4,1)S(1)}, s32[]{:S(2)}) async-start(s8[5734400]{0:T(1024)(128)(4,1)} %bitcast.292), calls=%async_computation.5 | async-start | bytes 3080192
  39.1 7.4 %copy-start = (bf16[4,4,1024]{2,1,0:T(4,128)(2,1)S(1)}, bf16[4,4,1024]{2,1,0:T(4,128)(2,1)}, u32[]{:S(2)}) copy-start(bf16[4,4,1024]{2,1,0:T(4,128)(2,1)} %param.13) | copy-start | bytes 98308
  40.8 7.0 %copy-start.1 = (bf16[25,4,32,24,50]{4,3,2,1,0:T(8,128)(2,1)}, bf16[25,4,32,24,50]{4,3,2,1,0:T(8,128)(2,1)S(1)}, u32[]{:S(2)}) copy-start(bf16[25,4,32,24,50]{4,3,2,1,0:T(8,128)(2,1)S(1)} %bitcast_dynamic-update-slice_fusion) | copy-start | bytes 23040004
  48.8 8.5 %all-to-all-start.1 = ((bf16[8,4,4,148]{3,2,1,0:T(4,128)(2,1)}), bf16[8,4,4,148]{3,2,1,0:T(4,128)(2,1)S(1)}, u32[]{:S(2)}, u32[]{:S(2)}) async-start(bf16[8,4,4,148]{3,2,1,0:T(4,128)(2,1)} %maximum_bitcast_fusion), calls=%async_computation.1 | async-start | bytes 131072 | tf_op jit(solution)/shard_map/all_to_all | solution.py:166
  73.8 1.7 %collective-permute-start.2 = (f32[640,125]{1,0:T(8,128)S(1)}, f32[640,125]{1,0:T(8,128)S(1)}, u32[]{:S(2)}, u32[]{:S(2)}) collective-permute-start(f32[640,125]{1,0:T(8,128)S(1)} %pad_dynamic-slice_fusion), channel_id=1, source_target_pairs={{0,8},{8,0},{1,9},{9,1},{2,10},{10,2},{3,11},{11,3},{4,12},{12,4},... | collective-permute-start | bytes 960008 | tf_op jit(solution)/shard_map/ppermute | solution.py:69
  109.8 4.1 %collective-permute-start.3 = (bf16[640,125]{1,0:T(8,128)(2,1)S(1)}, bf16[640,125]{1,0:T(8,128)(2,1)S(1)}, u32[]{:S(2)}, u32[]{:S(2)}) collective-permute-start(bf16[640,125]{1,0:T(8,128)(2,1)S(1)} %bitcast.261), channel_id=1, source_target_pairs={{0,8},{8,0},{1,9},{9,1},{2,10},{10,2},{3,11},{11,3},{4,12},{12,4},... | collective-permute-start | bytes 480008 | tf_op jit(solution)/shard_map/ppermute | solution.py:75
